TPU v7x, 512 devices: a whole 4x4x16 slice. The times are simulated.
512 devices in a mesh: dp: 32 (over y, z_hi, core), mp: 16 (over z_lo, x).
Axes of the slice: x: 4, y: 4, z: 16 (z_hi: 4, z_lo: 4; z = z_hi * 4 + z_lo), core: 2. Of those that a mesh axis runs over, the one named last changes fastest.
Arguments:
- inputs: bfloat16 [16384, 4096], P('mp', 'dp'), may hold values from -6 to 6
- cotangent: bfloat16 [16384, 4096], P('mp', 'dp'), may hold values from -6 to 6
- r_factor: bfloat16 [1, 128, 128, 128], P(None, 'mp'), may hold values from -0.5 to 0.5
- l_factor: bfloat16 [1, 128, 128, 128], P(None, 'mp'), may hold values from -0.5 to 0.5
Outputs:
- outputs: bfloat16 [16384, 4096], P('mp', 'dp')
- grad_inputs: bfloat16 [16384, 4096], P('mp', 'dp')
- grad_r: float32 [1, 128, 128, 128], P(None, 'mp', 'dp')
- grad_l: float32 [1, 128, 128, 128], P(None, 'mp', 'dp')
All inputs are finite; a program needn't handle non-finite values.
Results may differ from a plain program's by a relative error of at most 0.0063.
Values may be sent and summed in bfloat16 or wider, within the bound.
No kernel may reach another device: no remote copies, remote signals or barrier semaphores. Data moves between devices by JAX's collectives and lax.ppermute only.
A program may use at most 64 MiB of HBM per device.

v0:
```python
import jax
import jax.numpy as jnp
from jax import lax
from jax.sharding import PartitionSpec as P

LAYERS = 1


def activate(values):
    return jax.nn.gelu(values, approximate=True)


def second_product(received, left):
    return jnp.einsum("ijt,jim->jmt", received, left, preferred_element_type=jnp.float32)


def left_apply(left, received):
    return (received, second_product(received, left))


def first_product(current, right):
    return jnp.einsum("ikt,ikj->ijt", current, right, preferred_element_type=jnp.float32).astype(
        jnp.bfloat16
    )


def forward_layer(current, right, left):
    first_out = first_product(current, right)
    return left_apply(
        left, lax.all_to_all(first_out, "mp", split_axis=1, concat_axis=0, tiled=True)
    )


def shards(inputs, cotangent, r_factor, l_factor):
    block_count = r_factor.shape[1]
    block_size = r_factor.shape[2]
    tokens_here = inputs.shape[1]
    scale = float(lax.axis_size("dp") * tokens_here) ** (-0.5)
    current = inputs.reshape(block_count, block_size, tokens_here)
    layer_index = 0
    received, pre_act = forward_layer(current, r_factor[layer_index], l_factor[layer_index])
    saved = [(current, received, pre_act)]
    current = activate(pre_act).astype(jnp.bfloat16)
    outputs = current.reshape(block_count * block_size, tokens_here)
    grad_now = cotangent.reshape(block_count, block_size, tokens_here)
    parts_r = [None] * LAYERS
    parts_l = [None] * LAYERS
    for layer_index in reversed(range(LAYERS)):
        right = r_factor[layer_index]
        left = l_factor[layer_index]
        layer_in = saved[layer_index][0]
        received = saved[layer_index][1]
        pre_act = saved[layer_index][2]
        back_fn = jax.vjp(activate, pre_act)[1]
        grad_pre = back_fn(grad_now.astype(jnp.float32))[0].astype(jnp.bfloat16)
        term_l = (
            jnp.einsum("ijt,jmt->jim", received, grad_pre, preferred_element_type=jnp.float32)
            * scale
        )
        parts_l[layer_index] = lax.psum_scatter(term_l, "dp", scatter_dimension=1, tiled=True)
        grad_first = jnp.einsum(
            "jmt,jim->ijt", grad_pre, left, preferred_element_type=jnp.float32
        ).astype(jnp.bfloat16)

        def apply_back(returned, right=right):
            spread = jnp.einsum("ijt,ikj->ikt", returned, right, preferred_element_type=jnp.float32)
            return (returned, spread.astype(jnp.bfloat16))

        returned, grad_now = apply_back(
            lax.all_to_all(grad_first, "mp", split_axis=0, concat_axis=1, tiled=True)
        )
        term_r = (
            jnp.einsum("ikt,ijt->ikj", layer_in, returned, preferred_element_type=jnp.float32)
            * scale
        )
        parts_r[layer_index] = lax.psum_scatter(term_r, "dp", scatter_dimension=1, tiled=True)
    stack_r = jnp.stack(parts_r, 0)
    stack_l = jnp.stack(parts_l, 0)
    grad_inputs = grad_now.reshape(block_count * block_size, tokens_here)
    return (outputs, grad_inputs, stack_r, stack_l)


def solution(mesh):
    placed = (P("mp", "dp"), P("mp", "dp"), P(None, "mp", None, None), P(None, "mp", None, None))
    return jax.shard_map(
        shards,
        mesh=mesh,
        in_specs=placed,
        out_specs=(
            P("mp", "dp"),
            P("mp", "dp"),
            P(None, "mp", "dp", None),
            P(None, "mp", "dp", None),
        ),
        check_vma=False,
    )
```

profile of v0, /device:TPU:2, one launch (start us, length us, event | category | flops | bytes accessed | tf_op | source)
XLA Modules:
  0.0 270.8 jit_solution(16528090919166589030)
XLA Ops:
  7.2 0.0 copy-start
  7.2 1.3 convolution_convert_fusion.2
  8.5 0.2 copy.22
  8.7 0.0 copy-start.3
  8.7 18.1 %all_to_all.36 = bf16[8,128,128]{2,0,1:T(8,128)(2,1)S(1)} all-to-all(bf16[8,128,128]{2,0,1:T(8,128)(2,1)S(1)} %copy.22), channel_id=1, replica_groups=mesh['dp'=32,'mp'=16] {'mp'}, dimensions={1} | all-to-all | bytes 524288 | tf_op jit(solution)/shard_map/all_to_all | solution.py:30
  26.9 0.0 copy-done
  26.9 0.0 copy-done.3
  26.9 1.3 fusion.4
  28.2 0.3 fusion.1
  28.5 0.9 copy.26
  29.4 5.1 %all-to-all-start.1 = ((bf16[128,8,128]{2,1,0:T(8,128)(2,1)}), bf16[128,8,128]{2,1,0:T(8,128)(2,1)S(1)}, u32[]{:S(2)}, u32[]{:S(2)}) async-start(bf16[128,8,128]{2,1,0:T(8,128)(2,1)} %copy.26), calls=%async_computation.1 | async-start | bytes 524288 | tf_op jit(solution)/shard_map/all_to_all | solution.py:70
  34.6 0.0 reduce-scatter.5.cloned.1.call-start
  34.6 0.3 convolution_multiply_fusion
  34.9 1.1 copy.29
  36.0 0.0 copy-start.2
  36.0 0.0 reduce-scatter.5.cloned.1.call-update
  36.0 0.0 reduce-scatter.3.cloned.1.call-start
  36.1 7.1 %all-to-all-done.1 = bf16[128,8,128]{2,1,0:T(8,128)(2,1)S(1)} async-done(((bf16[128,8,128]{2,1,0:T(8,128)(2,1)}), bf16[128,8,128]{2,1,0:T(8,128)(2,1)S(1)}, u32[]{:S(2)}, u32[]{:S(2)}) %all-to-all-start.1) | async-done | bytes 262176 | tf_op jit(solution)/shard_map/all_to_all | solution.py:70
  43.2 0.0 copy-done.2
  43.2 0.3 fusion
  43.5 1.0 copy.28
  44.5 0.0 copy-start.1
  44.5 0.0 reduce-scatter.3.cloned.1.call-update
  44.5 108.3 %reduce-scatter.5.cloned.1.call-done = f32[8,4,128]{2,0,1:T(8,128)} async-done(((f32[8,128,128]{2,0,1:T(8,128)}), f32[8,4,128]{2,0,1:T(8,128)}) %reduce-scatter.5.cloned.1.call-update) | async-done | bytes 16400 | tf_op jit(solution)/shard_map/reduce_scatter | solution.py:60
  152.8 1.3 copy.31
  154.1 0.0 copy-done.1
  154.1 0.9 convolution_convert_fusion
  155.0 107.7 %reduce-scatter.3.cloned.1.call-done = f32[8,4,128]{2,0,1:T(8,128)} async-done(((f32[8,128,128]{2,0,1:T(8,128)}), f32[8,4,128]{2,0,1:T(8,128)}) %reduce-scatter.3.cloned.1.call-update) | async-done | bytes 16400 | tf_op jit(solution)/shard_map/reduce_scatter | solution.py:76
  262.7 1.3 copy.30
Async XLA Ops:
  7.2 19.7 %copy-start = (bf16[1,8,128,128]{3,2,1,0:T(8,128)(2,1)S(1)}, bf16[1,8,128,128]{3,2,1,0:T(8,128)(2,1)}, u32[]{:S(2)}) copy-start(bf16[1,8,128,128]{3,2,1,0:T(8,128)(2,1)} %param.7) | copy-start | bytes 786436
  8.7 18.2 %copy-start.3 = (bf16[1024,128]{1,0:T(8,128)(2,1)S(1)}, bf16[1024,128]{1,0:T(8,128)(2,1)}, u32[]{:S(2)}) copy-start(bf16[1024,128]{1,0:T(8,128)(2,1)} %param.5) | copy-start | bytes 786436
  29.4 13.8 %all-to-all-start.1 = ((bf16[128,8,128]{2,1,0:T(8,128)(2,1)}), bf16[128,8,128]{2,1,0:T(8,128)(2,1)S(1)}, u32[]{:S(2)}, u32[]{:S(2)}) async-start(bf16[128,8,128]{2,1,0:T(8,128)(2,1)} %copy.26), calls=%async_computation.1 | async-start | bytes 524288 | tf_op jit(solution)/shard_map/all_to_all | solution.py:70
  34.6 118.2 %reduce-scatter.5.cloned.1.call-start = ((), (), s32[]{:S(2)}) async-start(), calls=%async_computation.5 | async-start | bytes 540672 | tf_op jit(solution)/shard_map/reduce_scatter | solution.py:60
  36.0 7.2 %copy-start.2 = (bf16[1024,128]{1,0:T(8,128)(2,1)S(1)}, bf16[1024,128]{1,0:T(8,128)(2,1)}, u32[]{:S(2)}) copy-start(bf16[1024,128]{1,0:T(8,128)(2,1)} %param.4) | copy-start | bytes 786436
  36.0 226.7 %reduce-scatter.3.cloned.1.call-start = ((), (), s32[]{:S(2)}) async-start(), calls=%async_computation.4 | async-start | bytes 540672 | tf_op jit(solution)/shard_map/reduce_scatter | solution.py:76
  44.5 109.6 %copy-start.1 = (bf16[1,8,128,128]{3,2,1,0:T(8,128)(2,1)S(1)}, bf16[1,8,128,128]{3,2,1,0:T(8,128)(2,1)}, u32[]{:S(2)}) copy-start(bf16[1,8,128,128]{3,2,1,0:T(8,128)(2,1)} %param.6) | copy-start | bytes 786436
Sparse Core Ops, SparseCore 0:
  39.7 113.0 reduce-scatter.4
  157.1 105.5 reduce-scatter.2
where the time goes:
time: 271 us
  waiting for transfers between devices  223 us (82%)
  blocking collectives  18.1 us (7%)
  between operations  14.1 us (5%)
  local copies, waits for them, and re-layouts  5.83 us (2%)
  starting transfers between devices  5.21 us (2%)
  matrix products  4.5 us (2%)
    reduce_scatter x1, waiting for transfers between devices, shards(): lax.psum_scatter(term_l, 'dp', scatter_dimension=1, tiled=True)  108 us
    reduce_scatter x1, waiting for transfers between devices, shards(): lax.psum_scatter(term_r, 'dp', scatter_dimension=1, tiled=True)  108 us
    all_to_all x1, blocking collectives, forward_layer(): lax.all_to_all(first_out, 'mp', split_axis=1, concat_axis=0, tiled=True)  18.1 us
    all_to_all x1, waiting for transfers between devices, shards(): lax.all_to_all(grad_first, 'mp', split_axis=0, concat_axis=1, tiled=True)  7.1 us
  transfers between devices with their start and end apart: 3, of which 3 were waited for; matrix products, arithmetic and copies ran while one was open for 2% of the time, Pallas kernels for 0%

commit v1 on v0

--- a/solution.py
+++ b/solution.py
@@ -31,11 +31,72 @@
     )
 
 
-def shards(inputs, cotangent, r_factor, l_factor):
+def dp_stages(mesh):
+    names = list(mesh.axis_names)
+    devs = mesh.devices
+    devs = devs.transpose([names.index("dp")] + [k for k in range(devs.ndim) if names[k] != "dp"])
+    column = [devs[(d,) + (0,) * (devs.ndim - 1)] for d in range(devs.shape[0])]
+    count = len(column)
+
+    def key(dev):
+        coords = tuple(getattr(dev, "coords", (dev.id,)))
+        return coords + (getattr(dev, "core_on_chip", 0),)
+
+    keys = [key(dev) for dev in column]
+    stages = []
+    stride = 1
+    while stride < count:
+        base = keys[0]
+        step = keys[stride]
+        varying = [a for a in range(len(base)) if base[a] != step[a]]
+        size = 1
+        while size * stride < count:
+            probe = keys[size * stride]
+            if [a for a in range(len(base)) if base[a] != probe[a]] != varying:
+                break
+            size += 1
+        if count % (size * stride) != 0 or size < 2:
+            size = count // stride
+        distance = 0 if varying == [len(base) - 1] else max(
+            abs(step[a] - base[a]) for a in varying
+        )
+        stages.append((distance, size, stride))
+        stride *= size
+    return stages
+
+
+def staged_reduce_scatter(term, stages, count):
+    lead = term.shape[:-2]
+    rows, cols = term.shape[-2:]
+    piece = rows // count
+    by_stride = sorted(stages, key=lambda s: -s[2])
+    digit_sizes = [s[1] for s in by_stride]
+    x = term.reshape(lead + tuple(digit_sizes) + (piece, cols))
+    order = sorted(stages, key=lambda s: (s[0], s[2]))
+    nlead = len(lead)
+    perm = [nlead + by_stride.index(s) for s in order]
+    x = x.transpose(perm + list(range(nlead)) + list(range(nlead + len(stages), x.ndim)))
+    me = lax.axis_index("dp")
+    for _, size, stride in order:
+        mine = (me // stride) % size
+        total = lax.dynamic_index_in_dim(x, mine, 0, keepdims=False)
+        for shift in range(1, size):
+            pairs = []
+            for d in range(count):
+                own = (d // stride) % size
+                pairs.append((d, d + (((own + shift) % size) - own) * stride))
+            send = lax.dynamic_index_in_dim(x, (mine + shift) % size, 0, keepdims=False)
+            total = total + lax.ppermute(send, "dp", perm=pairs)
+        x = total
+    return x
+
+
+def shards(stages, inputs, cotangent, r_factor, l_factor):
     block_count = r_factor.shape[1]
     block_size = r_factor.shape[2]
     tokens_here = inputs.shape[1]
-    scale = float(lax.axis_size("dp") * tokens_here) ** (-0.5)
+    dp_count = lax.axis_size("dp")
+    scale = float(dp_count * tokens_here) ** (-0.5)
     current = inputs.reshape(block_count, block_size, tokens_here)
     layer_index = 0
     received, pre_act = forward_layer(current, r_factor[layer_index], l_factor[layer_index])
@@ -57,7 +118,6 @@
             jnp.einsum("ijt,jmt->jim", received, grad_pre, preferred_element_type=jnp.float32)
             * scale
         )
-        parts_l[layer_index] = lax.psum_scatter(term_l, "dp", scatter_dimension=1, tiled=True)
         grad_first = jnp.einsum(
             "jmt,jim->ijt", grad_pre, left, preferred_element_type=jnp.float32
         ).astype(jnp.bfloat16)
@@ -73,7 +133,9 @@
             jnp.einsum("ikt,ijt->ikj", layer_in, returned, preferred_element_type=jnp.float32)
             * scale
         )
-        parts_r[layer_index] = lax.psum_scatter(term_r, "dp", scatter_dimension=1, tiled=True)
+        both = staged_reduce_scatter(jnp.stack([term_l, term_r], 0), stages, dp_count)
+        parts_l[layer_index] = both[0]
+        parts_r[layer_index] = both[1]
     stack_r = jnp.stack(parts_r, 0)
     stack_l = jnp.stack(parts_l, 0)
     grad_inputs = grad_now.reshape(block_count * block_size, tokens_here)
@@ -81,9 +143,14 @@
 
 
 def solution(mesh):
+    stages = dp_stages(mesh)
     placed = (P("mp", "dp"), P("mp", "dp"), P(None, "mp", None, None), P(None, "mp", None, None))
+
+    def body(*args):
+        return shards(stages, *args)
+
     return jax.shard_map(
-        shards,
+        body,
         mesh=mesh,
         in_specs=placed,
         out_specs=(

time: 271 us -> 86.6 us (0.32)
  the two profiles are of different devices: /device:TPU:2 before, /device:TPU:1 now
where the time goes in v1:
time: 86.6 us; the launch traced here: 86.2 us
  starting transfers between devices  40.5 us (47%)
  waiting for transfers between devices  18.5 us (21%)
  blocking collectives  18.4 us (21%)
  matrix products  4.5 us (5%)
  local copies, waits for them, and re-layouts  2.95 us (3%)
  between operations  1.05 us (1%)
    ppermute x7, starting transfers between devices, staged_reduce_scatter(): total = total + lax.ppermute(send, 'dp', perm=pairs)  36.3 us
    all_to_all x1, blocking collectives, forward_layer(): lax.all_to_all(first_out, 'mp', split_axis=1, concat_axis=0, tiled=True)  18.4 us
    ppermute x7, waiting for transfers between devices, staged_reduce_scatter(): total = total + lax.ppermute(send, 'dp', perm=pairs)  10.3 us
    all_to_all x1, waiting for transfers between devices, shards(): lax.all_to_all(grad_first, 'mp', split_axis=0, concat_axis=1, tiled=True)  8.18 us
    all_to_all x1, starting transfers between devices, shards(): lax.all_to_all(grad_first, 'mp', split_axis=0, concat_axis=1, tiled=True)  4.19 us
  transfers between devices with their start and end apart: 8, of which 6 were waited for; matrix products, arithmetic and copies ran while one was open for 2% of the time, Pallas kernels for 0%

profile of v1, /device:TPU:1, one launch (start us, length us, event | category | flops | bytes accessed | tf_op | source)
XLA Modules:
  0.0 86.2 jit_solution(2538710392055947158)
XLA Ops:
  0.6 0.0 copy-start
  0.6 1.3 %convolution_convert_fusion.2 = bf16[8,128,128]{2,1,0:T(8,128)(2,1)S(1)} fusion(bf16[8,128,128]{2,1,0:T(8,128)(2,1)} %bitcast.93, bf16[1,8,128,128]{3,2,1,0:T(8,128)(2,1)} %param.6), kind=kOutput, calls=%fused_computation.10 | convolution fusion | flops 33685504 | bytes 786432 | tf_op jit(solution)/shard_map/ikt,ikj->ijt/dot_general | solution.py:22
  2.0 0.2 copy.47
  2.2 0.0 copy-start.3
  2.2 18.4 %all_to_all.36 = bf16[8,128,128]{2,0,1:T(8,128)(2,1)S(1)} all-to-all(bf16[8,128,128]{2,0,1:T(8,128)(2,1)S(1)} %copy.47), channel_id=1, replica_groups=mesh['dp'=32,'mp'=16] {'mp'}, dimensions={1} | all-to-all | bytes 524288 | tf_op jit(solution)/shard_map/all_to_all | solution.py:30
  20.6 0.0 copy-done
  20.6 0.0 copy-done.3
  20.6 1.3 %fusion.4 = (bf16[8,128,128]{2,1,0:T(8,128)(2,1)S(1)}, bf16[8,128,128]{2,1,0:T(8,128)(2,1)}) fusion(bf16[8,128,128]{2,1,0:T(8,128)(2,1)S(1)} %bitcast.101, bf16[1,8,128,128]{3,2,1,0:T(8,128)(2,1)S(1)} %copy-done, bf16[8,16,8,128]{3,0,2,1:T(8,128)(2,1)S(1)} %bitcast.95), kind=kOutput, calls=%fused_computation.18 | convolution fusion | flops 36569088 | bytes 1310720 | tf_op jit(solution)/shard_map/ijt,jim->jmt/dot_general | solution.py:14
  22.0 0.3 fusion.1
  22.3 0.9 %copy.51 = bf16[128,8,128]{2,1,0:T(8,128)(2,1)} copy(bf16[128,8,128]{0,2,1:T(8,128)(2,1)S(1)} %fusion.1) | data formatting | bytes 524288 | tf_op jit(solution)/shard_map/convert_element_type | solution.py:123
  23.2 4.2 %all-to-all-start.1 = ((bf16[128,8,128]{2,1,0:T(8,128)(2,1)}), bf16[128,8,128]{2,1,0:T(8,128)(2,1)S(1)}, u32[]{:S(2)}, u32[]{:S(2)}) async-start(bf16[128,8,128]{2,1,0:T(8,128)(2,1)} %copy.51), calls=%async_computation.1 | async-start | bytes 524288 | tf_op jit(solution)/shard_map/all_to_all | solution.py:130
  27.4 0.3 convolution_multiply_fusion.1
  27.7 0.0 copy-start.2
  27.7 0.3 copy.55
  28.0 8.2 %all-to-all-done.1 = bf16[128,8,128]{2,1,0:T(8,128)(2,1)S(1)} async-done(((bf16[128,8,128]{2,1,0:T(8,128)(2,1)}), bf16[128,8,128]{2,1,0:T(8,128)(2,1)S(1)}, u32[]{:S(2)}, u32[]{:S(2)}) %all-to-all-start.1) | async-done | bytes 262176 | tf_op jit(solution)/shard_map/all_to_all | solution.py:130
  36.2 0.0 copy-done.2
  36.2 0.3 fusion
  36.5 0.2 copy.54
  36.8 4.8 %collective-permute-start = (f32[4,4,2,8,4,128]{5,3,4,1,0,2:T(8,128)S(1)}, f32[4,4,2,8,4,128]{5,3,4,1,0,2:T(8,128)S(1)}, u32[]{:S(2)}, u32[]{:S(2)}) collective-permute-start(f32[4,4,2,8,4,128]{5,3,4,1,0,2:T(8,128)S(1)} %fusion.13), channel_id=1, source_target_pairs={{0,16},{16,0},{32,48},{48,32},{64,80},{80,64},{96,112},{112,96},{1... | collective-permute-start | bytes 1572872 | tf_op jit(solution)/shard_map/ppermute | solution.py:89
  41.7 1.4 %collective-permute-done = f32[4,4,2,8,4,128]{5,3,4,1,0,2:T(8,128)S(1)} collective-permute-done((f32[4,4,2,8,4,128]{5,3,4,1,0,2:T(8,128)S(1)}, f32[4,4,2,8,4,128]{5,3,4,1,0,2:T(8,128)S(1)}, u32[]{:S(2)}, u32[]{:S(2)}) %collective-permute-start) | collective-permute-done | bytes 524320 | tf_op jit(solution)/shard_map/ppermute | solution.py:89
  43.1 0.1 fusion.16
  43.3 4.7 %collective-permute-start.3 = (f32[4,2,8,4,128]{4,2,3,1,0:T(8,128)S(1)}, f32[4,2,8,4,128]{4,2,3,1,0:T(8,128)S(1)}, u32[]{:S(2)}, u32[]{:S(2)}) collective-permute-start(f32[4,2,8,4,128]{4,2,3,1,0:T(8,128)S(1)} %bitcast.98), channel_id=1, source_target_pairs={{0,384},{16,400},{32,416},{48,432},{64,448},{80,464},{96,480},{112... | collective-permute-start | bytes 393224 | tf_op jit(solution)/shard_map/ppermute | solution.py:89
  47.9 2.3 %collective-permute-start.2 = (f32[4,2,8,4,128]{4,2,3,1,0:T(8,128)S(1)}, f32[4,2,8,4,128]{4,2,3,1,0:T(8,128)S(1)}, u32[]{:S(2)}, u32[]{:S(2)}) collective-permute-start(f32[4,2,8,4,128]{4,2,3,1,0:T(8,128)S(1)} %bitcast.99), channel_id=1, source_target_pairs={{0,256},{16,272},{32,288},{48,304},{64,320},{80,336},{96,352},{112... | collective-permute-start | bytes 393224 | tf_op jit(solution)/shard_map/ppermute | solution.py:89
  50.2 2.6 %collective-permute-start.1 = (f32[4,2,8,4,128]{4,2,3,1,0:T(8,128)S(1)}, f32[4,2,8,4,128]{4,2,3,1,0:T(8,128)S(1)}, u32[]{:S(2)}, u32[]{:S(2)}) collective-permute-start(f32[4,2,8,4,128]{4,2,3,1,0:T(8,128)S(1)} %bitcast.100), channel_id=1, source_target_pairs={{0,128},{16,144},{32,160},{48,176},{64,192},{80,208},{96,224},{112... | collective-permute-start | bytes 393224 | tf_op jit(solution)/shard_map/ppermute | solution.py:89
  52.9 0.0 collective-permute-done.3
  52.9 2.8 %collective-permute-done.2 = f32[4,2,8,4,128]{4,2,3,1,0:T(8,128)S(1)} collective-permute-done((f32[4,2,8,4,128]{4,2,3,1,0:T(8,128)S(1)}, f32[4,2,8,4,128]{4,2,3,1,0:T(8,128)S(1)}, u32[]{:S(2)}, u32[]{:S(2)}) %collective-permute-start.2) | collective-permute-done | bytes 131104 | tf_op jit(solution)/shard_map/ppermute | solution.py:89
  55.7 3.2 %collective-permute-done.1 = f32[4,2,8,4,128]{4,2,3,1,0:T(8,128)S(1)} collective-permute-done((f32[4,2,8,4,128]{4,2,3,1,0:T(8,128)S(1)}, f32[4,2,8,4,128]{4,2,3,1,0:T(8,128)S(1)}, u32[]{:S(2)}, u32[]{:S(2)}) %collective-permute-start.1) | collective-permute-done | bytes 131104 | tf_op jit(solution)/shard_map/ppermute | solution.py:89
  58.9 0.0 copy-start.1
  59.0 9.9 %collective-permute-start.6 = (f32[2,8,4,128]{3,1,2,0:T(8,128)S(1)}, f32[2,8,4,128]{3,1,2,0:T(8,128)S(1)}, u32[]{:S(2)}, u32[]{:S(2)}) collective-permute-start(f32[2,8,4,128]{3,1,2,0:T(8,128)S(1)} %get-tuple-element.19), channel_id=1, source_target_pairs={{0,96},{16,112},{32,0},{48,16},{64,32},{80,48},{96,64},{112,80},{1... | collective-permute-start | bytes 98312 | tf_op jit(solution)/shard_map/ppermute | solution.py:89
  68.9 6.1 %collective-permute-start.5 = (f32[2,8,4,128]{3,1,2,0:T(8,128)S(1)}, f32[2,8,4,128]{3,1,2,0:T(8,128)S(1)}, u32[]{:S(2)}, u32[]{:S(2)}) collective-permute-start(f32[2,8,4,128]{3,1,2,0:T(8,128)S(1)} %get-tuple-element.20), channel_id=1, source_target_pairs={{0,64},{16,80},{32,96},{48,112},{64,0},{80,16},{96,32},{112,48},{1... | collective-permute-start | bytes 98312 | tf_op jit(solution)/shard_map/ppermute | solution.py:89
  75.0 6.1 %collective-permute-start.4 = (f32[2,8,4,128]{3,1,2,0:T(8,128)S(1)}, f32[2,8,4,128]{3,1,2,0:T(8,128)S(1)}, u32[]{:S(2)}, u32[]{:S(2)}) collective-permute-start(f32[2,8,4,128]{3,1,2,0:T(8,128)S(1)} %get-tuple-element.18), channel_id=1, source_target_pairs={{0,32},{16,48},{32,64},{48,80},{64,96},{80,112},{96,0},{112,16},{1... | collective-permute-start | bytes 98312 | tf_op jit(solution)/shard_map/ppermute | solution.py:89
  81.1 0.0 copy-done.1
  81.1 0.9 %convolution_convert_fusion = bf16[8,128,128]{1,2,0:T(8,128)(2,1)} fusion(bf16[1,8,128,128]{3,2,1,0:T(8,128)(2,1)S(1)} %copy-done.1, bf16[8,16,8,128]{3,2,0,1:T(8,128)(2,1)S(1)} %bitcast.91), kind=kOutput, calls=%fused_computation.8 | convolution fusion | flops 33685504 | bytes 786432 | tf_op jit(solution)/shard_map/ijt,ikj->ikt/dot_general | solution.py:126
  82.0 0.0 collective-permute-done.6
  82.0 0.4 collective-permute-done.5
  82.5 2.4 %collective-permute-done.4 = f32[2,8,4,128]{3,1,2,0:T(8,128)S(1)} collective-permute-done((f32[2,8,4,128]{3,1,2,0:T(8,128)S(1)}, f32[2,8,4,128]{3,1,2,0:T(8,128)S(1)}, u32[]{:S(2)}, u32[]{:S(2)}) %collective-permute-start.4) | collective-permute-done | bytes 32800 | tf_op jit(solution)/shard_map/ppermute | solution.py:89
  84.9 0.6 copy.61
  85.5 0.6 copy.62
  (9 shorter events, 0.2 us)
Async XLA Ops:
  0.6 20.0 %copy-start = (bf16[1,8,128,128]{3,2,1,0:T(8,128)(2,1)S(1)}, bf16[1,8,128,128]{3,2,1,0:T(8,128)(2,1)}, u32[]{:S(2)}) copy-start(bf16[1,8,128,128]{3,2,1,0:T(8,128)(2,1)} %param.7) | copy-start | bytes 786436
  2.2 18.5 %copy-start.3 = (bf16[1024,128]{1,0:T(8,128)(2,1)S(1)}, bf16[1024,128]{1,0:T(8,128)(2,1)}, u32[]{:S(2)}) copy-start(bf16[1024,128]{1,0:T(8,128)(2,1)} %param.5) | copy-start | bytes 786436
  23.2 13.0 %all-to-all-start.1 = ((bf16[128,8,128]{2,1,0:T(8,128)(2,1)}), bf16[128,8,128]{2,1,0:T(8,128)(2,1)S(1)}, u32[]{:S(2)}, u32[]{:S(2)}) async-start(bf16[128,8,128]{2,1,0:T(8,128)(2,1)} %copy.51), calls=%async_computation.1 | async-start | bytes 524288 | tf_op jit(solution)/shard_map/all_to_all | solution.py:130
  27.7 8.5 %copy-start.2 = (bf16[1024,128]{1,0:T(8,128)(2,1)S(1)}, bf16[1024,128]{1,0:T(8,128)(2,1)}, u32[]{:S(2)}) copy-start(bf16[1024,128]{1,0:T(8,128)(2,1)} %param.4) | copy-start | bytes 786436
  36.8 6.3 %collective-permute-start = (f32[4,4,2,8,4,128]{5,3,4,1,0,2:T(8,128)S(1)}, f32[4,4,2,8,4,128]{5,3,4,1,0,2:T(8,128)S(1)}, u32[]{:S(2)}, u32[]{:S(2)}) collective-permute-start(f32[4,4,2,8,4,128]{5,3,4,1,0,2:T(8,128)S(1)} %fusion.13), channel_id=1, source_target_pairs={{0,16},{16,0},{32,48},{48,32},{64,80},{80,64},{96,112},{112,96},{1... | collective-permute-start | bytes 1572872 | tf_op jit(solution)/shard_map/ppermute | solution.py:89
  43.3 9.7 %collective-permute-start.3 = (f32[4,2,8,4,128]{4,2,3,1,0:T(8,128)S(1)}, f32[4,2,8,4,128]{4,2,3,1,0:T(8,128)S(1)}, u32[]{:S(2)}, u32[]{:S(2)}) collective-permute-start(f32[4,2,8,4,128]{4,2,3,1,0:T(8,128)S(1)} %bitcast.98), channel_id=1, source_target_pairs={{0,384},{16,400},{32,416},{48,432},{64,448},{80,464},{96,480},{112... | collective-permute-start | bytes 393224 | tf_op jit(solution)/shard_map/ppermute | solution.py:89
  47.9 7.8 %collective-permute-start.2 = (f32[4,2,8,4,128]{4,2,3,1,0:T(8,128)S(1)}, f32[4,2,8,4,128]{4,2,3,1,0:T(8,128)S(1)}, u32[]{:S(2)}, u32[]{:S(2)}) collective-permute-start(f32[4,2,8,4,128]{4,2,3,1,0:T(8,128)S(1)} %bitcast.99), channel_id=1, source_target_pairs={{0,256},{16,272},{32,288},{48,304},{64,320},{80,336},{96,352},{112... | collective-permute-start | bytes 393224 | tf_op jit(solution)/shard_map/ppermute | solution.py:89
  50.2 8.7 %collective-permute-start.1 = (f32[4,2,8,4,128]{4,2,3,1,0:T(8,128)S(1)}, f32[4,2,8,4,128]{4,2,3,1,0:T(8,128)S(1)}, u32[]{:S(2)}, u32[]{:S(2)}) collective-permute-start(f32[4,2,8,4,128]{4,2,3,1,0:T(8,128)S(1)} %bitcast.100), channel_id=1, source_target_pairs={{0,128},{16,144},{32,160},{48,176},{64,192},{80,208},{96,224},{112... | collective-permute-start | bytes 393224 | tf_op jit(solution)/shard_map/ppermute | solution.py:89
  58.9 22.2 %copy-start.1 = (bf16[1,8,128,128]{3,2,1,0:T(8,128)(2,1)S(1)}, bf16[1,8,128,128]{3,2,1,0:T(8,128)(2,1)}, u32[]{:S(2)}) copy-start(bf16[1,8,128,128]{3,2,1,0:T(8,128)(2,1)} %param.6) | copy-start | bytes 786436
  59.0 23.0 %collective-permute-start.6 = (f32[2,8,4,128]{3,1,2,0:T(8,128)S(1)}, f32[2,8,4,128]{3,1,2,0:T(8,128)S(1)}, u32[]{:S(2)}, u32[]{:S(2)}) collective-permute-start(f32[2,8,4,128]{3,1,2,0:T(8,128)S(1)} %get-tuple-element.19), channel_id=1, source_target_pairs={{0,96},{16,112},{32,0},{48,16},{64,32},{80,48},{96,64},{112,80},{1... | collective-permute-start | bytes 98312 | tf_op jit(solution)/shard_map/ppermute | solution.py:89
  68.9 13.6 %collective-permute-start.5 = (f32[2,8,4,128]{3,1,2,0:T(8,128)S(1)}, f32[2,8,4,128]{3,1,2,0:T(8,128)S(1)}, u32[]{:S(2)}, u32[]{:S(2)}) collective-permute-start(f32[2,8,4,128]{3,1,2,0:T(8,128)S(1)} %get-tuple-element.20), channel_id=1, source_target_pairs={{0,64},{16,80},{32,96},{48,112},{64,0},{80,16},{96,32},{112,48},{1... | collective-permute-start | bytes 98312 | tf_op jit(solution)/shard_map/ppermute | solution.py:89
  75.0 9.9 %collective-permute-start.4 = (f32[2,8,4,128]{3,1,2,0:T(8,128)S(1)}, f32[2,8,4,128]{3,1,2,0:T(8,128)S(1)}, u32[]{:S(2)}, u32[]{:S(2)}) collective-permute-start(f32[2,8,4,128]{3,1,2,0:T(8,128)S(1)} %get-tuple-element.18), channel_id=1, source_target_pairs={{0,32},{16,48},{32,64},{48,80},{64,96},{80,112},{96,0},{112,16},{1... | collective-permute-start | bytes 98312 | tf_op jit(solution)/shard_map/ppermute | solution.py:89

commit v2 on v1

--- a/solution.py
+++ b/solution.py
@@ -77,16 +77,28 @@
     perm = [nlead + by_stride.index(s) for s in order]
     x = x.transpose(perm + list(range(nlead)) + list(range(nlead + len(stages), x.ndim)))
     me = lax.axis_index("dp")
-    for _, size, stride in order:
+    for distance, size, stride in order:
         mine = (me // stride) % size
-        total = lax.dynamic_index_in_dim(x, mine, 0, keepdims=False)
-        for shift in range(1, size):
-            pairs = []
+
+        def pick(shift, x=x, mine=mine, size=size):
+            return lax.dynamic_index_in_dim(x, (mine + shift) % size, 0, keepdims=False)
+
+        def pairs(shift, size=size, stride=stride):
+            out = []
             for d in range(count):
                 own = (d // stride) % size
-                pairs.append((d, d + (((own + shift) % size) - own) * stride))
-            send = lax.dynamic_index_in_dim(x, (mine + shift) % size, 0, keepdims=False)
-            total = total + lax.ppermute(send, "dp", perm=pairs)
+                out.append((d, d + (((own + shift) % size) - own) * stride))
+            return out
+
+        if size == 4 and distance > 1:
+            ahead = lax.ppermute(jnp.stack([pick(1), pick(2)], 0), "dp", perm=pairs(1))
+            behind = lax.ppermute(pick(-1), "dp", perm=pairs(-1))
+            relayed = lax.ppermute(ahead[1], "dp", perm=pairs(1))
+            x = pick(0) + ahead[0] + behind + relayed
+            continue
+        total = pick(0)
+        for shift in range(1, size):
+            total = total + lax.ppermute(pick(shift), "dp", perm=pairs(shift))
         x = total
     return x
 

time: 86.6 us -> 84.2 us (0.972)
  the two profiles are of different devices: /device:TPU:1 before, /device:TPU:2 now
where the time goes in v2:
time: 84.2 us; the launch traced here: 83.8 us
  starting transfers between devices  36.8 us (44%)
  waiting for transfers between devices  20.2 us (24%)
  blocking collectives  18.1 us (21%)
  matrix products  4.51 us (5%)
  local copies, waits for them, and re-layouts  2.96 us (4%)
  between operations  1.08 us (1%)
    all_to_all x1, blocking collectives, forward_layer(): lax.all_to_all(first_out, 'mp', split_axis=1, concat_axis=0, tiled=True)  18.1 us
    ppermute x4, starting transfers between devices, staged_reduce_scatter(): total = total + lax.ppermute(pick(shift), 'dp', perm=pairs(shift))  12.3 us
    ppermute x1, starting transfers between devices, staged_reduce_scatter(): ahead = lax.ppermute(jnp.stack([pick(1), pick(2)], 0), 'dp', perm=pairs(1))  9.24 us
    all_to_all x1, waiting for transfers between devices, shards(): lax.all_to_all(grad_first, 'mp', split_axis=0, concat_axis=1, tiled=True)  7.99 us
    ppermute x4, waiting for transfers between devices, staged_reduce_scatter(): total = total + lax.ppermute(pick(shift), 'dp', perm=pairs(shift))  7.71 us
    ppermute x1, starting transfers between devices, staged_reduce_scatter(): relayed = lax.ppermute(ahead[1], 'dp', perm=pairs(1))  7.27 us
    all_to_all x1, starting transfers between devices, shards(): lax.all_to_all(grad_first, 'mp', split_axis=0, concat_axis=1, tiled=True)  5.13 us
    ppermute x1, waiting for transfers between devices, staged_reduce_scatter(): relayed = lax.ppermute(ahead[1], 'dp', perm=pairs(1))  3.92 us
  transfers between devices with their start and end apart: 8, of which 6 were waited for; matrix products, arithmetic and copies ran while one was open for 2% of the time, Pallas kernels for 0%

profile of v2, /device:TPU:2, one launch (start us, length us, event | category | flops | bytes accessed | tf_op | source)
XLA Modules:
  0.0 83.8 jit_solution(3562103146383347827)
XLA Ops:
  0.6 0.0 copy-start
  0.6 1.3 %convolution_convert_fusion.2 = bf16[8,128,128]{2,1,0:T(8,128)(2,1)S(1)} fusion(bf16[8,128,128]{2,1,0:T(8,128)(2,1)} %bitcast.91, bf16[1,8,128,128]{3,2,1,0:T(8,128)(2,1)} %param.6), kind=kOutput, calls=%fused_computation.10 | convolution fusion | flops 33685504 | bytes 786432 | tf_op jit(solution)/shard_map/ikt,ikj->ijt/dot_general | solution.py:22
  2.0 0.2 copy.47
  2.2 0.0 copy-start.3
  2.2 18.1 %all_to_all.36 = bf16[8,128,128]{2,0,1:T(8,128)(2,1)S(1)} all-to-all(bf16[8,128,128]{2,0,1:T(8,128)(2,1)S(1)} %copy.47), channel_id=1, replica_groups=mesh['dp'=32,'mp'=16] {'mp'}, dimensions={1} | all-to-all | bytes 524288 | tf_op jit(solution)/shard_map/all_to_all | solution.py:30
  20.3 0.0 copy-done
  20.3 0.0 copy-done.3
  20.3 1.3 %fusion.4 = (bf16[8,128,128]{2,1,0:T(8,128)(2,1)S(1)}, bf16[8,128,128]{2,1,0:T(8,128)(2,1)}) fusion(bf16[8,128,128]{2,1,0:T(8,128)(2,1)S(1)} %bitcast.99, bf16[1,8,128,128]{3,2,1,0:T(8,128)(2,1)S(1)} %copy-done, bf16[8,16,8,128]{3,0,2,1:T(8,128)(2,1)S(1)} %bitcast.93), kind=kOutput, calls=%fused_computation.18 | convolution fusion | flops 36569088 | bytes 1310720 | tf_op jit(solution)/shard_map/ijt,jim->jmt/dot_general | solution.py:14
  21.7 0.3 fusion.1
  22.0 0.9 %copy.51 = bf16[128,8,128]{2,1,0:T(8,128)(2,1)} copy(bf16[128,8,128]{0,2,1:T(8,128)(2,1)S(1)} %fusion.1) | data formatting | bytes 524288 | tf_op jit(solution)/shard_map/convert_element_type | solution.py:135
  22.9 5.1 %all-to-all-start.1 = ((bf16[128,8,128]{2,1,0:T(8,128)(2,1)}), bf16[128,8,128]{2,1,0:T(8,128)(2,1)S(1)}, u32[]{:S(2)}, u32[]{:S(2)}) async-start(bf16[128,8,128]{2,1,0:T(8,128)(2,1)} %copy.51), calls=%async_computation.1 | async-start | bytes 524288 | tf_op jit(solution)/shard_map/all_to_all | solution.py:142
  28.0 0.3 convolution_multiply_fusion.1
  28.3 0.0 copy-start.2
  28.3 0.3 copy.55
  28.6 8.0 %all-to-all-done.1 = bf16[128,8,128]{2,1,0:T(8,128)(2,1)S(1)} async-done(((bf16[128,8,128]{2,1,0:T(8,128)(2,1)}), bf16[128,8,128]{2,1,0:T(8,128)(2,1)S(1)}, u32[]{:S(2)}, u32[]{:S(2)}) %all-to-all-start.1) | async-done | bytes 262176 | tf_op jit(solution)/shard_map/all_to_all | solution.py:142
  36.6 0.0 copy-done.2
  36.6 0.3 fusion
  36.9 0.2 copy.54
  37.2 1.9 %collective-permute-start = (f32[4,4,2,8,4,128]{5,3,4,1,0,2:T(8,128)S(1)}, f32[4,4,2,8,4,128]{5,3,4,1,0,2:T(8,128)S(1)}, u32[]{:S(2)}, u32[]{:S(2)}) collective-permute-start(f32[4,4,2,8,4,128]{5,3,4,1,0,2:T(8,128)S(1)} %fusion.13), channel_id=1, source_target_pairs={{0,16},{16,0},{32,48},{48,32},{64,80},{80,64},{96,112},{112,96},{1... | collective-permute-start | bytes 1572872 | tf_op jit(solution)/shard_map/ppermute | solution.py:101
  39.3 1.8 %collective-permute-done = f32[4,4,2,8,4,128]{5,3,4,1,0,2:T(8,128)S(1)} collective-permute-done((f32[4,4,2,8,4,128]{5,3,4,1,0,2:T(8,128)S(1)}, f32[4,4,2,8,4,128]{5,3,4,1,0,2:T(8,128)S(1)}, u32[]{:S(2)}, u32[]{:S(2)}) %collective-permute-start) | collective-permute-done | bytes 524320 | tf_op jit(solution)/shard_map/ppermute | solution.py:101
  41.0 0.1 fusion.16
  41.2 4.9 %collective-permute-start.3 = (f32[4,2,8,4,128]{4,2,3,1,0:T(8,128)S(1)}, f32[4,2,8,4,128]{4,2,3,1,0:T(8,128)S(1)}, u32[]{:S(2)}, u32[]{:S(2)}) collective-permute-start(f32[4,2,8,4,128]{4,2,3,1,0:T(8,128)S(1)} %bitcast.96), channel_id=1, source_target_pairs={{0,384},{16,400},{32,416},{48,432},{64,448},{80,464},{96,480},{112... | collective-permute-start | bytes 393224 | tf_op jit(solution)/shard_map/ppermute | solution.py:101
  46.2 2.5 %collective-permute-start.2 = (f32[4,2,8,4,128]{4,2,3,1,0:T(8,128)S(1)}, f32[4,2,8,4,128]{4,2,3,1,0:T(8,128)S(1)}, u32[]{:S(2)}, u32[]{:S(2)}) collective-permute-start(f32[4,2,8,4,128]{4,2,3,1,0:T(8,128)S(1)} %bitcast.97), channel_id=1, source_target_pairs={{0,256},{16,272},{32,288},{48,304},{64,320},{80,336},{96,352},{112... | collective-permute-start | bytes 393224 | tf_op jit(solution)/shard_map/ppermute | solution.py:101
  48.7 2.9 %collective-permute-start.1 = (f32[4,2,8,4,128]{4,2,3,1,0:T(8,128)S(1)}, f32[4,2,8,4,128]{4,2,3,1,0:T(8,128)S(1)}, u32[]{:S(2)}, u32[]{:S(2)}) collective-permute-start(f32[4,2,8,4,128]{4,2,3,1,0:T(8,128)S(1)} %bitcast.98), channel_id=1, source_target_pairs={{0,128},{16,144},{32,160},{48,176},{64,192},{80,208},{96,224},{112... | collective-permute-start | bytes 393224 | tf_op jit(solution)/shard_map/ppermute | solution.py:101
  51.7 0.0 collective-permute-done.3
  51.7 4.0 %collective-permute-done.2 = f32[4,2,8,4,128]{4,2,3,1,0:T(8,128)S(1)} collective-permute-done((f32[4,2,8,4,128]{4,2,3,1,0:T(8,128)S(1)}, f32[4,2,8,4,128]{4,2,3,1,0:T(8,128)S(1)}, u32[]{:S(2)}, u32[]{:S(2)}) %collective-permute-start.2) | collective-permute-done | bytes 131104 | tf_op jit(solution)/shard_map/ppermute | solution.py:101
  55.7 2.0 %collective-permute-done.1 = f32[4,2,8,4,128]{4,2,3,1,0:T(8,128)S(1)} collective-permute-done((f32[4,2,8,4,128]{4,2,3,1,0:T(8,128)S(1)}, f32[4,2,8,4,128]{4,2,3,1,0:T(8,128)S(1)}, u32[]{:S(2)}, u32[]{:S(2)}) %collective-permute-start.1) | collective-permute-done | bytes 131104 | tf_op jit(solution)/shard_map/ppermute | solution.py:101
  57.7 0.0 copy-start.1
  57.7 9.2 %collective-permute-start.4 = (f32[2,2,8,4,128]{4,2,3,1,0:T(8,128)S(1)}, f32[2,2,8,4,128]{4,2,3,1,0:T(8,128)S(1)}, u32[]{:S(2)}, u32[]{:S(2)}) collective-permute-start(f32[2,2,8,4,128]{4,2,3,1,0:T(8,128)S(1)} %pad_maximum_fusion), channel_id=1, source_target_pairs={{0,32},{16,48},{32,64},{48,80},{64,96},{80,112},{96,0},{112,16},{1... | collective-permute-start | bytes 196616 | tf_op jit(solution)/shard_map/ppermute | solution.py:94
  67.0 2.8 %collective-permute-start.5 = (f32[2,8,4,128]{3,1,2,0:T(8,128)S(1)}, f32[2,8,4,128]{3,1,2,0:T(8,128)S(1)}, u32[]{:S(2)}, u32[]{:S(2)}) collective-permute-start(f32[2,8,4,128]{3,1,2,0:T(8,128)S(1)} %get-tuple-element.18), channel_id=1, source_target_pairs={{0,96},{16,112},{32,0},{48,16},{64,32},{80,48},{96,64},{112,80},{1... | collective-permute-start | bytes 98312 | tf_op jit(solution)/shard_map/ppermute | solution.py:95
  69.9 0.5 collective-permute-done.4
  70.4 7.3 %collective-permute-start.6 = (f32[2,8,4,128]{3,1,2,0:T(8,128)S(1)}, f32[2,8,4,128]{3,1,2,0:T(8,128)S(1)}, u32[]{:S(2)}, u32[]{:S(2)}) collective-permute-start(f32[2,8,4,128]{3,1,2,0:T(8,128)S(1)} %slice_bitcast_fusion), channel_id=1, source_target_pairs={{0,32},{16,48},{32,64},{48,80},{64,96},{80,112},{96,0},{112,16},{1... | collective-permute-start | bytes 98312 | tf_op jit(solution)/shard_map/ppermute | solution.py:96
  77.7 0.0 copy-done.1
  77.7 0.9 %convolution_convert_fusion = bf16[8,128,128]{1,2,0:T(8,128)(2,1)} fusion(bf16[1,8,128,128]{3,2,1,0:T(8,128)(2,1)S(1)} %copy-done.1, bf16[8,16,8,128]{3,2,0,1:T(8,128)(2,1)S(1)} %bitcast.89), kind=kOutput, calls=%fused_computation.8 | convolution fusion | flops 33685504 | bytes 786432 | tf_op jit(solution)/shard_map/ijt,ikj->ikt/dot_general | solution.py:138
  78.6 0.0 collective-permute-done.5
  78.6 3.9 %collective-permute-done.6 = f32[2,8,4,128]{3,1,2,0:T(8,128)S(1)} collective-permute-done((f32[2,8,4,128]{3,1,2,0:T(8,128)S(1)}, f32[2,8,4,128]{3,1,2,0:T(8,128)S(1)}, u32[]{:S(2)}, u32[]{:S(2)}) %collective-permute-start.6) | collective-permute-done | bytes 32800 | tf_op jit(solution)/shard_map/ppermute | solution.py:96
  82.6 0.6 copy.61
  83.2 0.6 copy.62
  (11 shorter events, 0.2 us)
Async XLA Ops:
  0.6 19.7 %copy-start = (bf16[1,8,128,128]{3,2,1,0:T(8,128)(2,1)S(1)}, bf16[1,8,128,128]{3,2,1,0:T(8,128)(2,1)}, u32[]{:S(2)}) copy-start(bf16[1,8,128,128]{3,2,1,0:T(8,128)(2,1)} %param.7) | copy-start | bytes 786436
  2.2 18.2 %copy-start.3 = (bf16[1024,128]{1,0:T(8,128)(2,1)S(1)}, bf16[1024,128]{1,0:T(8,128)(2,1)}, u32[]{:S(2)}) copy-start(bf16[1024,128]{1,0:T(8,128)(2,1)} %param.5) | copy-start | bytes 786436
  22.9 13.7 %all-to-all-start.1 = ((bf16[128,8,128]{2,1,0:T(8,128)(2,1)}), bf16[128,8,128]{2,1,0:T(8,128)(2,1)S(1)}, u32[]{:S(2)}, u32[]{:S(2)}) async-start(bf16[128,8,128]{2,1,0:T(8,128)(2,1)} %copy.51), calls=%async_computation.1 | async-start | bytes 524288 | tf_op jit(solution)/shard_map/all_to_all | solution.py:142
  28.3 8.3 %copy-start.2 = (bf16[1024,128]{1,0:T(8,128)(2,1)S(1)}, bf16[1024,128]{1,0:T(8,128)(2,1)}, u32[]{:S(2)}) copy-start(bf16[1024,128]{1,0:T(8,128)(2,1)} %param.4) | copy-start | bytes 786436
  37.2 3.8 %collective-permute-start = (f32[4,4,2,8,4,128]{5,3,4,1,0,2:T(8,128)S(1)}, f32[4,4,2,8,4,128]{5,3,4,1,0,2:T(8,128)S(1)}, u32[]{:S(2)}, u32[]{:S(2)}) collective-permute-start(f32[4,4,2,8,4,128]{5,3,4,1,0,2:T(8,128)S(1)} %fusion.13), channel_id=1, source_target_pairs={{0,16},{16,0},{32,48},{48,32},{64,80},{80,64},{96,112},{112,96},{1... | collective-permute-start | bytes 1572872 | tf_op jit(solution)/shard_map/ppermute | solution.py:101
  41.2 10.5 %collective-permute-start.3 = (f32[4,2,8,4,128]{4,2,3,1,0:T(8,128)S(1)}, f32[4,2,8,4,128]{4,2,3,1,0:T(8,128)S(1)}, u32[]{:S(2)}, u32[]{:S(2)}) collective-permute-start(f32[4,2,8,4,128]{4,2,3,1,0:T(8,128)S(1)} %bitcast.96), channel_id=1, source_target_pairs={{0,384},{16,400},{32,416},{48,432},{64,448},{80,464},{96,480},{112... | collective-permute-start | bytes 393224 | tf_op jit(solution)/shard_map/ppermute | solution.py:101
  46.2 9.5 %collective-permute-start.2 = (f32[4,2,8,4,128]{4,2,3,1,0:T(8,128)S(1)}, f32[4,2,8,4,128]{4,2,3,1,0:T(8,128)S(1)}, u32[]{:S(2)}, u32[]{:S(2)}) collective-permute-start(f32[4,2,8,4,128]{4,2,3,1,0:T(8,128)S(1)} %bitcast.97), channel_id=1, source_target_pairs={{0,256},{16,272},{32,288},{48,304},{64,320},{80,336},{96,352},{112... | collective-permute-start | bytes 393224 | tf_op jit(solution)/shard_map/ppermute | solution.py:101
  48.7 8.9 %collective-permute-start.1 = (f32[4,2,8,4,128]{4,2,3,1,0:T(8,128)S(1)}, f32[4,2,8,4,128]{4,2,3,1,0:T(8,128)S(1)}, u32[]{:S(2)}, u32[]{:S(2)}) collective-permute-start(f32[4,2,8,4,128]{4,2,3,1,0:T(8,128)S(1)} %bitcast.98), channel_id=1, source_target_pairs={{0,128},{16,144},{32,160},{48,176},{64,192},{80,208},{96,224},{112... | collective-permute-start | bytes 393224 | tf_op jit(solution)/shard_map/ppermute | solution.py:101
  57.7 20.0 %copy-start.1 = (bf16[1,8,128,128]{3,2,1,0:T(8,128)(2,1)S(1)}, bf16[1,8,128,128]{3,2,1,0:T(8,128)(2,1)}, u32[]{:S(2)}) copy-start(bf16[1,8,128,128]{3,2,1,0:T(8,128)(2,1)} %param.6) | copy-start | bytes 786436
  57.7 12.7 %collective-permute-start.4 = (f32[2,2,8,4,128]{4,2,3,1,0:T(8,128)S(1)}, f32[2,2,8,4,128]{4,2,3,1,0:T(8,128)S(1)}, u32[]{:S(2)}, u32[]{:S(2)}) collective-permute-start(f32[2,2,8,4,128]{4,2,3,1,0:T(8,128)S(1)} %pad_maximum_fusion), channel_id=1, source_target_pairs={{0,32},{16,48},{32,64},{48,80},{64,96},{80,112},{96,0},{112,16},{1... | collective-permute-start | bytes 196616 | tf_op jit(solution)/shard_map/ppermute | solution.py:94
  67.0 11.6 %collective-permute-start.5 = (f32[2,8,4,128]{3,1,2,0:T(8,128)S(1)}, f32[2,8,4,128]{3,1,2,0:T(8,128)S(1)}, u32[]{:S(2)}, u32[]{:S(2)}) collective-permute-start(f32[2,8,4,128]{3,1,2,0:T(8,128)S(1)} %get-tuple-element.18), channel_id=1, source_target_pairs={{0,96},{16,112},{32,0},{48,16},{64,32},{80,48},{96,64},{112,80},{1... | collective-permute-start | bytes 98312 | tf_op jit(solution)/shard_map/ppermute | solution.py:95
  70.4 12.1 %collective-permute-start.6 = (f32[2,8,4,128]{3,1,2,0:T(8,128)S(1)}, f32[2,8,4,128]{3,1,2,0:T(8,128)S(1)}, u32[]{:S(2)}, u32[]{:S(2)}) collective-permute-start(f32[2,8,4,128]{3,1,2,0:T(8,128)S(1)} %slice_bitcast_fusion), channel_id=1, source_target_pairs={{0,32},{16,48},{32,64},{48,80},{64,96},{80,112},{96,0},{112,16},{1... | collective-permute-start | bytes 98312 | tf_op jit(solution)/shard_map/ppermute | solution.py:96

commit v3 on v2

--- a/solution.py
+++ b/solution.py
@@ -98,7 +98,8 @@
             continue
         total = pick(0)
         for shift in range(1, size):
-            total = total + lax.ppermute(pick(shift), "dp", perm=pairs(shift))
+            sent = lax.ppermute(pick(shift).astype(jnp.bfloat16), "dp", perm=pairs(shift))
+            total = total + sent.astype(total.dtype)
         x = total
     return x
 

time: 84.2 us -> 81.6 us (0.969)
  waiting for transfers between devices: 20.2 us -> 17.7 us
    ppermute x4, waiting for transfers between devices: 7.71 us -> 5.76 us  [staged_reduce_scatter(): lax.ppermute(pick(shift).astype(jnp.bfloat16), 'dp', perm=pairs(shift))]
    ppermute x1, waiting for transfers between devices: 3.92 us -> 2.96 us  [staged_reduce_scatter(): relayed = lax.ppermute(ahead[1], 'dp', perm=pairs(1))]
where the time goes in v3:
time: 81.6 us; the launch traced here: 81.1 us
  starting transfers between devices  36.6 us (45%)
  blocking collectives  18.1 us (22%)
  waiting for transfers between devices  17.7 us (22%)
  matrix products  4.51 us (6%)
  local copies, waits for them, and re-layouts  2.92 us (4%)
  between operations  1.06 us (1%)
    all_to_all x1, blocking collectives, forward_layer(): lax.all_to_all(first_out, 'mp', split_axis=1, concat_axis=0, tiled=True)  18.1 us
    ppermute x4, starting transfers between devices, staged_reduce_scatter(): lax.ppermute(pick(shift).astype(jnp.bfloat16), 'dp', perm=pairs(shift))  12.3 us
    ppermute x1, starting transfers between devices, staged_reduce_scatter(): ahead = lax.ppermute(jnp.stack([pick(1), pick(2)], 0), 'dp', perm=pairs(1))  9.24 us
    all_to_all x1, waiting for transfers between devices, shards(): lax.all_to_all(grad_first, 'mp', split_axis=0, concat_axis=1, tiled=True)  7.99 us
    ppermute x1, starting transfers between devices, staged_reduce_scatter(): relayed = lax.ppermute(ahead[1], 'dp', perm=pairs(1))  7.11 us
    ppermute x4, waiting for transfers between devices, staged_reduce_scatter(): lax.ppermute(pick(shift).astype(jnp.bfloat16), 'dp', perm=pairs(shift))  5.76 us
    all_to_all x1, starting transfers between devices, shards(): lax.all_to_all(grad_first, 'mp', split_axis=0, concat_axis=1, tiled=True)  5.13 us
    ppermute x1, waiting for transfers between devices, staged_reduce_scatter(): relayed = lax.ppermute(ahead[1], 'dp', perm=pairs(1))  2.96 us
  transfers between devices with their start and end apart: 8, of which 6 were waited for; matrix products, arithmetic and copies ran while one was open for 2% of the time, Pallas kernels for 0%

profile of v3, /device:TPU:2, one launch (start us, length us, event | category | flops | bytes accessed | tf_op | source)
XLA Modules:
  0.0 81.1 jit_solution(10472553743738586615)
XLA Ops:
  0.6 0.0 copy-start
  0.6 1.3 %convolution_convert_fusion.2 = bf16[8,128,128]{2,1,0:T(8,128)(2,1)S(1)} fusion(bf16[8,128,128]{2,1,0:T(8,128)(2,1)} %bitcast.108, bf16[1,8,128,128]{3,2,1,0:T(8,128)(2,1)} %param.6), kind=kOutput, calls=%fused_computation.10 | convolution fusion | flops 33685504 | bytes 786432 | tf_op jit(solution)/shard_map/ikt,ikj->ijt/dot_general | solution.py:22
  2.0 0.2 copy.33
  2.2 0.0 copy-start.3
  2.2 18.1 %all_to_all.36 = bf16[8,128,128]{2,0,1:T(8,128)(2,1)S(1)} all-to-all(bf16[8,128,128]{2,0,1:T(8,128)(2,1)S(1)} %copy.33), channel_id=1, replica_groups=mesh['dp'=32,'mp'=16] {'mp'}, dimensions={1} | all-to-all | bytes 524288 | tf_op jit(solution)/shard_map/all_to_all | solution.py:30
  20.3 0.0 copy-done
  20.3 0.0 copy-done.3
  20.3 1.3 %fusion.4 = (bf16[8,128,128]{2,1,0:T(8,128)(2,1)S(1)}, bf16[8,128,128]{2,1,0:T(8,128)(2,1)}) fusion(bf16[8,128,128]{2,1,0:T(8,128)(2,1)S(1)} %bitcast.113, bf16[1,8,128,128]{3,2,1,0:T(8,128)(2,1)S(1)} %copy-done, bf16[8,16,8,128]{3,0,2,1:T(8,128)(2,1)S(1)} %bitcast.110), kind=kOutput, calls=%fused_computation.18 | convolution fusion | flops 36569088 | bytes 1310720 | tf_op jit(solution)/shard_map/ijt,jim->jmt/dot_general | solution.py:14
  21.7 0.3 fusion.1
  22.0 0.9 %copy.37 = bf16[128,8,128]{2,1,0:T(8,128)(2,1)} copy(bf16[128,8,128]{0,2,1:T(8,128)(2,1)S(1)} %fusion.1) | data formatting | bytes 524288 | tf_op jit(solution)/shard_map/convert_element_type | solution.py:136
  22.9 5.1 %all-to-all-start.1 = ((bf16[128,8,128]{2,1,0:T(8,128)(2,1)}), bf16[128,8,128]{2,1,0:T(8,128)(2,1)S(1)}, u32[]{:S(2)}, u32[]{:S(2)}) async-start(bf16[128,8,128]{2,1,0:T(8,128)(2,1)} %copy.37), calls=%async_computation.1 | async-start | bytes 524288 | tf_op jit(solution)/shard_map/all_to_all | solution.py:143
  28.0 0.3 convolution_multiply_fusion.1
  28.3 0.0 copy-start.2
  28.3 0.3 copy.41
  28.6 8.0 %all-to-all-done.1 = bf16[128,8,128]{2,1,0:T(8,128)(2,1)S(1)} async-done(((bf16[128,8,128]{2,1,0:T(8,128)(2,1)}), bf16[128,8,128]{2,1,0:T(8,128)(2,1)S(1)}, u32[]{:S(2)}, u32[]{:S(2)}) %all-to-all-start.1) | async-done | bytes 262176 | tf_op jit(solution)/shard_map/all_to_all | solution.py:143
  36.6 0.0 copy-done.2
  36.6 0.3 fusion
  36.9 0.2 copy.40
  37.2 1.9 %collective-permute-start = (bf16[4,4,2,8,4,128]{5,3,4,1,0,2:T(8,128)(2,1)S(1)}, bf16[4,4,2,8,4,128]{5,3,4,1,0,2:T(8,128)(2,1)S(1)}, u32[]{:S(2)}, u32[]{:S(2)}) collective-permute-start(bf16[4,4,2,8,4,128]{5,3,4,1,0,2:T(8,128)(2,1)S(1)} %fusion.17), channel_id=1, source_target_pairs={{0,16},{16,0},{32,48},{48,32},{64,80},{80,64},{96,112},{112,96},{1... | collective-permute-start | bytes 786440 | tf_op jit(solution)/shard_map/ppermute | solution.py:101
  39.3 1.4 %collective-permute-done = bf16[4,4,2,8,4,128]{5,3,4,1,0,2:T(8,128)(2,1)S(1)} collective-permute-done((bf16[4,4,2,8,4,128]{5,3,4,1,0,2:T(8,128)(2,1)S(1)}, bf16[4,4,2,8,4,128]{5,3,4,1,0,2:T(8,128)(2,1)S(1)}, u32[]{:S(2)}, u32[]{:S(2)}) %collective-permute-start) | collective-permute-done | bytes 262176 | tf_op jit(solution)/shard_map/ppermute | solution.py:101
  40.7 0.1 fusion.16
  40.8 4.9 %collective-permute-start.3 = (bf16[4,2,8,4,128]{4,2,3,0,1:T(8,128)(2,1)S(1)}, bf16[4,2,8,4,128]{4,2,3,0,1:T(8,128)(2,1)S(1)}, u32[]{:S(2)}, u32[]{:S(2)}) collective-permute-start(bf16[4,2,8,4,128]{4,2,3,0,1:T(8,128)(2,1)S(1)} %get-tuple-element.13), channel_id=1, source_target_pairs={{0,384},{16,400},{32,416},{48,432},{64,448},{80,464},{96,480},{112... | collective-permute-start | bytes 196616 | tf_op jit(solution)/shard_map/ppermute | solution.py:101
  45.7 2.5 %collective-permute-start.2 = (bf16[4,2,8,4,128]{4,2,3,0,1:T(8,128)(2,1)S(1)}, bf16[4,2,8,4,128]{4,2,3,0,1:T(8,128)(2,1)S(1)}, u32[]{:S(2)}, u32[]{:S(2)}) collective-permute-start(bf16[4,2,8,4,128]{4,2,3,0,1:T(8,128)(2,1)S(1)} %get-tuple-element.14), channel_id=1, source_target_pairs={{0,256},{16,272},{32,288},{48,304},{64,320},{80,336},{96,352},{112... | collective-permute-start | bytes 196616 | tf_op jit(solution)/shard_map/ppermute | solution.py:101
  48.3 2.9 %collective-permute-start.1 = (bf16[4,2,8,4,128]{4,2,3,0,1:T(8,128)(2,1)S(1)}, bf16[4,2,8,4,128]{4,2,3,0,1:T(8,128)(2,1)S(1)}, u32[]{:S(2)}, u32[]{:S(2)}) collective-permute-start(bf16[4,2,8,4,128]{4,2,3,0,1:T(8,128)(2,1)S(1)} %get-tuple-element.12), channel_id=1, source_target_pairs={{0,128},{16,144},{32,160},{48,176},{64,192},{80,208},{96,224},{112... | collective-permute-start | bytes 196616 | tf_op jit(solution)/shard_map/ppermute | solution.py:101
  51.3 0.0 collective-permute-done.3
  51.3 2.1 %collective-permute-done.2 = bf16[4,2,8,4,128]{4,2,3,0,1:T(8,128)(2,1)S(1)} collective-permute-done((bf16[4,2,8,4,128]{4,2,3,0,1:T(8,128)(2,1)S(1)}, bf16[4,2,8,4,128]{4,2,3,0,1:T(8,128)(2,1)S(1)}, u32[]{:S(2)}, u32[]{:S(2)}) %collective-permute-start.2) | collective-permute-done | bytes 65568 | tf_op jit(solution)/shard_map/ppermute | solution.py:101
  53.4 2.2 %collective-permute-done.1 = bf16[4,2,8,4,128]{4,2,3,0,1:T(8,128)(2,1)S(1)} collective-permute-done((bf16[4,2,8,4,128]{4,2,3,0,1:T(8,128)(2,1)S(1)}, bf16[4,2,8,4,128]{4,2,3,0,1:T(8,128)(2,1)S(1)}, u32[]{:S(2)}, u32[]{:S(2)}) %collective-permute-start.1) | collective-permute-done | bytes 65568 | tf_op jit(solution)/shard_map/ppermute | solution.py:101
  55.7 0.0 copy-start.1
  55.7 9.2 %collective-permute-start.4 = (f32[2,2,8,4,128]{4,2,3,0,1:T(8,128)S(1)}, f32[2,2,8,4,128]{4,2,3,0,1:T(8,128)S(1)}, u32[]{:S(2)}, u32[]{:S(2)}) collective-permute-start(f32[2,2,8,4,128]{4,2,3,0,1:T(8,128)S(1)} %pad_maximum_fusion), channel_id=1, source_target_pairs={{0,32},{16,48},{32,64},{48,80},{64,96},{80,112},{96,0},{112,16},{1... | collective-permute-start | bytes 196616 | tf_op jit(solution)/shard_map/ppermute | solution.py:94
  65.0 2.8 %collective-permute-start.5 = (f32[2,8,4,128]{3,1,2,0:T(8,128)S(1)}, f32[2,8,4,128]{3,1,2,0:T(8,128)S(1)}, u32[]{:S(2)}, u32[]{:S(2)}) collective-permute-start(f32[2,8,4,128]{3,1,2,0:T(8,128)S(1)} %get-tuple-element.17), channel_id=1, source_target_pairs={{0,96},{16,112},{32,0},{48,16},{64,32},{80,48},{96,64},{112,80},{1... | collective-permute-start | bytes 98312 | tf_op jit(solution)/shard_map/ppermute | solution.py:95
  67.9 1.0 %collective-permute-done.4 = f32[2,2,8,4,128]{4,2,3,0,1:T(8,128)S(1)} collective-permute-done((f32[2,2,8,4,128]{4,2,3,0,1:T(8,128)S(1)}, f32[2,2,8,4,128]{4,2,3,0,1:T(8,128)S(1)}, u32[]{:S(2)}, u32[]{:S(2)}) %collective-permute-start.4) | collective-permute-done | bytes 65568 | tf_op jit(solution)/shard_map/ppermute | solution.py:94
  68.9 7.1 %collective-permute-start.6 = (f32[2,8,4,128]{3,1,2,0:T(8,128)S(1)}, f32[2,8,4,128]{3,1,2,0:T(8,128)S(1)}, u32[]{:S(2)}, u32[]{:S(2)}) collective-permute-start(f32[2,8,4,128]{3,1,2,0:T(8,128)S(1)} %slice_bitcast_fusion), channel_id=1, source_target_pairs={{0,32},{16,48},{32,64},{48,80},{64,96},{80,112},{96,0},{112,16},{1... | collective-permute-start | bytes 98312 | tf_op jit(solution)/shard_map/ppermute | solution.py:96
  76.0 0.0 copy-done.1
  76.0 0.9 %convolution_convert_fusion = bf16[8,128,128]{1,2,0:T(8,128)(2,1)} fusion(bf16[1,8,128,128]{3,2,1,0:T(8,128)(2,1)S(1)} %copy-done.1, bf16[8,16,8,128]{3,2,0,1:T(8,128)(2,1)S(1)} %bitcast.106), kind=kOutput, calls=%fused_computation.8 | convolution fusion | flops 33685504 | bytes 786432 | tf_op jit(solution)/shard_map/ijt,ikj->ikt/dot_general | solution.py:139
  76.9 0.0 collective-permute-done.5
  76.9 3.0 %collective-permute-done.6 = f32[2,8,4,128]{3,1,2,0:T(8,128)S(1)} collective-permute-done((f32[2,8,4,128]{3,1,2,0:T(8,128)S(1)}, f32[2,8,4,128]{3,1,2,0:T(8,128)S(1)}, u32[]{:S(2)}, u32[]{:S(2)}) %collective-permute-start.6) | collective-permute-done | bytes 32800 | tf_op jit(solution)/shard_map/ppermute | solution.py:96
  79.9 0.6 copy.47
  80.5 0.6 copy.48
  (8 shorter events, 0.2 us)
Async XLA Ops:
  0.6 19.7 %copy-start = (bf16[1,8,128,128]{3,2,1,0:T(8,128)(2,1)S(1)}, bf16[1,8,128,128]{3,2,1,0:T(8,128)(2,1)}, u32[]{:S(2)}) copy-start(bf16[1,8,128,128]{3,2,1,0:T(8,128)(2,1)} %param.7) | copy-start | bytes 786436
  2.2 18.2 %copy-start.3 = (bf16[1024,128]{1,0:T(8,128)(2,1)S(1)}, bf16[1024,128]{1,0:T(8,128)(2,1)}, u32[]{:S(2)}) copy-start(bf16[1024,128]{1,0:T(8,128)(2,1)} %param.5) | copy-start | bytes 786436
  22.9 13.7 %all-to-all-start.1 = ((bf16[128,8,128]{2,1,0:T(8,128)(2,1)}), bf16[128,8,128]{2,1,0:T(8,128)(2,1)S(1)}, u32[]{:S(2)}, u32[]{:S(2)}) async-start(bf16[128,8,128]{2,1,0:T(8,128)(2,1)} %copy.37), calls=%async_computation.1 | async-start | bytes 524288 | tf_op jit(solution)/shard_map/all_to_all | solution.py:143
  28.3 8.3 %copy-start.2 = (bf16[1024,128]{1,0:T(8,128)(2,1)S(1)}, bf16[1024,128]{1,0:T(8,128)(2,1)}, u32[]{:S(2)}) copy-start(bf16[1024,128]{1,0:T(8,128)(2,1)} %param.4) | copy-start | bytes 786436
  37.2 3.4 %collective-permute-start = (bf16[4,4,2,8,4,128]{5,3,4,1,0,2:T(8,128)(2,1)S(1)}, bf16[4,4,2,8,4,128]{5,3,4,1,0,2:T(8,128)(2,1)S(1)}, u32[]{:S(2)}, u32[]{:S(2)}) collective-permute-start(bf16[4,4,2,8,4,128]{5,3,4,1,0,2:T(8,128)(2,1)S(1)} %fusion.17), channel_id=1, source_target_pairs={{0,16},{16,0},{32,48},{48,32},{64,80},{80,64},{96,112},{112,96},{1... | collective-permute-start | bytes 786440 | tf_op jit(solution)/shard_map/ppermute | solution.py:101
  40.8 10.5 %collective-permute-start.3 = (bf16[4,2,8,4,128]{4,2,3,0,1:T(8,128)(2,1)S(1)}, bf16[4,2,8,4,128]{4,2,3,0,1:T(8,128)(2,1)S(1)}, u32[]{:S(2)}, u32[]{:S(2)}) collective-permute-start(bf16[4,2,8,4,128]{4,2,3,0,1:T(8,128)(2,1)S(1)} %get-tuple-element.13), channel_id=1, source_target_pairs={{0,384},{16,400},{32,416},{48,432},{64,448},{80,464},{96,480},{112... | collective-permute-start | bytes 196616 | tf_op jit(solution)/shard_map/ppermute | solution.py:101
  45.7 7.7 %collective-permute-start.2 = (bf16[4,2,8,4,128]{4,2,3,0,1:T(8,128)(2,1)S(1)}, bf16[4,2,8,4,128]{4,2,3,0,1:T(8,128)(2,1)S(1)}, u32[]{:S(2)}, u32[]{:S(2)}) collective-permute-start(bf16[4,2,8,4,128]{4,2,3,0,1:T(8,128)(2,1)S(1)} %get-tuple-element.14), channel_id=1, source_target_pairs={{0,256},{16,272},{32,288},{48,304},{64,320},{80,336},{96,352},{112... | collective-permute-start | bytes 196616 | tf_op jit(solution)/shard_map/ppermute | solution.py:101
  48.3 7.4 %collective-permute-start.1 = (bf16[4,2,8,4,128]{4,2,3,0,1:T(8,128)(2,1)S(1)}, bf16[4,2,8,4,128]{4,2,3,0,1:T(8,128)(2,1)S(1)}, u32[]{:S(2)}, u32[]{:S(2)}) collective-permute-start(bf16[4,2,8,4,128]{4,2,3,0,1:T(8,128)(2,1)S(1)} %get-tuple-element.12), channel_id=1, source_target_pairs={{0,128},{16,144},{32,160},{48,176},{64,192},{80,208},{96,224},{112... | collective-permute-start | bytes 196616 | tf_op jit(solution)/shard_map/ppermute | solution.py:101
  55.7 20.3 %copy-start.1 = (bf16[1,8,128,128]{3,2,1,0:T(8,128)(2,1)S(1)}, bf16[1,8,128,128]{3,2,1,0:T(8,128)(2,1)}, u32[]{:S(2)}) copy-start(bf16[1,8,128,128]{3,2,1,0:T(8,128)(2,1)} %param.6) | copy-start | bytes 786436
  55.7 13.1 %collective-permute-start.4 = (f32[2,2,8,4,128]{4,2,3,0,1:T(8,128)S(1)}, f32[2,2,8,4,128]{4,2,3,0,1:T(8,128)S(1)}, u32[]{:S(2)}, u32[]{:S(2)}) collective-permute-start(f32[2,2,8,4,128]{4,2,3,0,1:T(8,128)S(1)} %pad_maximum_fusion), channel_id=1, source_target_pairs={{0,32},{16,48},{32,64},{48,80},{64,96},{80,112},{96,0},{112,16},{1... | collective-permute-start | bytes 196616 | tf_op jit(solution)/shard_map/ppermute | solution.py:94
  65.0 11.9 %collective-permute-start.5 = (f32[2,8,4,128]{3,1,2,0:T(8,128)S(1)}, f32[2,8,4,128]{3,1,2,0:T(8,128)S(1)}, u32[]{:S(2)}, u32[]{:S(2)}) collective-permute-start(f32[2,8,4,128]{3,1,2,0:T(8,128)S(1)} %get-tuple-element.17), channel_id=1, source_target_pairs={{0,96},{16,112},{32,0},{48,16},{64,32},{80,48},{96,64},{112,80},{1... | collective-permute-start | bytes 98312 | tf_op jit(solution)/shard_map/ppermute | solution.py:95
  68.9 11.0 %collective-permute-start.6 = (f32[2,8,4,128]{3,1,2,0:T(8,128)S(1)}, f32[2,8,4,128]{3,1,2,0:T(8,128)S(1)}, u32[]{:S(2)}, u32[]{:S(2)}) collective-permute-start(f32[2,8,4,128]{3,1,2,0:T(8,128)S(1)} %slice_bitcast_fusion), channel_id=1, source_target_pairs={{0,32},{16,48},{32,64},{48,80},{64,96},{80,112},{96,0},{112,16},{1... | collective-permute-start | bytes 98312 | tf_op jit(solution)/shard_map/ppermute | solution.py:96

commit v4 on v3

--- a/solution.py
+++ b/solution.py
@@ -96,6 +96,16 @@
             relayed = lax.ppermute(ahead[1], "dp", perm=pairs(1))
             x = pick(0) + ahead[0] + behind + relayed
             continue
+        if size == 4:
+            groups = []
+            for d in range(count):
+                if (d // stride) % size == 0:
+                    groups.append([d + k * stride for k in range(size)])
+            sent = lax.all_to_all(
+                x.astype(jnp.bfloat16), "dp", 0, 0, tiled=True, axis_index_groups=groups
+            )
+            x = sent.astype(x.dtype).sum(0)
+            continue
         total = pick(0)
         for shift in range(1, size):
             sent = lax.ppermute(pick(shift).astype(jnp.bfloat16), "dp", perm=pairs(shift))

time: 81.6 us -> 79.2 us (0.971)
  starting transfers between devices: 36.6 us -> 30.9 us
  waiting for transfers between devices: 17.7 us -> 20.6 us
    ppermute x4 -> x1, starting transfers between devices: 12.3 us -> 1.92 us  [staged_reduce_scatter(): lax.ppermute(pick(shift).astype(jnp.bfloat16), 'dp', perm=pairs(shift))]
    all_to_all x0 -> x1, waiting for transfers between devices: none -> 6.96 us  [staged_reduce_scatter(): lax.all_to_all(x.astype(jnp.bfloat16), 'dp', 0, 0, tiled=True, axis_index...]
    all_to_all x0 -> x1, starting transfers between devices: none -> 4.48 us  [staged_reduce_scatter(): lax.all_to_all(x.astype(jnp.bfloat16), 'dp', 0, 0, tiled=True, axis_index...]
    ppermute x4 -> x1, waiting for transfers between devices: 5.76 us -> 1.48 us  [staged_reduce_scatter(): lax.ppermute(pick(shift).astype(jnp.bfloat16), 'dp', perm=pairs(shift))]
  transfers between devices with their start and end apart: 8 -> 6, of which waited for: 6 -> 5; matrix products, arithmetic and copies ran while one was open for 2% -> 2% of each run, Pallas kernels for 0% -> 0%
where the time goes in v4:
time: 79.2 us; the launch traced here: 78.7 us
  starting transfers between devices  30.9 us (39%)
  waiting for transfers between devices  20.6 us (26%)
  blocking collectives  18.1 us (23%)
  matrix products  4.51 us (6%)
  local copies, waits for them, and re-layouts  3.6 us (5%)
  between operations  0.83 us (1%)
    all_to_all x1, blocking collectives, forward_layer(): lax.all_to_all(first_out, 'mp', split_axis=1, concat_axis=0, tiled=True)  18.1 us
    ppermute x1, starting transfers between devices, staged_reduce_scatter(): ahead = lax.ppermute(jnp.stack([pick(1), pick(2)], 0), 'dp', perm=pairs(1))  9.23 us
    all_to_all x1, waiting for transfers between devices, shards(): lax.all_to_all(grad_first, 'mp', split_axis=0, concat_axis=1, tiled=True)  7.99 us
    ppermute x1, starting transfers between devices, staged_reduce_scatter(): relayed = lax.ppermute(ahead[1], 'dp', perm=pairs(1))  7.27 us
    all_to_all x1, waiting for transfers between devices, staged_reduce_scatter(): lax.all_to_all(x.astype(jnp.bfloat16), 'dp', 0, 0, tiled=True, axis_index...  6.96 us
    all_to_all x1, starting transfers between devices, shards(): lax.all_to_all(grad_first, 'mp', split_axis=0, concat_axis=1, tiled=True)  5.13 us
    all_to_all x1, starting transfers between devices, staged_reduce_scatter(): lax.all_to_all(x.astype(jnp.bfloat16), 'dp', 0, 0, tiled=True, axis_index...  4.48 us
    ppermute x1, waiting for transfers between devices, staged_reduce_scatter(): relayed = lax.ppermute(ahead[1], 'dp', perm=pairs(1))  3.7 us
  transfers between devices with their start and end apart: 6, of which 5 were waited for; matrix products, arithmetic and copies ran while one was open for 2% of the time, Pallas kernels for 0%

profile of v4, /device:TPU:2, one launch (start us, length us, event | category | flops | bytes accessed | tf_op | source)
XLA Modules:
  0.0 78.7 jit_solution(410995433468030722)
XLA Ops:
  0.6 0.0 copy-start
  0.6 1.3 %convolution_convert_fusion.2 = bf16[8,128,128]{2,1,0:T(8,128)(2,1)S(1)} fusion(bf16[8,128,128]{2,1,0:T(8,128)(2,1)} %bitcast.90, bf16[1,8,128,128]{3,2,1,0:T(8,128)(2,1)} %param.6), kind=kOutput, calls=%fused_computation.10 | convolution fusion | flops 33685504 | bytes 786432 | tf_op jit(solution)/shard_map/ikt,ikj->ijt/dot_general | solution.py:22
  2.0 0.2 copy.27
  2.2 0.0 copy-start.3
  2.2 18.1 %all_to_all.41 = bf16[8,128,128]{2,0,1:T(8,128)(2,1)S(1)} all-to-all(bf16[8,128,128]{2,0,1:T(8,128)(2,1)S(1)} %copy.27), channel_id=1, replica_groups=mesh['dp'=32,'mp'=16] {'mp'}, dimensions={1} | all-to-all | bytes 524288 | tf_op jit(solution)/shard_map/all_to_all | solution.py:30
  20.3 0.0 copy-done
  20.3 0.0 copy-done.3
  20.3 1.3 %fusion.4 = (bf16[8,128,128]{2,1,0:T(8,128)(2,1)S(1)}, bf16[8,128,128]{2,1,0:T(8,128)(2,1)}) fusion(bf16[8,128,128]{2,1,0:T(8,128)(2,1)S(1)} %bitcast.95, bf16[1,8,128,128]{3,2,1,0:T(8,128)(2,1)S(1)} %copy-done, bf16[8,16,8,128]{3,0,2,1:T(8,128)(2,1)S(1)} %bitcast.92), kind=kOutput, calls=%fused_computation.18 | convolution fusion | flops 36569088 | bytes 1310720 | tf_op jit(solution)/shard_map/ijt,jim->jmt/dot_general | solution.py:14
  21.7 0.3 fusion.1
  22.0 0.9 %copy.31 = bf16[128,8,128]{2,1,0:T(8,128)(2,1)} copy(bf16[128,8,128]{0,2,1:T(8,128)(2,1)S(1)} %fusion.1) | data formatting | bytes 524288 | tf_op jit(solution)/shard_map/convert_element_type | solution.py:146
  22.9 5.1 %all-to-all-start.1 = ((bf16[128,8,128]{2,1,0:T(8,128)(2,1)}), bf16[128,8,128]{2,1,0:T(8,128)(2,1)S(1)}, u32[]{:S(2)}, u32[]{:S(2)}) async-start(bf16[128,8,128]{2,1,0:T(8,128)(2,1)} %copy.31), calls=%async_computation.1 | async-start | bytes 524288 | tf_op jit(solution)/shard_map/all_to_all | solution.py:153
  28.0 0.3 convolution_multiply_fusion.1
  28.3 0.0 copy-start.2
  28.3 0.3 copy.35
  28.6 8.0 %all-to-all-done.1 = bf16[128,8,128]{2,1,0:T(8,128)(2,1)S(1)} async-done(((bf16[128,8,128]{2,1,0:T(8,128)(2,1)}), bf16[128,8,128]{2,1,0:T(8,128)(2,1)S(1)}, u32[]{:S(2)}, u32[]{:S(2)}) %all-to-all-start.1) | async-done | bytes 262176 | tf_op jit(solution)/shard_map/all_to_all | solution.py:153
  36.6 0.0 copy-done.2
  36.6 0.3 fusion
  36.9 0.2 copy.34
  37.2 1.9 %collective-permute-start = (bf16[4,4,2,8,4,128]{5,3,4,1,0,2:T(8,128)(2,1)S(1)}, bf16[4,4,2,8,4,128]{5,3,4,1,0,2:T(8,128)(2,1)S(1)}, u32[]{:S(2)}, u32[]{:S(2)}) collective-permute-start(bf16[4,4,2,8,4,128]{5,3,4,1,0,2:T(8,128)(2,1)S(1)} %fusion.18), channel_id=1, source_target_pairs={{0,16},{16,0},{32,48},{48,32},{64,80},{80,64},{96,112},{112,96},{1... | collective-permute-start | bytes 786440 | tf_op jit(solution)/shard_map/ppermute | solution.py:111
  39.2 1.5 %collective-permute-done = bf16[4,4,2,8,4,128]{5,3,4,1,0,2:T(8,128)(2,1)S(1)} collective-permute-done((bf16[4,4,2,8,4,128]{5,3,4,1,0,2:T(8,128)(2,1)S(1)}, bf16[4,4,2,8,4,128]{5,3,4,1,0,2:T(8,128)(2,1)S(1)}, u32[]{:S(2)}, u32[]{:S(2)}) %collective-permute-start) | collective-permute-done | bytes 262176 | tf_op jit(solution)/shard_map/ppermute | solution.py:111
  40.7 0.1 fusion.17
  40.7 0.7 copy.37
  41.5 4.5 %all-to-all-start.2 = ((bf16[4,4,2,8,4,128]{5,3,4,1,2,0:T(8,128)(2,1)}), bf16[4,4,2,8,4,128]{5,3,4,1,2,0:T(8,128)(2,1)S(1)}, u32[]{:S(2)}, u32[]{:S(2)}) async-start(bf16[4,4,2,8,4,128]{5,3,4,1,2,0:T(8,128)(2,1)} %copy.37), calls=%async_computation.2 | async-start | bytes 524288 | tf_op jit(solution)/shard_map/all_to_all | solution.py:104
  45.9 7.0 %all-to-all-done.2 = bf16[4,4,2,8,4,128]{5,3,4,1,2,0:T(8,128)(2,1)S(1)} async-done(((bf16[4,4,2,8,4,128]{5,3,4,1,2,0:T(8,128)(2,1)}), bf16[4,4,2,8,4,128]{5,3,4,1,2,0:T(8,128)(2,1)S(1)}, u32[]{:S(2)}, u32[]{:S(2)}) %all-to-all-start.2) | async-done | bytes 262176 | tf_op jit(solution)/shard_map/all_to_all | solution.py:104
  52.9 0.0 copy-start.1
  53.0 9.2 %collective-permute-start.1 = (f32[2,2,8,4,128]{4,2,3,0,1:T(8,128)S(1)}, f32[2,2,8,4,128]{4,2,3,0,1:T(8,128)S(1)}, u32[]{:S(2)}, u32[]{:S(2)}) collective-permute-start(f32[2,2,8,4,128]{4,2,3,0,1:T(8,128)S(1)} %pad_maximum_fusion), channel_id=1, source_target_pairs={{0,32},{16,48},{32,64},{48,80},{64,96},{80,112},{96,0},{112,16},{1... | collective-permute-start | bytes 196616 | tf_op jit(solution)/shard_map/ppermute | solution.py:94
  62.2 2.9 %collective-permute-start.2 = (f32[2,8,4,128]{3,1,2,0:T(8,128)S(1)}, f32[2,8,4,128]{3,1,2,0:T(8,128)S(1)}, u32[]{:S(2)}, u32[]{:S(2)}) collective-permute-start(f32[2,8,4,128]{3,1,2,0:T(8,128)S(1)} %get-tuple-element.10), channel_id=1, source_target_pairs={{0,96},{16,112},{32,0},{48,16},{64,32},{80,48},{96,64},{112,80},{1... | collective-permute-start | bytes 98312 | tf_op jit(solution)/shard_map/ppermute | solution.py:95
  65.1 0.4 collective-permute-done.1
  65.5 7.3 %collective-permute-start.3 = (f32[2,8,4,128]{3,1,2,0:T(8,128)S(1)}, f32[2,8,4,128]{3,1,2,0:T(8,128)S(1)}, u32[]{:S(2)}, u32[]{:S(2)}) collective-permute-start(f32[2,8,4,128]{3,1,2,0:T(8,128)S(1)} %slice_bitcast_fusion), channel_id=1, source_target_pairs={{0,32},{16,48},{32,64},{48,80},{64,96},{80,112},{96,0},{112,16},{1... | collective-permute-start | bytes 98312 | tf_op jit(solution)/shard_map/ppermute | solution.py:96
  72.8 0.0 copy-done.1
  72.8 0.9 %convolution_convert_fusion = bf16[8,128,128]{1,2,0:T(8,128)(2,1)} fusion(bf16[1,8,128,128]{3,2,1,0:T(8,128)(2,1)S(1)} %copy-done.1, bf16[8,16,8,128]{3,2,0,1:T(8,128)(2,1)S(1)} %bitcast.88), kind=kOutput, calls=%fused_computation.8 | convolution fusion | flops 33685504 | bytes 786432 | tf_op jit(solution)/shard_map/ijt,ikj->ikt/dot_general | solution.py:149
  73.8 0.0 collective-permute-done.2
  73.8 3.7 %collective-permute-done.3 = f32[2,8,4,128]{3,1,2,0:T(8,128)S(1)} collective-permute-done((f32[2,8,4,128]{3,1,2,0:T(8,128)S(1)}, f32[2,8,4,128]{3,1,2,0:T(8,128)S(1)}, u32[]{:S(2)}, u32[]{:S(2)}) %collective-permute-start.3) | collective-permute-done | bytes 32800 | tf_op jit(solution)/shard_map/ppermute | solution.py:96
  77.5 0.6 copy.42
  78.1 0.6 copy.41
  (7 shorter events, 0.1 us)
Async XLA Ops:
  0.6 19.7 %copy-start = (bf16[1,8,128,128]{3,2,1,0:T(8,128)(2,1)S(1)}, bf16[1,8,128,128]{3,2,1,0:T(8,128)(2,1)}, u32[]{:S(2)}) copy-start(bf16[1,8,128,128]{3,2,1,0:T(8,128)(2,1)} %param.7) | copy-start | bytes 786436
  2.2 18.2 %copy-start.3 = (bf16[1024,128]{1,0:T(8,128)(2,1)S(1)}, bf16[1024,128]{1,0:T(8,128)(2,1)}, u32[]{:S(2)}) copy-start(bf16[1024,128]{1,0:T(8,128)(2,1)} %param.5) | copy-start | bytes 786436
  22.9 13.7 %all-to-all-start.1 = ((bf16[128,8,128]{2,1,0:T(8,128)(2,1)}), bf16[128,8,128]{2,1,0:T(8,128)(2,1)S(1)}, u32[]{:S(2)}, u32[]{:S(2)}) async-start(bf16[128,8,128]{2,1,0:T(8,128)(2,1)} %copy.31), calls=%async_computation.1 | async-start | bytes 524288 | tf_op jit(solution)/shard_map/all_to_all | solution.py:153
  28.3 8.3 %copy-start.2 = (bf16[1024,128]{1,0:T(8,128)(2,1)S(1)}, bf16[1024,128]{1,0:T(8,128)(2,1)}, u32[]{:S(2)}) copy-start(bf16[1024,128]{1,0:T(8,128)(2,1)} %param.4) | copy-start | bytes 786436
  37.2 3.4 %collective-permute-start = (bf16[4,4,2,8,4,128]{5,3,4,1,0,2:T(8,128)(2,1)S(1)}, bf16[4,4,2,8,4,128]{5,3,4,1,0,2:T(8,128)(2,1)S(1)}, u32[]{:S(2)}, u32[]{:S(2)}) collective-permute-start(bf16[4,4,2,8,4,128]{5,3,4,1,0,2:T(8,128)(2,1)S(1)} %fusion.18), channel_id=1, source_target_pairs={{0,16},{16,0},{32,48},{48,32},{64,80},{80,64},{96,112},{112,96},{1... | collective-permute-start | bytes 786440 | tf_op jit(solution)/shard_map/ppermute | solution.py:111
  41.5 11.4 %all-to-all-start.2 = ((bf16[4,4,2,8,4,128]{5,3,4,1,2,0:T(8,128)(2,1)}), bf16[4,4,2,8,4,128]{5,3,4,1,2,0:T(8,128)(2,1)S(1)}, u32[]{:S(2)}, u32[]{:S(2)}) async-start(bf16[4,4,2,8,4,128]{5,3,4,1,2,0:T(8,128)(2,1)} %copy.37), calls=%async_computation.2 | async-start | bytes 524288 | tf_op jit(solution)/shard_map/all_to_all | solution.py:104
  52.9 19.9 %copy-start.1 = (bf16[1,8,128,128]{3,2,1,0:T(8,128)(2,1)S(1)}, bf16[1,8,128,128]{3,2,1,0:T(8,128)(2,1)}, u32[]{:S(2)}) copy-start(bf16[1,8,128,128]{3,2,1,0:T(8,128)(2,1)} %param.6) | copy-start | bytes 786436
  53.0 12.6 %collective-permute-start.1 = (f32[2,2,8,4,128]{4,2,3,0,1:T(8,128)S(1)}, f32[2,2,8,4,128]{4,2,3,0,1:T(8,128)S(1)}, u32[]{:S(2)}, u32[]{:S(2)}) collective-permute-start(f32[2,2,8,4,128]{4,2,3,0,1:T(8,128)S(1)} %pad_maximum_fusion), channel_id=1, source_target_pairs={{0,32},{16,48},{32,64},{48,80},{64,96},{80,112},{96,0},{112,16},{1... | collective-permute-start | bytes 196616 | tf_op jit(solution)/shard_map/ppermute | solution.py:94
  62.2 11.5 %collective-permute-start.2 = (f32[2,8,4,128]{3,1,2,0:T(8,128)S(1)}, f32[2,8,4,128]{3,1,2,0:T(8,128)S(1)}, u32[]{:S(2)}, u32[]{:S(2)}) collective-permute-start(f32[2,8,4,128]{3,1,2,0:T(8,128)S(1)} %get-tuple-element.10), channel_id=1, source_target_pairs={{0,96},{16,112},{32,0},{48,16},{64,32},{80,48},{96,64},{112,80},{1... | collective-permute-start | bytes 98312 | tf_op jit(solution)/shard_map/ppermute | solution.py:95
  65.5 11.9 %collective-permute-start.3 = (f32[2,8,4,128]{3,1,2,0:T(8,128)S(1)}, f32[2,8,4,128]{3,1,2,0:T(8,128)S(1)}, u32[]{:S(2)}, u32[]{:S(2)}) collective-permute-start(f32[2,8,4,128]{3,1,2,0:T(8,128)S(1)} %slice_bitcast_fusion), channel_id=1, source_target_pairs={{0,32},{16,48},{32,64},{48,80},{64,96},{80,112},{96,0},{112,16},{1... | collective-permute-start | bytes 98312 | tf_op jit(solution)/shard_map/ppermute | solution.py:96

commit v5 on v4

--- a/solution.py
+++ b/solution.py
@@ -91,10 +91,12 @@
             return out
 
         if size == 4 and distance > 1:
-            ahead = lax.ppermute(jnp.stack([pick(1), pick(2)], 0), "dp", perm=pairs(1))
-            behind = lax.ppermute(pick(-1), "dp", perm=pairs(-1))
+            wide = x.dtype
+            ahead = jnp.stack([pick(1), pick(2)], 0).astype(jnp.bfloat16)
+            ahead = lax.ppermute(ahead, "dp", perm=pairs(1))
+            behind = lax.ppermute(pick(-1).astype(jnp.bfloat16), "dp", perm=pairs(-1))
             relayed = lax.ppermute(ahead[1], "dp", perm=pairs(1))
-            x = pick(0) + ahead[0] + behind + relayed
+            x = pick(0) + ahead[0].astype(wide) + behind.astype(wide) + relayed.astype(wide)
             continue
         if size == 4:
             groups = []

time: 79.2 us -> 76.6 us (0.967)
  waiting for transfers between devices: 20.6 us -> 18.5 us
    ppermute x1, waiting for transfers between devices: 3.7 us -> 2.04 us  [staged_reduce_scatter(): relayed = lax.ppermute(ahead[1], 'dp', perm=pairs(1))]
  transfers between devices with their start and end apart: 6 -> 6, of which waited for: 5 -> 4; matrix products, arithmetic and copies ran while one was open for 2% -> 2% of each run, Pallas kernels for 0% -> 0%
where the time goes in v5:
time: 76.6 us; the launch traced here: 76.1 us
  starting transfers between devices  30.4 us (40%)
  waiting for transfers between devices  18.5 us (24%)
  blocking collectives  18.1 us (24%)
  matrix products  4.51 us (6%)
  local copies, waits for them, and re-layouts  3.6 us (5%)
  between operations  0.84 us (1%)
    all_to_all x1, blocking collectives, forward_layer(): lax.all_to_all(first_out, 'mp', split_axis=1, concat_axis=0, tiled=True)  18.1 us
    ppermute x1, starting transfers between devices, staged_reduce_scatter(): ahead = lax.ppermute(ahead, 'dp', perm=pairs(1))  9.1 us
    all_to_all x1, waiting for transfers between devices, shards(): lax.all_to_all(grad_first, 'mp', split_axis=0, concat_axis=1, tiled=True)  7.99 us
    all_to_all x1, waiting for transfers between devices, staged_reduce_scatter(): lax.all_to_all(x.astype(jnp.bfloat16), 'dp', 0, 0, tiled=True, axis_index...  6.96 us
    ppermute x1, starting transfers between devices, staged_reduce_scatter(): relayed = lax.ppermute(ahead[1], 'dp', perm=pairs(1))  6.9 us
    all_to_all x1, starting transfers between devices, shards(): lax.all_to_all(grad_first, 'mp', split_axis=0, concat_axis=1, tiled=True)  5.13 us
    all_to_all x1, starting transfers between devices, staged_reduce_scatter(): lax.all_to_all(x.astype(jnp.bfloat16), 'dp', 0, 0, tiled=True, axis_index...  4.48 us
    ppermute x1, starting transfers between devices, staged_reduce_scatter(): behind = lax.ppermute(pick(-1).astype(jnp.bfloat16), 'dp', perm=pairs(-1))  2.85 us
  transfers between devices with their start and end apart: 6, of which 4 were waited for; matrix products, arithmetic and copies ran while one was open for 2% of the time, Pallas kernels for 0%

profile of v5, /device:TPU:2, one launch (start us, length us, event | category | flops | bytes accessed | tf_op | source)
XLA Modules:
  0.0 76.1 jit_solution(2309071659900590406)
XLA Ops:
  0.6 0.0 copy-start
  0.6 1.3 %convolution_convert_fusion.2 = bf16[8,128,128]{2,1,0:T(8,128)(2,1)S(1)} fusion(bf16[8,128,128]{2,1,0:T(8,128)(2,1)} %bitcast.90, bf16[1,8,128,128]{3,2,1,0:T(8,128)(2,1)} %param.6), kind=kOutput, calls=%fused_computation.10 | convolution fusion | flops 33685504 | bytes 786432 | tf_op jit(solution)/shard_map/ikt,ikj->ijt/dot_general | solution.py:22
  2.0 0.2 copy.27
  2.2 0.0 copy-start.3
  2.2 18.1 %all_to_all.41 = bf16[8,128,128]{2,0,1:T(8,128)(2,1)S(1)} all-to-all(bf16[8,128,128]{2,0,1:T(8,128)(2,1)S(1)} %copy.27), channel_id=1, replica_groups=mesh['dp'=32,'mp'=16] {'mp'}, dimensions={1} | all-to-all | bytes 524288 | tf_op jit(solution)/shard_map/all_to_all | solution.py:30
  20.3 0.0 copy-done
  20.3 0.0 copy-done.3
  20.3 1.3 %fusion.4 = (bf16[8,128,128]{2,1,0:T(8,128)(2,1)S(1)}, bf16[8,128,128]{2,1,0:T(8,128)(2,1)}) fusion(bf16[8,128,128]{2,1,0:T(8,128)(2,1)S(1)} %bitcast.95, bf16[1,8,128,128]{3,2,1,0:T(8,128)(2,1)S(1)} %copy-done, bf16[8,16,8,128]{3,0,2,1:T(8,128)(2,1)S(1)} %bitcast.92), kind=kOutput, calls=%fused_computation.18 | convolution fusion | flops 36569088 | bytes 1310720 | tf_op jit(solution)/shard_map/ijt,jim->jmt/dot_general | solution.py:14
  21.7 0.3 fusion.1
  22.0 0.9 %copy.31 = bf16[128,8,128]{2,1,0:T(8,128)(2,1)} copy(bf16[128,8,128]{0,2,1:T(8,128)(2,1)S(1)} %fusion.1) | data formatting | bytes 524288 | tf_op jit(solution)/shard_map/convert_element_type | solution.py:148
  22.9 5.1 %all-to-all-start.1 = ((bf16[128,8,128]{2,1,0:T(8,128)(2,1)}), bf16[128,8,128]{2,1,0:T(8,128)(2,1)S(1)}, u32[]{:S(2)}, u32[]{:S(2)}) async-start(bf16[128,8,128]{2,1,0:T(8,128)(2,1)} %copy.31), calls=%async_computation.1 | async-start | bytes 524288 | tf_op jit(solution)/shard_map/all_to_all | solution.py:155
  28.0 0.3 convolution_multiply_fusion.1
  28.3 0.0 copy-start.2
  28.3 0.3 copy.35
  28.6 8.0 %all-to-all-done.1 = bf16[128,8,128]{2,1,0:T(8,128)(2,1)S(1)} async-done(((bf16[128,8,128]{2,1,0:T(8,128)(2,1)}), bf16[128,8,128]{2,1,0:T(8,128)(2,1)S(1)}, u32[]{:S(2)}, u32[]{:S(2)}) %all-to-all-start.1) | async-done | bytes 262176 | tf_op jit(solution)/shard_map/all_to_all | solution.py:155
  36.6 0.0 copy-done.2
  36.6 0.3 fusion
  36.9 0.2 copy.34
  37.2 1.9 %collective-permute-start = (bf16[4,4,2,8,4,128]{5,3,4,1,0,2:T(8,128)(2,1)S(1)}, bf16[4,4,2,8,4,128]{5,3,4,1,0,2:T(8,128)(2,1)S(1)}, u32[]{:S(2)}, u32[]{:S(2)}) collective-permute-start(bf16[4,4,2,8,4,128]{5,3,4,1,0,2:T(8,128)(2,1)S(1)} %fusion.18), channel_id=1, source_target_pairs={{0,16},{16,0},{32,48},{48,32},{64,80},{80,64},{96,112},{112,96},{1... | collective-permute-start | bytes 786440 | tf_op jit(solution)/shard_map/ppermute | solution.py:113
  39.2 1.5 %collective-permute-done = bf16[4,4,2,8,4,128]{5,3,4,1,0,2:T(8,128)(2,1)S(1)} collective-permute-done((bf16[4,4,2,8,4,128]{5,3,4,1,0,2:T(8,128)(2,1)S(1)}, bf16[4,4,2,8,4,128]{5,3,4,1,0,2:T(8,128)(2,1)S(1)}, u32[]{:S(2)}, u32[]{:S(2)}) %collective-permute-start) | collective-permute-done | bytes 262176 | tf_op jit(solution)/shard_map/ppermute | solution.py:113
  40.7 0.1 fusion.17
  40.7 0.7 copy.37
  41.5 4.5 %all-to-all-start.2 = ((bf16[4,4,2,8,4,128]{5,3,4,1,2,0:T(8,128)(2,1)}), bf16[4,4,2,8,4,128]{5,3,4,1,2,0:T(8,128)(2,1)S(1)}, u32[]{:S(2)}, u32[]{:S(2)}) async-start(bf16[4,4,2,8,4,128]{5,3,4,1,2,0:T(8,128)(2,1)} %copy.37), calls=%async_computation.2 | async-start | bytes 524288 | tf_op jit(solution)/shard_map/all_to_all | solution.py:106
  45.9 0.0 copy-start.1
  45.9 7.0 %all-to-all-done.2 = bf16[4,4,2,8,4,128]{5,3,4,1,2,0:T(8,128)(2,1)S(1)} async-done(((bf16[4,4,2,8,4,128]{5,3,4,1,2,0:T(8,128)(2,1)}), bf16[4,4,2,8,4,128]{5,3,4,1,2,0:T(8,128)(2,1)S(1)}, u32[]{:S(2)}, u32[]{:S(2)}) %all-to-all-start.2) | async-done | bytes 262176 | tf_op jit(solution)/shard_map/all_to_all | solution.py:106
  53.0 9.1 %collective-permute-start.1 = (bf16[2,2,8,4,128]{4,2,3,1,0:T(8,128)(2,1)S(1)}, bf16[2,2,8,4,128]{4,2,3,1,0:T(8,128)(2,1)S(1)}, u32[]{:S(2)}, u32[]{:S(2)}) collective-permute-start(bf16[2,2,8,4,128]{4,2,3,1,0:T(8,128)(2,1)S(1)} %pad_maximum_fusion), channel_id=1, source_target_pairs={{0,32},{16,48},{32,64},{48,80},{64,96},{80,112},{96,0},{112,16},{1... | collective-permute-start | bytes 98312 | tf_op jit(solution)/shard_map/ppermute | solution.py:96
  62.1 2.9 %collective-permute-start.2 = (bf16[2,8,4,128]{3,1,2,0:T(8,128)(2,1)S(1)}, bf16[2,8,4,128]{3,1,2,0:T(8,128)(2,1)S(1)}, u32[]{:S(2)}, u32[]{:S(2)}) collective-permute-start(bf16[2,8,4,128]{3,1,2,0:T(8,128)(2,1)S(1)} %get-tuple-element.10), channel_id=1, source_target_pairs={{0,96},{16,112},{32,0},{48,16},{64,32},{80,48},{96,64},{112,80},{1... | collective-permute-start | bytes 49160 | tf_op jit(solution)/shard_map/ppermute | solution.py:97
  65.0 0.0 collective-permute-done.1
  65.0 6.9 %collective-permute-start.3 = (bf16[2,8,4,128]{3,1,2,0:T(8,128)(2,1)S(1)}, bf16[2,8,4,128]{3,1,2,0:T(8,128)(2,1)S(1)}, u32[]{:S(2)}, u32[]{:S(2)}) collective-permute-start(bf16[2,8,4,128]{3,1,2,0:T(8,128)(2,1)S(1)} %slice_bitcast_fusion), channel_id=1, source_target_pairs={{0,32},{16,48},{32,64},{48,80},{64,96},{80,112},{96,0},{112,16},{1... | collective-permute-start | bytes 49160 | tf_op jit(solution)/shard_map/ppermute | solution.py:98
  71.9 0.0 copy-done.1
  71.9 0.9 %convolution_convert_fusion = bf16[8,128,128]{1,2,0:T(8,128)(2,1)} fusion(bf16[1,8,128,128]{3,2,1,0:T(8,128)(2,1)S(1)} %copy-done.1, bf16[8,16,8,128]{3,2,0,1:T(8,128)(2,1)S(1)} %bitcast.88), kind=kOutput, calls=%fused_computation.8 | convolution fusion | flops 33685504 | bytes 786432 | tf_op jit(solution)/shard_map/ijt,ikj->ikt/dot_general | solution.py:151
  72.8 0.0 collective-permute-done.2
  72.8 2.0 %collective-permute-done.3 = bf16[2,8,4,128]{3,1,2,0:T(8,128)(2,1)S(1)} collective-permute-done((bf16[2,8,4,128]{3,1,2,0:T(8,128)(2,1)S(1)}, bf16[2,8,4,128]{3,1,2,0:T(8,128)(2,1)S(1)}, u32[]{:S(2)}, u32[]{:S(2)}) %collective-permute-start.3) | collective-permute-done | bytes 16416 | tf_op jit(solution)/shard_map/ppermute | solution.py:98
  74.9 0.6 copy.43
  75.5 0.6 copy.42
  (7 shorter events, 0.1 us)
Async XLA Ops:
  0.6 19.7 %copy-start = (bf16[1,8,128,128]{3,2,1,0:T(8,128)(2,1)S(1)}, bf16[1,8,128,128]{3,2,1,0:T(8,128)(2,1)}, u32[]{:S(2)}) copy-start(bf16[1,8,128,128]{3,2,1,0:T(8,128)(2,1)} %param.7) | copy-start | bytes 786436
  2.2 18.2 %copy-start.3 = (bf16[1024,128]{1,0:T(8,128)(2,1)S(1)}, bf16[1024,128]{1,0:T(8,128)(2,1)}, u32[]{:S(2)}) copy-start(bf16[1024,128]{1,0:T(8,128)(2,1)} %param.5) | copy-start | bytes 786436
  22.9 13.7 %all-to-all-start.1 = ((bf16[128,8,128]{2,1,0:T(8,128)(2,1)}), bf16[128,8,128]{2,1,0:T(8,128)(2,1)S(1)}, u32[]{:S(2)}, u32[]{:S(2)}) async-start(bf16[128,8,128]{2,1,0:T(8,128)(2,1)} %copy.31), calls=%async_computation.1 | async-start | bytes 524288 | tf_op jit(solution)/shard_map/all_to_all | solution.py:155
  28.3 8.3 %copy-start.2 = (bf16[1024,128]{1,0:T(8,128)(2,1)S(1)}, bf16[1024,128]{1,0:T(8,128)(2,1)}, u32[]{:S(2)}) copy-start(bf16[1024,128]{1,0:T(8,128)(2,1)} %param.4) | copy-start | bytes 786436
  37.2 3.4 %collective-permute-start = (bf16[4,4,2,8,4,128]{5,3,4,1,0,2:T(8,128)(2,1)S(1)}, bf16[4,4,2,8,4,128]{5,3,4,1,0,2:T(8,128)(2,1)S(1)}, u32[]{:S(2)}, u32[]{:S(2)}) collective-permute-start(bf16[4,4,2,8,4,128]{5,3,4,1,0,2:T(8,128)(2,1)S(1)} %fusion.18), channel_id=1, source_target_pairs={{0,16},{16,0},{32,48},{48,32},{64,80},{80,64},{96,112},{112,96},{1... | collective-permute-start | bytes 786440 | tf_op jit(solution)/shard_map/ppermute | solution.py:113
  41.5 11.4 %all-to-all-start.2 = ((bf16[4,4,2,8,4,128]{5,3,4,1,2,0:T(8,128)(2,1)}), bf16[4,4,2,8,4,128]{5,3,4,1,2,0:T(8,128)(2,1)S(1)}, u32[]{:S(2)}, u32[]{:S(2)}) async-start(bf16[4,4,2,8,4,128]{5,3,4,1,2,0:T(8,128)(2,1)} %copy.37), calls=%async_computation.2 | async-start | bytes 524288 | tf_op jit(solution)/shard_map/all_to_all | solution.py:106
  45.9 26.0 %copy-start.1 = (bf16[1,8,128,128]{3,2,1,0:T(8,128)(2,1)S(1)}, bf16[1,8,128,128]{3,2,1,0:T(8,128)(2,1)}, u32[]{:S(2)}) copy-start(bf16[1,8,128,128]{3,2,1,0:T(8,128)(2,1)} %param.6) | copy-start | bytes 786436
  53.0 12.0 %collective-permute-start.1 = (bf16[2,2,8,4,128]{4,2,3,1,0:T(8,128)(2,1)S(1)}, bf16[2,2,8,4,128]{4,2,3,1,0:T(8,128)(2,1)S(1)}, u32[]{:S(2)}, u32[]{:S(2)}) collective-permute-start(bf16[2,2,8,4,128]{4,2,3,1,0:T(8,128)(2,1)S(1)} %pad_maximum_fusion), channel_id=1, source_target_pairs={{0,32},{16,48},{32,64},{48,80},{64,96},{80,112},{96,0},{112,16},{1... | collective-permute-start | bytes 98312 | tf_op jit(solution)/shard_map/ppermute | solution.py:96
  62.1 10.7 %collective-permute-start.2 = (bf16[2,8,4,128]{3,1,2,0:T(8,128)(2,1)S(1)}, bf16[2,8,4,128]{3,1,2,0:T(8,128)(2,1)S(1)}, u32[]{:S(2)}, u32[]{:S(2)}) collective-permute-start(bf16[2,8,4,128]{3,1,2,0:T(8,128)(2,1)S(1)} %get-tuple-element.10), channel_id=1, source_target_pairs={{0,96},{16,112},{32,0},{48,16},{64,32},{80,48},{96,64},{112,80},{1... | collective-permute-start | bytes 49160 | tf_op jit(solution)/shard_map/ppermute | solution.py:97
  65.0 9.9 %collective-permute-start.3 = (bf16[2,8,4,128]{3,1,2,0:T(8,128)(2,1)S(1)}, bf16[2,8,4,128]{3,1,2,0:T(8,128)(2,1)S(1)}, u32[]{:S(2)}, u32[]{:S(2)}) collective-permute-start(bf16[2,8,4,128]{3,1,2,0:T(8,128)(2,1)S(1)} %slice_bitcast_fusion), channel_id=1, source_target_pairs={{0,32},{16,48},{32,64},{48,80},{64,96},{80,112},{96,0},{112,16},{1... | collective-permute-start | bytes 49160 | tf_op jit(solution)/shard_map/ppermute | solution.py:98

commit v6 on v5

--- a/solution.py
+++ b/solution.py
@@ -76,6 +76,10 @@
     nlead = len(lead)
     perm = [nlead + by_stride.index(s) for s in order]
     x = x.transpose(perm + list(range(nlead)) + list(range(nlead + len(stages), x.ndim)))
+    inner = 1
+    for extent in lead[1:]:
+        inner *= extent
+    x = x.reshape(x.shape[: len(stages)] + lead[:1] + (inner * piece, cols))
     me = lax.axis_index("dp")
     for distance, size, stride in order:
         mine = (me // stride) % size
@@ -113,7 +117,7 @@
             sent = lax.ppermute(pick(shift).astype(jnp.bfloat16), "dp", perm=pairs(shift))
             total = total + sent.astype(total.dtype)
         x = total
-    return x
+    return x.reshape(lead + (piece, cols))
 
 
 def shards(stages, inputs, cotangent, r_factor, l_factor):

time: 76.6 us -> 76.4 us (level)
  local copies, waits for them, and re-layouts: 3.6 us -> 2.63 us
  other arithmetic: 0.16 us -> 0.93 us
    unnamed x10 -> x8, local copies, waits for them, and re-layouts: 1.24 us -> 0.02 us
where the time goes in v6:
time: 76.4 us; the launch traced here: 75.9 us
  starting transfers between devices  30.4 us (40%)
  waiting for transfers between devices  18.5 us (24%)
  blocking collectives  18.1 us (24%)
  matrix products  4.51 us (6%)
  local copies, waits for them, and re-layouts  2.63 us (3%)
  other arithmetic  0.93 us (1%)
  between operations  0.84 us (1%)
    all_to_all x1, blocking collectives, forward_layer(): lax.all_to_all(first_out, 'mp', split_axis=1, concat_axis=0, tiled=True)  18.1 us
    ppermute x1, starting transfers between devices, staged_reduce_scatter(): ahead = lax.ppermute(ahead, 'dp', perm=pairs(1))  9.1 us
    all_to_all x1, waiting for transfers between devices, shards(): lax.all_to_all(grad_first, 'mp', split_axis=0, concat_axis=1, tiled=True)  7.99 us
    all_to_all x1, waiting for transfers between devices, staged_reduce_scatter(): lax.all_to_all(x.astype(jnp.bfloat16), 'dp', 0, 0, tiled=True, axis_index...  6.97 us
    ppermute x1, starting transfers between devices, staged_reduce_scatter(): relayed = lax.ppermute(ahead[1], 'dp', perm=pairs(1))  6.9 us
    all_to_all x1, starting transfers between devices, shards(): lax.all_to_all(grad_first, 'mp', split_axis=0, concat_axis=1, tiled=True)  5.13 us
    all_to_all x1, starting transfers between devices, staged_reduce_scatter(): lax.all_to_all(x.astype(jnp.bfloat16), 'dp', 0, 0, tiled=True, axis_index...  4.48 us
    ppermute x1, starting transfers between devices, staged_reduce_scatter(): behind = lax.ppermute(pick(-1).astype(jnp.bfloat16), 'dp', perm=pairs(-1))  2.85 us
  transfers between devices with their start and end apart: 6, of which 4 were waited for; matrix products, arithmetic and copies ran while one was open for 2% of the time, Pallas kernels for 0%

profile of v6, /device:TPU:2, one launch (start us, length us, event | category | flops | bytes accessed | tf_op | source)
XLA Modules:
  0.0 75.9 jit_solution(2336797891508681014)
XLA Ops:
  0.6 0.0 copy-start
  0.6 1.3 %convolution_convert_fusion.2 = bf16[8,128,128]{2,1,0:T(8,128)(2,1)S(1)} fusion(bf16[8,128,128]{2,1,0:T(8,128)(2,1)} %bitcast.74, bf16[1,8,128,128]{3,2,1,0:T(8,128)(2,1)} %param.6), kind=kOutput, calls=%fused_computation.6 | convolution fusion | flops 33685504 | bytes 786432 | tf_op jit(solution)/shard_map/ikt,ikj->ijt/dot_general | solution.py:22
  2.0 0.2 copy.26
  2.2 0.0 copy-start.3
  2.2 18.1 %all_to_all.41 = bf16[8,128,128]{2,0,1:T(8,128)(2,1)S(1)} all-to-all(bf16[8,128,128]{2,0,1:T(8,128)(2,1)S(1)} %copy.26), channel_id=1, replica_groups=mesh['dp'=32,'mp'=16] {'mp'}, dimensions={1} | all-to-all | bytes 524288 | tf_op jit(solution)/shard_map/all_to_all | solution.py:30
  20.3 0.0 copy-done
  20.3 0.0 copy-done.3
  20.3 1.3 %fusion.4 = (bf16[8,128,128]{2,1,0:T(8,128)(2,1)S(1)}, bf16[8,128,128]{2,1,0:T(8,128)(2,1)}) fusion(bf16[8,128,128]{2,1,0:T(8,128)(2,1)S(1)} %bitcast.81, bf16[1,8,128,128]{3,2,1,0:T(8,128)(2,1)S(1)} %copy-done, bf16[8,16,8,128]{3,0,2,1:T(8,128)(2,1)S(1)} %bitcast.76), kind=kOutput, calls=%fused_computation.15 | convolution fusion | flops 36569088 | bytes 1310720 | tf_op jit(solution)/shard_map/ijt,jim->jmt/dot_general | solution.py:14
  21.7 0.3 fusion.1
  22.0 0.9 %copy.30 = bf16[128,8,128]{2,1,0:T(8,128)(2,1)} copy(bf16[128,8,128]{0,2,1:T(8,128)(2,1)S(1)} %fusion.1) | data formatting | bytes 524288 | tf_op jit(solution)/shard_map/convert_element_type | solution.py:152
  22.9 5.1 %all-to-all-start.1 = ((bf16[128,8,128]{2,1,0:T(8,128)(2,1)}), bf16[128,8,128]{2,1,0:T(8,128)(2,1)S(1)}, u32[]{:S(2)}, u32[]{:S(2)}) async-start(bf16[128,8,128]{2,1,0:T(8,128)(2,1)} %copy.30), calls=%async_computation.1 | async-start | bytes 524288 | tf_op jit(solution)/shard_map/all_to_all | solution.py:159
  28.0 0.3 convolution_multiply_fusion.1
  28.3 0.0 copy-start.2
  28.3 0.3 copy.34
  28.6 8.0 %all-to-all-done.1 = bf16[128,8,128]{2,1,0:T(8,128)(2,1)S(1)} async-done(((bf16[128,8,128]{2,1,0:T(8,128)(2,1)}), bf16[128,8,128]{2,1,0:T(8,128)(2,1)S(1)}, u32[]{:S(2)}, u32[]{:S(2)}) %all-to-all-start.1) | async-done | bytes 262176 | tf_op jit(solution)/shard_map/all_to_all | solution.py:159
  36.6 0.0 copy-done.2
  36.6 0.3 fusion
  36.9 0.2 copy.33
  37.2 0.1 maximum_bitcast_fusion
  37.3 0.3 copy.35
  37.7 1.9 %collective-permute-start = (bf16[4,4,2,32,128]{4,3,2,1,0:T(8,128)(2,1)S(1)}, bf16[4,4,2,32,128]{4,3,2,1,0:T(8,128)(2,1)S(1)}, u32[]{:S(2)}, u32[]{:S(2)}) collective-permute-start(bf16[4,4,2,32,128]{4,3,2,1,0:T(8,128)(2,1)S(1)} %fusion.13), channel_id=1, source_target_pairs={{0,16},{16,0},{32,48},{48,32},{64,80},{80,64},{96,112},{112,96},{1... | collective-permute-start | bytes 786440 | tf_op jit(solution)/shard_map/ppermute | solution.py:117
  39.6 1.5 %collective-permute-done = bf16[4,4,2,32,128]{4,3,2,1,0:T(8,128)(2,1)S(1)} collective-permute-done((bf16[4,4,2,32,128]{4,3,2,1,0:T(8,128)(2,1)S(1)}, bf16[4,4,2,32,128]{4,3,2,1,0:T(8,128)(2,1)S(1)}, u32[]{:S(2)}, u32[]{:S(2)}) %collective-permute-start) | collective-permute-done | bytes 262176 | tf_op jit(solution)/shard_map/ppermute | solution.py:117
  41.1 0.8 %fusion.12 = bf16[4,4,2,32,128]{4,3,2,1,0:T(8,128)(2,1)} fusion(bf16[4,4,2,32,128]{4,3,2,1,0:T(8,128)(2,1)S(1)} %collective-permute-done, f32[2,4,4,2,32,128]{5,4,3,2,1,0:T(8,128)S(1)} %bitcast.69, s32[]{:T(128)S(6)} %select_n.62), kind=kLoop, calls=%fused_computation.24 | loop fusion | flops 393216 | bytes 1048580 | tf_op jit(solution)/shard_map/convert_element_type | solution.py:111
  41.9 4.5 %all-to-all-start.2 = ((bf16[4,4,2,32,128]{4,3,2,1,0:T(8,128)(2,1)}), bf16[4,4,2,32,128]{4,3,2,1,0:T(8,128)(2,1)S(1)}, u32[]{:S(2)}, u32[]{:S(2)}) async-start(bf16[4,4,2,32,128]{4,3,2,1,0:T(8,128)(2,1)} %fusion.12), calls=%async_computation.2 | async-start | bytes 524288 | tf_op jit(solution)/shard_map/all_to_all | solution.py:110
  46.3 0.0 copy-start.1
  46.4 7.0 %all-to-all-done.2 = bf16[4,4,2,32,128]{4,3,2,1,0:T(8,128)(2,1)S(1)} async-done(((bf16[4,4,2,32,128]{4,3,2,1,0:T(8,128)(2,1)}), bf16[4,4,2,32,128]{4,3,2,1,0:T(8,128)(2,1)S(1)}, u32[]{:S(2)}, u32[]{:S(2)}) %all-to-all-start.2) | async-done | bytes 262176 | tf_op jit(solution)/shard_map/all_to_all | solution.py:110
  53.4 9.1 %collective-permute-start.1 = (bf16[2,2,32,128]{3,2,1,0:T(8,128)(2,1)S(1)}, bf16[2,2,32,128]{3,2,1,0:T(8,128)(2,1)S(1)}, u32[]{:S(2)}, u32[]{:S(2)}) collective-permute-start(bf16[2,2,32,128]{3,2,1,0:T(8,128)(2,1)S(1)} %pad_maximum_fusion), channel_id=1, source_target_pairs={{0,32},{16,48},{32,64},{48,80},{64,96},{80,112},{96,0},{112,16},{1... | collective-permute-start | bytes 98312 | tf_op jit(solution)/shard_map/ppermute | solution.py:100
  62.5 2.9 %collective-permute-start.2 = (bf16[2,32,128]{2,1,0:T(8,128)(2,1)S(1)}, bf16[2,32,128]{2,1,0:T(8,128)(2,1)S(1)}, u32[]{:S(2)}, u32[]{:S(2)}) collective-permute-start(bf16[2,32,128]{2,1,0:T(8,128)(2,1)S(1)} %get-tuple-element.6), channel_id=1, source_target_pairs={{0,96},{16,112},{32,0},{48,16},{64,32},{80,48},{96,64},{112,80},{1... | collective-permute-start | bytes 49160 | tf_op jit(solution)/shard_map/ppermute | solution.py:101
  65.4 0.0 collective-permute-done.1
  65.4 6.9 %collective-permute-start.3 = (bf16[2,32,128]{2,1,0:T(8,128)(2,1)S(1)}, bf16[2,32,128]{2,1,0:T(8,128)(2,1)S(1)}, u32[]{:S(2)}, u32[]{:S(2)}) collective-permute-start(bf16[2,32,128]{2,1,0:T(8,128)(2,1)S(1)} %slice_bitcast_fusion), channel_id=1, source_target_pairs={{0,32},{16,48},{32,64},{48,80},{64,96},{80,112},{96,0},{112,16},{1... | collective-permute-start | bytes 49160 | tf_op jit(solution)/shard_map/ppermute | solution.py:102
  72.3 0.0 copy-done.1
  72.3 0.9 %convolution_convert_fusion = bf16[8,128,128]{1,2,0:T(8,128)(2,1)} fusion(bf16[1,8,128,128]{3,2,1,0:T(8,128)(2,1)S(1)} %copy-done.1, bf16[8,16,8,128]{3,2,0,1:T(8,128)(2,1)S(1)} %bitcast.71), kind=kOutput, calls=%fused_computation.4 | convolution fusion | flops 33685504 | bytes 786432 | tf_op jit(solution)/shard_map/ijt,ikj->ikt/dot_general | solution.py:155
  73.2 0.0 collective-permute-done.2
  73.3 2.0 %collective-permute-done.3 = bf16[2,32,128]{2,1,0:T(8,128)(2,1)S(1)} collective-permute-done((bf16[2,32,128]{2,1,0:T(8,128)(2,1)S(1)}, bf16[2,32,128]{2,1,0:T(8,128)(2,1)S(1)}, u32[]{:S(2)}, u32[]{:S(2)}) %collective-permute-start.3) | collective-permute-done | bytes 16416 | tf_op jit(solution)/shard_map/ppermute | solution.py:102
  75.3 0.6 fusion.28
  (6 shorter events, 0.1 us)
Async XLA Ops:
  0.6 19.7 %copy-start = (bf16[1,8,128,128]{3,2,1,0:T(8,128)(2,1)S(1)}, bf16[1,8,128,128]{3,2,1,0:T(8,128)(2,1)}, u32[]{:S(2)}) copy-start(bf16[1,8,128,128]{3,2,1,0:T(8,128)(2,1)} %param.7) | copy-start | bytes 786436
  2.2 18.2 %copy-start.3 = (bf16[1024,128]{1,0:T(8,128)(2,1)S(1)}, bf16[1024,128]{1,0:T(8,128)(2,1)}, u32[]{:S(2)}) copy-start(bf16[1024,128]{1,0:T(8,128)(2,1)} %param.5) | copy-start | bytes 786436
  22.9 13.7 %all-to-all-start.1 = ((bf16[128,8,128]{2,1,0:T(8,128)(2,1)}), bf16[128,8,128]{2,1,0:T(8,128)(2,1)S(1)}, u32[]{:S(2)}, u32[]{:S(2)}) async-start(bf16[128,8,128]{2,1,0:T(8,128)(2,1)} %copy.30), calls=%async_computation.1 | async-start | bytes 524288 | tf_op jit(solution)/shard_map/all_to_all | solution.py:159
  28.3 8.3 %copy-start.2 = (bf16[1024,128]{1,0:T(8,128)(2,1)S(1)}, bf16[1024,128]{1,0:T(8,128)(2,1)}, u32[]{:S(2)}) copy-start(bf16[1024,128]{1,0:T(8,128)(2,1)} %param.4) | copy-start | bytes 786436
  37.7 3.4 %collective-permute-start = (bf16[4,4,2,32,128]{4,3,2,1,0:T(8,128)(2,1)S(1)}, bf16[4,4,2,32,128]{4,3,2,1,0:T(8,128)(2,1)S(1)}, u32[]{:S(2)}, u32[]{:S(2)}) collective-permute-start(bf16[4,4,2,32,128]{4,3,2,1,0:T(8,128)(2,1)S(1)} %fusion.13), channel_id=1, source_target_pairs={{0,16},{16,0},{32,48},{48,32},{64,80},{80,64},{96,112},{112,96},{1... | collective-permute-start | bytes 786440 | tf_op jit(solution)/shard_map/ppermute | solution.py:117
  41.9 11.4 %all-to-all-start.2 = ((bf16[4,4,2,32,128]{4,3,2,1,0:T(8,128)(2,1)}), bf16[4,4,2,32,128]{4,3,2,1,0:T(8,128)(2,1)S(1)}, u32[]{:S(2)}, u32[]{:S(2)}) async-start(bf16[4,4,2,32,128]{4,3,2,1,0:T(8,128)(2,1)} %fusion.12), calls=%async_computation.2 | async-start | bytes 524288 | tf_op jit(solution)/shard_map/all_to_all | solution.py:110
  46.3 26.0 %copy-start.1 = (bf16[1,8,128,128]{3,2,1,0:T(8,128)(2,1)S(1)}, bf16[1,8,128,128]{3,2,1,0:T(8,128)(2,1)}, u32[]{:S(2)}) copy-start(bf16[1,8,128,128]{3,2,1,0:T(8,128)(2,1)} %param.6) | copy-start | bytes 786436
  53.4 12.0 %collective-permute-start.1 = (bf16[2,2,32,128]{3,2,1,0:T(8,128)(2,1)S(1)}, bf16[2,2,32,128]{3,2,1,0:T(8,128)(2,1)S(1)}, u32[]{:S(2)}, u32[]{:S(2)}) collective-permute-start(bf16[2,2,32,128]{3,2,1,0:T(8,128)(2,1)S(1)} %pad_maximum_fusion), channel_id=1, source_target_pairs={{0,32},{16,48},{32,64},{48,80},{64,96},{80,112},{96,0},{112,16},{1... | collective-permute-start | bytes 98312 | tf_op jit(solution)/shard_map/ppermute | solution.py:100
  62.5 10.7 %collective-permute-start.2 = (bf16[2,32,128]{2,1,0:T(8,128)(2,1)S(1)}, bf16[2,32,128]{2,1,0:T(8,128)(2,1)S(1)}, u32[]{:S(2)}, u32[]{:S(2)}) collective-permute-start(bf16[2,32,128]{2,1,0:T(8,128)(2,1)S(1)} %get-tuple-element.6), channel_id=1, source_target_pairs={{0,96},{16,112},{32,0},{48,16},{64,32},{80,48},{96,64},{112,80},{1... | collective-permute-start | bytes 49160 | tf_op jit(solution)/shard_map/ppermute | solution.py:101
  65.4 9.9 %collective-permute-start.3 = (bf16[2,32,128]{2,1,0:T(8,128)(2,1)S(1)}, bf16[2,32,128]{2,1,0:T(8,128)(2,1)S(1)}, u32[]{:S(2)}, u32[]{:S(2)}) collective-permute-start(bf16[2,32,128]{2,1,0:T(8,128)(2,1)S(1)} %slice_bitcast_fusion), channel_id=1, source_target_pairs={{0,32},{16,48},{32,64},{48,80},{64,96},{80,112},{96,0},{112,16},{1... | collective-permute-start | bytes 49160 | tf_op jit(solution)/shard_map/ppermute | solution.py:102

commit v7 on v6

--- a/solution.py
+++ b/solution.py
@@ -96,11 +96,11 @@
 
         if size == 4 and distance > 1:
             wide = x.dtype
-            ahead = jnp.stack([pick(1), pick(2)], 0).astype(jnp.bfloat16)
-            ahead = lax.ppermute(ahead, "dp", perm=pairs(1))
+            ahead = lax.ppermute(pick(2).astype(jnp.bfloat16), "dp", perm=pairs(1))
             behind = lax.ppermute(pick(-1).astype(jnp.bfloat16), "dp", perm=pairs(-1))
-            relayed = lax.ppermute(ahead[1], "dp", perm=pairs(1))
-            x = pick(0) + ahead[0].astype(wide) + behind.astype(wide) + relayed.astype(wide)
+            carried = (ahead.astype(wide) + pick(1)).astype(jnp.bfloat16)
+            relayed = lax.ppermute(carried, "dp", perm=pairs(1))
+            x = pick(0) + behind.astype(wide) + relayed.astype(wide)
             continue
         if size == 4:
             groups = []

time: 76.4 us -> 76 us (level)
  no operation moved by 1% of the time
where the time goes in v7:
time: 76 us; the launch traced here: 75.6 us
  starting transfers between devices  30.4 us (40%)
  waiting for transfers between devices  18.2 us (24%)
  blocking collectives  18.1 us (24%)
  matrix products  4.51 us (6%)
  local copies, waits for them, and re-layouts  2.62 us (3%)
  other arithmetic  0.93 us (1%)
  between operations  0.85 us (1%)
    all_to_all x1, blocking collectives, forward_layer(): lax.all_to_all(first_out, 'mp', split_axis=1, concat_axis=0, tiled=True)  18.1 us
    ppermute x1, starting transfers between devices, staged_reduce_scatter(): ahead = lax.ppermute(pick(2).astype(jnp.bfloat16), 'dp', perm=pairs(1))  9.1 us
    all_to_all x1, waiting for transfers between devices, shards(): lax.all_to_all(grad_first, 'mp', split_axis=0, concat_axis=1, tiled=True)  7.99 us
    all_to_all x1, waiting for transfers between devices, staged_reduce_scatter(): lax.all_to_all(x.astype(jnp.bfloat16), 'dp', 0, 0, tiled=True, axis_index...  6.97 us
    ppermute x1, starting transfers between devices, staged_reduce_scatter(): relayed = lax.ppermute(carried, 'dp', perm=pairs(1))  6.9 us
    all_to_all x1, starting transfers between devices, shards(): lax.all_to_all(grad_first, 'mp', split_axis=0, concat_axis=1, tiled=True)  5.13 us
    all_to_all x1, starting transfers between devices, staged_reduce_scatter(): lax.all_to_all(x.astype(jnp.bfloat16), 'dp', 0, 0, tiled=True, axis_index...  4.48 us
    ppermute x1, starting transfers between devices, staged_reduce_scatter(): behind = lax.ppermute(pick(-1).astype(jnp.bfloat16), 'dp', perm=pairs(-1))  2.85 us
  transfers between devices with their start and end apart: 6, of which 4 were waited for; matrix products, arithmetic and copies ran while one was open for 2% of the time, Pallas kernels for 0%

profile of v7, /device:TPU:2, one launch (start us, length us, event | category | flops | bytes accessed | tf_op | source)
XLA Modules:
  0.0 75.6 jit_solution(12089183813816211438)
XLA Ops:
  0.6 0.0 copy-start
  0.6 1.3 %convolution_convert_fusion.2 = bf16[8,128,128]{2,1,0:T(8,128)(2,1)S(1)} fusion(bf16[8,128,128]{2,1,0:T(8,128)(2,1)} %bitcast.78, bf16[1,8,128,128]{3,2,1,0:T(8,128)(2,1)} %param.6), kind=kOutput, calls=%fused_computation.6 | convolution fusion | flops 33685504 | bytes 786432 | tf_op jit(solution)/shard_map/ikt,ikj->ijt/dot_general | solution.py:22
  2.0 0.2 copy.26
  2.2 0.0 copy-start.3
  2.2 18.1 %all_to_all.41 = bf16[8,128,128]{2,0,1:T(8,128)(2,1)S(1)} all-to-all(bf16[8,128,128]{2,0,1:T(8,128)(2,1)S(1)} %copy.26), channel_id=1, replica_groups=mesh['dp'=32,'mp'=16] {'mp'}, dimensions={1} | all-to-all | bytes 524288 | tf_op jit(solution)/shard_map/all_to_all | solution.py:30
  20.3 0.0 copy-done
  20.3 0.0 copy-done.3
  20.3 1.3 %fusion.4 = (bf16[8,128,128]{2,1,0:T(8,128)(2,1)S(1)}, bf16[8,128,128]{2,1,0:T(8,128)(2,1)}) fusion(bf16[8,128,128]{2,1,0:T(8,128)(2,1)S(1)} %bitcast.85, bf16[1,8,128,128]{3,2,1,0:T(8,128)(2,1)S(1)} %copy-done, bf16[8,16,8,128]{3,0,2,1:T(8,128)(2,1)S(1)} %bitcast.80), kind=kOutput, calls=%fused_computation.15 | convolution fusion | flops 36569088 | bytes 1310720 | tf_op jit(solution)/shard_map/ijt,jim->jmt/dot_general | solution.py:14
  21.7 0.3 fusion.1
  22.0 0.9 %copy.30 = bf16[128,8,128]{2,1,0:T(8,128)(2,1)} copy(bf16[128,8,128]{0,2,1:T(8,128)(2,1)S(1)} %fusion.1) | data formatting | bytes 524288 | tf_op jit(solution)/shard_map/convert_element_type | solution.py:152
  22.9 5.1 %all-to-all-start.1 = ((bf16[128,8,128]{2,1,0:T(8,128)(2,1)}), bf16[128,8,128]{2,1,0:T(8,128)(2,1)S(1)}, u32[]{:S(2)}, u32[]{:S(2)}) async-start(bf16[128,8,128]{2,1,0:T(8,128)(2,1)} %copy.30), calls=%async_computation.1 | async-start | bytes 524288 | tf_op jit(solution)/shard_map/all_to_all | solution.py:159
  28.0 0.3 convolution_multiply_fusion.1
  28.3 0.0 copy-start.2
  28.3 0.3 copy.34
  28.6 8.0 %all-to-all-done.1 = bf16[128,8,128]{2,1,0:T(8,128)(2,1)S(1)} async-done(((bf16[128,8,128]{2,1,0:T(8,128)(2,1)}), bf16[128,8,128]{2,1,0:T(8,128)(2,1)S(1)}, u32[]{:S(2)}, u32[]{:S(2)}) %all-to-all-start.1) | async-done | bytes 262176 | tf_op jit(solution)/shard_map/all_to_all | solution.py:159
  36.6 0.0 copy-done.2
  36.6 0.3 fusion
  36.9 0.2 copy.33
  37.2 0.1 maximum_bitcast_fusion
  37.3 0.3 copy.35
  37.7 1.9 %collective-permute-start = (bf16[4,4,2,32,128]{4,3,2,1,0:T(8,128)(2,1)S(1)}, bf16[4,4,2,32,128]{4,3,2,1,0:T(8,128)(2,1)S(1)}, u32[]{:S(2)}, u32[]{:S(2)}) collective-permute-start(bf16[4,4,2,32,128]{4,3,2,1,0:T(8,128)(2,1)S(1)} %fusion.13), channel_id=1, source_target_pairs={{0,16},{16,0},{32,48},{48,32},{64,80},{80,64},{96,112},{112,96},{1... | collective-permute-start | bytes 786440 | tf_op jit(solution)/shard_map/ppermute | solution.py:117
  39.6 1.5 %collective-permute-done = bf16[4,4,2,32,128]{4,3,2,1,0:T(8,128)(2,1)S(1)} collective-permute-done((bf16[4,4,2,32,128]{4,3,2,1,0:T(8,128)(2,1)S(1)}, bf16[4,4,2,32,128]{4,3,2,1,0:T(8,128)(2,1)S(1)}, u32[]{:S(2)}, u32[]{:S(2)}) %collective-permute-start) | collective-permute-done | bytes 262176 | tf_op jit(solution)/shard_map/ppermute | solution.py:117
  41.1 0.8 %fusion.12 = bf16[4,4,2,32,128]{4,3,2,1,0:T(8,128)(2,1)} fusion(bf16[4,4,2,32,128]{4,3,2,1,0:T(8,128)(2,1)S(1)} %collective-permute-done, f32[2,4,4,2,32,128]{5,4,3,2,1,0:T(8,128)S(1)} %bitcast.73, s32[]{:T(128)S(6)} %select_n.62), kind=kLoop, calls=%fused_computation.24 | loop fusion | flops 393216 | bytes 1048580 | tf_op jit(solution)/shard_map/convert_element_type | solution.py:111
  41.9 4.5 %all-to-all-start.2 = ((bf16[4,4,2,32,128]{4,3,2,1,0:T(8,128)(2,1)}), bf16[4,4,2,32,128]{4,3,2,1,0:T(8,128)(2,1)S(1)}, u32[]{:S(2)}, u32[]{:S(2)}) async-start(bf16[4,4,2,32,128]{4,3,2,1,0:T(8,128)(2,1)} %fusion.12), calls=%async_computation.2 | async-start | bytes 524288 | tf_op jit(solution)/shard_map/all_to_all | solution.py:110
  46.3 0.0 copy-start.1
  46.4 7.0 %all-to-all-done.2 = bf16[4,4,2,32,128]{4,3,2,1,0:T(8,128)(2,1)S(1)} async-done(((bf16[4,4,2,32,128]{4,3,2,1,0:T(8,128)(2,1)}), bf16[4,4,2,32,128]{4,3,2,1,0:T(8,128)(2,1)S(1)}, u32[]{:S(2)}, u32[]{:S(2)}) %all-to-all-start.2) | async-done | bytes 262176 | tf_op jit(solution)/shard_map/all_to_all | solution.py:110
  53.4 9.1 %collective-permute-start.2 = (bf16[2,32,128]{2,1,0:T(8,128)(2,1)S(1)}, bf16[2,32,128]{2,1,0:T(8,128)(2,1)S(1)}, u32[]{:S(2)}, u32[]{:S(2)}) collective-permute-start(bf16[2,32,128]{2,1,0:T(8,128)(2,1)S(1)} %get-tuple-element.7), channel_id=1, source_target_pairs={{0,32},{16,48},{32,64},{48,80},{64,96},{80,112},{96,0},{112,16},{1... | collective-permute-start | bytes 49160 | tf_op jit(solution)/shard_map/ppermute | solution.py:99
  62.5 2.9 %collective-permute-start.1 = (bf16[2,32,128]{2,1,0:T(8,128)(2,1)S(1)}, bf16[2,32,128]{2,1,0:T(8,128)(2,1)S(1)}, u32[]{:S(2)}, u32[]{:S(2)}) collective-permute-start(bf16[2,32,128]{2,1,0:T(8,128)(2,1)S(1)} %get-tuple-element.6), channel_id=1, source_target_pairs={{0,96},{16,112},{32,0},{48,16},{64,32},{80,48},{96,64},{112,80},{1... | collective-permute-start | bytes 49160 | tf_op jit(solution)/shard_map/ppermute | solution.py:100
  65.4 0.0 collective-permute-done.2
  65.4 6.9 %collective-permute-start.3 = (bf16[2,32,128]{2,1,0:T(8,128)(2,1)S(1)}, bf16[2,32,128]{2,1,0:T(8,128)(2,1)S(1)}, u32[]{:S(2)}, u32[]{:S(2)}) collective-permute-start(bf16[2,32,128]{2,1,0:T(8,128)(2,1)S(1)} %fusion.26), channel_id=1, source_target_pairs={{0,32},{16,48},{32,64},{48,80},{64,96},{80,112},{96,0},{112,16},{1... | collective-permute-start | bytes 49160 | tf_op jit(solution)/shard_map/ppermute | solution.py:102
  72.3 0.0 copy-done.1
  72.3 0.9 %convolution_convert_fusion = bf16[8,128,128]{1,2,0:T(8,128)(2,1)} fusion(bf16[1,8,128,128]{3,2,1,0:T(8,128)(2,1)S(1)} %copy-done.1, bf16[8,16,8,128]{3,2,0,1:T(8,128)(2,1)S(1)} %bitcast.75), kind=kOutput, calls=%fused_computation.4 | convolution fusion | flops 33685504 | bytes 786432 | tf_op jit(solution)/shard_map/ijt,ikj->ikt/dot_general | solution.py:155
  73.3 0.0 collective-permute-done.1
  73.3 1.7 %collective-permute-done.3 = bf16[2,32,128]{2,1,0:T(8,128)(2,1)S(1)} collective-permute-done((bf16[2,32,128]{2,1,0:T(8,128)(2,1)S(1)}, bf16[2,32,128]{2,1,0:T(8,128)(2,1)S(1)}, u32[]{:S(2)}, u32[]{:S(2)}) %collective-permute-start.3) | collective-permute-done | bytes 16416 | tf_op jit(solution)/shard_map/ppermute | solution.py:102
  75.0 0.6 fusion.30
  (5 shorter events, 0.1 us)
Async XLA Ops:
  0.6 19.7 %copy-start = (bf16[1,8,128,128]{3,2,1,0:T(8,128)(2,1)S(1)}, bf16[1,8,128,128]{3,2,1,0:T(8,128)(2,1)}, u32[]{:S(2)}) copy-start(bf16[1,8,128,128]{3,2,1,0:T(8,128)(2,1)} %param.7) | copy-start | bytes 786436
  2.2 18.2 %copy-start.3 = (bf16[1024,128]{1,0:T(8,128)(2,1)S(1)}, bf16[1024,128]{1,0:T(8,128)(2,1)}, u32[]{:S(2)}) copy-start(bf16[1024,128]{1,0:T(8,128)(2,1)} %param.5) | copy-start | bytes 786436
  22.9 13.7 %all-to-all-start.1 = ((bf16[128,8,128]{2,1,0:T(8,128)(2,1)}), bf16[128,8,128]{2,1,0:T(8,128)(2,1)S(1)}, u32[]{:S(2)}, u32[]{:S(2)}) async-start(bf16[128,8,128]{2,1,0:T(8,128)(2,1)} %copy.30), calls=%async_computation.1 | async-start | bytes 524288 | tf_op jit(solution)/shard_map/all_to_all | solution.py:159
  28.3 8.3 %copy-start.2 = (bf16[1024,128]{1,0:T(8,128)(2,1)S(1)}, bf16[1024,128]{1,0:T(8,128)(2,1)}, u32[]{:S(2)}) copy-start(bf16[1024,128]{1,0:T(8,128)(2,1)} %param.4) | copy-start | bytes 786436
  37.7 3.4 %collective-permute-start = (bf16[4,4,2,32,128]{4,3,2,1,0:T(8,128)(2,1)S(1)}, bf16[4,4,2,32,128]{4,3,2,1,0:T(8,128)(2,1)S(1)}, u32[]{:S(2)}, u32[]{:S(2)}) collective-permute-start(bf16[4,4,2,32,128]{4,3,2,1,0:T(8,128)(2,1)S(1)} %fusion.13), channel_id=1, source_target_pairs={{0,16},{16,0},{32,48},{48,32},{64,80},{80,64},{96,112},{112,96},{1... | collective-permute-start | bytes 786440 | tf_op jit(solution)/shard_map/ppermute | solution.py:117
  41.9 11.4 %all-to-all-start.2 = ((bf16[4,4,2,32,128]{4,3,2,1,0:T(8,128)(2,1)}), bf16[4,4,2,32,128]{4,3,2,1,0:T(8,128)(2,1)S(1)}, u32[]{:S(2)}, u32[]{:S(2)}) async-start(bf16[4,4,2,32,128]{4,3,2,1,0:T(8,128)(2,1)} %fusion.12), calls=%async_computation.2 | async-start | bytes 524288 | tf_op jit(solution)/shard_map/all_to_all | solution.py:110
  46.3 26.0 %copy-start.1 = (bf16[1,8,128,128]{3,2,1,0:T(8,128)(2,1)S(1)}, bf16[1,8,128,128]{3,2,1,0:T(8,128)(2,1)}, u32[]{:S(2)}) copy-start(bf16[1,8,128,128]{3,2,1,0:T(8,128)(2,1)} %param.6) | copy-start | bytes 786436
  53.4 12.0 %collective-permute-start.2 = (bf16[2,32,128]{2,1,0:T(8,128)(2,1)S(1)}, bf16[2,32,128]{2,1,0:T(8,128)(2,1)S(1)}, u32[]{:S(2)}, u32[]{:S(2)}) collective-permute-start(bf16[2,32,128]{2,1,0:T(8,128)(2,1)S(1)} %get-tuple-element.7), channel_id=1, source_target_pairs={{0,32},{16,48},{32,64},{48,80},{64,96},{80,112},{96,0},{112,16},{1... | collective-permute-start | bytes 49160 | tf_op jit(solution)/shard_map/ppermute | solution.py:99
  62.5 10.7 %collective-permute-start.1 = (bf16[2,32,128]{2,1,0:T(8,128)(2,1)S(1)}, bf16[2,32,128]{2,1,0:T(8,128)(2,1)S(1)}, u32[]{:S(2)}, u32[]{:S(2)}) collective-permute-start(bf16[2,32,128]{2,1,0:T(8,128)(2,1)S(1)} %get-tuple-element.6), channel_id=1, source_target_pairs={{0,96},{16,112},{32,0},{48,16},{64,32},{80,48},{96,64},{112,80},{1... | collective-permute-start | bytes 49160 | tf_op jit(solution)/shard_map/ppermute | solution.py:100
  65.4 9.6 %collective-permute-start.3 = (bf16[2,32,128]{2,1,0:T(8,128)(2,1)S(1)}, bf16[2,32,128]{2,1,0:T(8,128)(2,1)S(1)}, u32[]{:S(2)}, u32[]{:S(2)}) collective-permute-start(bf16[2,32,128]{2,1,0:T(8,128)(2,1)S(1)} %fusion.26), channel_id=1, source_target_pairs={{0,32},{16,48},{32,64},{48,80},{64,96},{80,112},{96,0},{112,16},{1... | collective-permute-start | bytes 49160 | tf_op jit(solution)/shard_map/ppermute | solution.py:102

commit v8 on v5

--- a/solution.py
+++ b/solution.py
@@ -65,19 +65,23 @@
     return stages
 
 
-def staged_reduce_scatter(term, stages, count):
-    lead = term.shape[:-2]
-    rows, cols = term.shape[-2:]
+def stage_order(stages):
+    return sorted(stages, key=lambda s: (s[0], s[2]))
+
+
+def to_pieces(term, stages, count):
+    blocks, rows, cols = term.shape
     piece = rows // count
     by_stride = sorted(stages, key=lambda s: -s[2])
-    digit_sizes = [s[1] for s in by_stride]
-    x = term.reshape(lead + tuple(digit_sizes) + (piece, cols))
-    order = sorted(stages, key=lambda s: (s[0], s[2]))
-    nlead = len(lead)
-    perm = [nlead + by_stride.index(s) for s in order]
-    x = x.transpose(perm + list(range(nlead)) + list(range(nlead + len(stages), x.ndim)))
+    x = term.reshape((blocks,) + tuple(s[1] for s in by_stride) + (piece, cols))
+    perm = [1 + by_stride.index(s) for s in stage_order(stages)]
+    x = x.transpose(perm + [0, len(stages) + 1, len(stages) + 2])
+    return x.reshape(x.shape[: len(stages)] + (blocks * piece, cols))
+
+
+def reduce_stages(x, stages, count):
     me = lax.axis_index("dp")
-    for distance, size, stride in order:
+    for distance, size, stride in stages:
         mine = (me // stride) % size
 
         def pick(shift, x=x, mine=mine, size=size):
@@ -143,6 +147,8 @@
             jnp.einsum("ijt,jmt->jim", received, grad_pre, preferred_element_type=jnp.float32)
             * scale
         )
+        order = stage_order(stages)
+        early_l = reduce_stages(to_pieces(term_l, stages, dp_count), order[:1], dp_count)
         grad_first = jnp.einsum(
             "jmt,jim->ijt", grad_pre, left, preferred_element_type=jnp.float32
         ).astype(jnp.bfloat16)
@@ -158,9 +164,12 @@
             jnp.einsum("ikt,ijt->ikj", layer_in, returned, preferred_element_type=jnp.float32)
             * scale
         )
-        both = staged_reduce_scatter(jnp.stack([term_l, term_r], 0), stages, dp_count)
-        parts_l[layer_index] = both[0]
-        parts_r[layer_index] = both[1]
+        early_r = reduce_stages(to_pieces(term_r, stages, dp_count), order[:1], dp_count)
+        both = jnp.stack([early_l, early_r], len(stages) - 1)
+        both = reduce_stages(both, order[1:], dp_count)
+        piece = block_size // dp_count
+        parts_l[layer_index] = both[0].reshape(block_count, piece, block_size)
+        parts_r[layer_index] = both[1].reshape(block_count, piece, block_size)
     stack_r = jnp.stack(parts_r, 0)
     stack_l = jnp.stack(parts_l, 0)
     grad_inputs = grad_now.reshape(block_count * block_size, tokens_here)

time: 76.6 us -> 76.1 us (level)
  starting transfers between devices: 30.4 us -> 32.4 us
  waiting for transfers between devices: 18.5 us -> 16.5 us
    ppermute x4 -> x5, starting transfers between devices: 20.8 us -> 22.8 us  [the longest x1 9.1 us: reduce_stages(): ahead = lax.ppermute(ahead, 'dp', perm=pairs(1))]
    all_to_all x1, waiting for transfers between devices: 7.99 us -> 6.06 us  [shards(): lax.all_to_all(grad_first, 'mp', split_axis=0, concat_axis=1, tiled=True)]
    unnamed x10 -> x8, local copies, waits for them, and re-layouts: 1.24 us -> 0.03 us
    ppermute x4 -> x5, waiting for transfers between devices: 3.52 us -> 3.42 us  [the longest x1 2.16 us: reduce_stages(): relayed = lax.ppermute(ahead[1], 'dp', perm=pairs(1))]
  transfers between devices with their start and end apart: 6 -> 7, of which waited for: 4 -> 4; matrix products, arithmetic and copies ran while one was open for 2% -> 3% of each run, Pallas kernels for 0% -> 0%
where the time goes in v8:
time: 76.1 us; the launch traced here: 75.6 us
  starting transfers between devices  32.4 us (43%)
  blocking collectives  18.1 us (24%)
  waiting for transfers between devices  16.5 us (22%)
  matrix products  4.51 us (6%)
  local copies, waits for them, and re-layouts  3.02 us (4%)
  between operations  0.86 us (1%)
    all_to_all x1, blocking collectives, forward_layer(): lax.all_to_all(first_out, 'mp', split_axis=1, concat_axis=0, tiled=True)  18.1 us
    ppermute x1, starting transfers between devices, reduce_stages(): ahead = lax.ppermute(ahead, 'dp', perm=pairs(1))  9.1 us
    all_to_all x1, waiting for transfers between devices, reduce_stages(): lax.all_to_all(x.astype(jnp.bfloat16), 'dp', 0, 0, tiled=True, axis_index...  6.98 us
    ppermute x1, starting transfers between devices, reduce_stages(): relayed = lax.ppermute(ahead[1], 'dp', perm=pairs(1))  6.9 us
    all_to_all x1, waiting for transfers between devices, shards(): lax.all_to_all(grad_first, 'mp', split_axis=0, concat_axis=1, tiled=True)  6.06 us
    all_to_all x1, starting transfers between devices, shards(): lax.all_to_all(grad_first, 'mp', split_axis=0, concat_axis=1, tiled=True)  5.13 us
    all_to_all x1, starting transfers between devices, reduce_stages(): lax.all_to_all(x.astype(jnp.bfloat16), 'dp', 0, 0, tiled=True, axis_index...  4.48 us
    ppermute x2, starting transfers between devices, reduce_stages(): lax.ppermute(pick(shift).astype(jnp.bfloat16), 'dp', perm=pairs(shift))  3.97 us
  transfers between devices with their start and end apart: 7, of which 4 were waited for; matrix products, arithmetic and copies ran while one was open for 3% of the time, Pallas kernels for 0%

profile of v8, /device:TPU:2, one launch (start us, length us, event | category | flops | bytes accessed | tf_op | source)
XLA Modules:
  0.0 75.6 jit_solution(3672980516060191751)
XLA Ops:
  0.6 0.0 copy-start
  0.6 1.3 %convolution_convert_fusion.2 = bf16[8,128,128]{2,1,0:T(8,128)(2,1)S(1)} fusion(bf16[8,128,128]{2,1,0:T(8,128)(2,1)} %bitcast.107, bf16[1,8,128,128]{3,2,1,0:T(8,128)(2,1)} %param.6), kind=kOutput, calls=%fused_computation.6 | convolution fusion | flops 33685504 | bytes 786432 | tf_op jit(solution)/shard_map/ikt,ikj->ijt/dot_general | solution.py:22
  2.0 0.2 copy.25
  2.2 0.0 copy-start.3
  2.2 18.1 %all_to_all.41 = bf16[8,128,128]{2,0,1:T(8,128)(2,1)S(1)} all-to-all(bf16[8,128,128]{2,0,1:T(8,128)(2,1)S(1)} %copy.25), channel_id=1, replica_groups=mesh['dp'=32,'mp'=16] {'mp'}, dimensions={1} | all-to-all | bytes 524288 | tf_op jit(solution)/shard_map/all_to_all | solution.py:30
  20.3 0.0 copy-done
  20.3 0.0 copy-done.3
  20.3 1.3 %fusion.4 = (bf16[8,128,128]{2,1,0:T(8,128)(2,1)S(1)}, bf16[8,128,128]{2,1,0:T(8,128)(2,1)}) fusion(bf16[8,128,128]{2,1,0:T(8,128)(2,1)S(1)} %bitcast.114, bf16[1,8,128,128]{3,2,1,0:T(8,128)(2,1)S(1)} %copy-done, bf16[8,16,8,128]{3,0,2,1:T(8,128)(2,1)S(1)} %bitcast.109), kind=kOutput, calls=%fused_computation.14 | convolution fusion | flops 36569088 | bytes 1310720 | tf_op jit(solution)/shard_map/ijt,jim->jmt/dot_general | solution.py:14
  21.7 0.3 fusion.1
  22.0 0.9 %copy.29 = bf16[128,8,128]{2,1,0:T(8,128)(2,1)} copy(bf16[128,8,128]{0,2,1:T(8,128)(2,1)S(1)} %fusion.1) | data formatting | bytes 524288 | tf_op jit(solution)/shard_map/convert_element_type | solution.py:154
  22.9 5.1 %all-to-all-start.1 = ((bf16[128,8,128]{2,1,0:T(8,128)(2,1)}), bf16[128,8,128]{2,1,0:T(8,128)(2,1)S(1)}, u32[]{:S(2)}, u32[]{:S(2)}) async-start(bf16[128,8,128]{2,1,0:T(8,128)(2,1)} %copy.29), calls=%async_computation.1 | async-start | bytes 524288 | tf_op jit(solution)/shard_map/all_to_all | solution.py:161
  28.0 0.3 convolution_multiply_fusion.1
  28.3 0.1 copy.31
  28.5 0.0 copy-start.2
  28.5 2.1 %collective-permute-start = (bf16[4,4,32,128]{3,2,1,0:T(8,128)(2,1)S(1)}, bf16[4,4,32,128]{3,2,1,0:T(8,128)(2,1)S(1)}, u32[]{:S(2)}, u32[]{:S(2)}) collective-permute-start(bf16[4,4,32,128]{3,2,1,0:T(8,128)(2,1)S(1)} %fusion.26), channel_id=1, source_target_pairs={{0,16},{16,0},{32,48},{48,32},{64,80},{80,64},{96,112},{112,96},{1... | collective-permute-start | bytes 393224 | tf_op jit(solution)/shard_map/ppermute | solution.py:117
  30.6 6.1 %all-to-all-done.1 = bf16[128,8,128]{2,1,0:T(8,128)(2,1)S(1)} async-done(((bf16[128,8,128]{2,1,0:T(8,128)(2,1)}), bf16[128,8,128]{2,1,0:T(8,128)(2,1)S(1)}, u32[]{:S(2)}, u32[]{:S(2)}) %all-to-all-start.1) | async-done | bytes 262176 | tf_op jit(solution)/shard_map/all_to_all | solution.py:161
  36.6 0.0 copy-done.2
  36.6 0.3 fusion
  36.9 0.2 copy.33
  37.2 0.1 copy.34
  37.4 1.9 %collective-permute-start.1 = (bf16[4,4,32,128]{3,2,1,0:T(8,128)(2,1)S(1)}, bf16[4,4,32,128]{3,2,1,0:T(8,128)(2,1)S(1)}, u32[]{:S(2)}, u32[]{:S(2)}) collective-permute-start(bf16[4,4,32,128]{3,2,1,0:T(8,128)(2,1)S(1)} %fusion.27), channel_id=1, source_target_pairs={{0,16},{16,0},{32,48},{48,32},{64,80},{80,64},{96,112},{112,96},{1... | collective-permute-start | bytes 393224 | tf_op jit(solution)/shard_map/ppermute | solution.py:117
  39.3 0.0 collective-permute-done
  39.3 1.3 %collective-permute-done.1 = bf16[4,4,32,128]{3,2,1,0:T(8,128)(2,1)S(1)} collective-permute-done((bf16[4,4,32,128]{3,2,1,0:T(8,128)(2,1)S(1)}, bf16[4,4,32,128]{3,2,1,0:T(8,128)(2,1)S(1)}, u32[]{:S(2)}, u32[]{:S(2)}) %collective-permute-start.1) | collective-permute-done | bytes 131104 | tf_op jit(solution)/shard_map/ppermute | solution.py:117
  40.7 0.7 copy.35
  41.4 4.5 %all-to-all-start.2 = ((bf16[4,4,2,32,128]{4,3,1,2,0:T(8,128)(2,1)}), bf16[4,4,2,32,128]{4,3,1,2,0:T(8,128)(2,1)S(1)}, u32[]{:S(2)}, u32[]{:S(2)}) async-start(bf16[4,4,2,32,128]{4,3,1,2,0:T(8,128)(2,1)} %copy.35), calls=%async_computation.2 | async-start | bytes 524288 | tf_op jit(solution)/shard_map/all_to_all | solution.py:110
  45.9 0.0 copy-start.1
  45.9 7.0 %all-to-all-done.2 = bf16[4,4,2,32,128]{4,3,1,2,0:T(8,128)(2,1)S(1)} async-done(((bf16[4,4,2,32,128]{4,3,1,2,0:T(8,128)(2,1)}), bf16[4,4,2,32,128]{4,3,1,2,0:T(8,128)(2,1)S(1)}, u32[]{:S(2)}, u32[]{:S(2)}) %all-to-all-start.2) | async-done | bytes 262176 | tf_op jit(solution)/shard_map/all_to_all | solution.py:110
  52.9 9.1 %collective-permute-start.2 = (bf16[2,2,32,128]{3,2,1,0:T(8,128)(2,1)S(1)}, bf16[2,2,32,128]{3,2,1,0:T(8,128)(2,1)S(1)}, u32[]{:S(2)}, u32[]{:S(2)}) collective-permute-start(bf16[2,2,32,128]{3,2,1,0:T(8,128)(2,1)S(1)} %pad_maximum_fusion.1), channel_id=1, source_target_pairs={{0,32},{16,48},{32,64},{48,80},{64,96},{80,112},{96,0},{112,16},{1... | collective-permute-start | bytes 98312 | tf_op jit(solution)/shard_map/ppermute | solution.py:100
  62.1 2.9 %collective-permute-start.3 = (bf16[2,32,128]{2,1,0:T(8,128)(2,1)S(1)}, bf16[2,32,128]{2,1,0:T(8,128)(2,1)S(1)}, u32[]{:S(2)}, u32[]{:S(2)}) collective-permute-start(bf16[2,32,128]{2,1,0:T(8,128)(2,1)S(1)} %get-tuple-element.6), channel_id=1, source_target_pairs={{0,96},{16,112},{32,0},{48,16},{64,32},{80,48},{96,64},{112,80},{1... | collective-permute-start | bytes 49160 | tf_op jit(solution)/shard_map/ppermute | solution.py:101
  64.9 0.0 collective-permute-done.2
  64.9 6.9 %collective-permute-start.4 = (bf16[2,32,128]{2,1,0:T(8,128)(2,1)S(1)}, bf16[2,32,128]{2,1,0:T(8,128)(2,1)S(1)}, u32[]{:S(2)}, u32[]{:S(2)}) collective-permute-start(bf16[2,32,128]{2,1,0:T(8,128)(2,1)S(1)} %slice_bitcast_fusion), channel_id=1, source_target_pairs={{0,32},{16,48},{32,64},{48,80},{64,96},{80,112},{96,0},{112,16},{1... | collective-permute-start | bytes 49160 | tf_op jit(solution)/shard_map/ppermute | solution.py:102
  71.9 0.0 copy-done.1
  71.9 0.9 %convolution_convert_fusion = bf16[8,128,128]{1,2,0:T(8,128)(2,1)} fusion(bf16[1,8,128,128]{3,2,1,0:T(8,128)(2,1)S(1)} %copy-done.1, bf16[8,16,8,128]{3,2,0,1:T(8,128)(2,1)S(1)} %bitcast.100), kind=kOutput, calls=%fused_computation.4 | convolution fusion | flops 33685504 | bytes 786432 | tf_op jit(solution)/shard_map/ijt,ikj->ikt/dot_general | solution.py:157
  72.8 0.0 collective-permute-done.3
  72.8 2.2 %collective-permute-done.4 = bf16[2,32,128]{2,1,0:T(8,128)(2,1)S(1)} collective-permute-done((bf16[2,32,128]{2,1,0:T(8,128)(2,1)S(1)}, bf16[2,32,128]{2,1,0:T(8,128)(2,1)S(1)}, u32[]{:S(2)}, u32[]{:S(2)}) %collective-permute-start.4) | collective-permute-done | bytes 16416 | tf_op jit(solution)/shard_map/ppermute | solution.py:102
  75.0 0.6 fusion.34
  (10 shorter events, 0.2 us)
Async XLA Ops:
  0.6 19.7 %copy-start = (bf16[1,8,128,128]{3,2,1,0:T(8,128)(2,1)S(1)}, bf16[1,8,128,128]{3,2,1,0:T(8,128)(2,1)}, u32[]{:S(2)}) copy-start(bf16[1,8,128,128]{3,2,1,0:T(8,128)(2,1)} %param.7) | copy-start | bytes 786436
  2.2 18.2 %copy-start.3 = (bf16[1024,128]{1,0:T(8,128)(2,1)S(1)}, bf16[1024,128]{1,0:T(8,128)(2,1)}, u32[]{:S(2)}) copy-start(bf16[1024,128]{1,0:T(8,128)(2,1)} %param.5) | copy-start | bytes 786436
  22.9 13.7 %all-to-all-start.1 = ((bf16[128,8,128]{2,1,0:T(8,128)(2,1)}), bf16[128,8,128]{2,1,0:T(8,128)(2,1)S(1)}, u32[]{:S(2)}, u32[]{:S(2)}) async-start(bf16[128,8,128]{2,1,0:T(8,128)(2,1)} %copy.29), calls=%async_computation.1 | async-start | bytes 524288 | tf_op jit(solution)/shard_map/all_to_all | solution.py:161
  28.5 8.2 %copy-start.2 = (bf16[1024,128]{1,0:T(8,128)(2,1)S(1)}, bf16[1024,128]{1,0:T(8,128)(2,1)}, u32[]{:S(2)}) copy-start(bf16[1024,128]{1,0:T(8,128)(2,1)} %param.4) | copy-start | bytes 786436
  28.5 10.8 %collective-permute-start = (bf16[4,4,32,128]{3,2,1,0:T(8,128)(2,1)S(1)}, bf16[4,4,32,128]{3,2,1,0:T(8,128)(2,1)S(1)}, u32[]{:S(2)}, u32[]{:S(2)}) collective-permute-start(bf16[4,4,32,128]{3,2,1,0:T(8,128)(2,1)S(1)} %fusion.26), channel_id=1, source_target_pairs={{0,16},{16,0},{32,48},{48,32},{64,80},{80,64},{96,112},{112,96},{1... | collective-permute-start | bytes 393224 | tf_op jit(solution)/shard_map/ppermute | solution.py:117
  37.4 3.2 %collective-permute-start.1 = (bf16[4,4,32,128]{3,2,1,0:T(8,128)(2,1)S(1)}, bf16[4,4,32,128]{3,2,1,0:T(8,128)(2,1)S(1)}, u32[]{:S(2)}, u32[]{:S(2)}) collective-permute-start(bf16[4,4,32,128]{3,2,1,0:T(8,128)(2,1)S(1)} %fusion.27), channel_id=1, source_target_pairs={{0,16},{16,0},{32,48},{48,32},{64,80},{80,64},{96,112},{112,96},{1... | collective-permute-start | bytes 393224 | tf_op jit(solution)/shard_map/ppermute | solution.py:117
  41.4 11.5 %all-to-all-start.2 = ((bf16[4,4,2,32,128]{4,3,1,2,0:T(8,128)(2,1)}), bf16[4,4,2,32,128]{4,3,1,2,0:T(8,128)(2,1)S(1)}, u32[]{:S(2)}, u32[]{:S(2)}) async-start(bf16[4,4,2,32,128]{4,3,1,2,0:T(8,128)(2,1)} %copy.35), calls=%async_computation.2 | async-start | bytes 524288 | tf_op jit(solution)/shard_map/all_to_all | solution.py:110
  45.9 26.0 %copy-start.1 = (bf16[1,8,128,128]{3,2,1,0:T(8,128)(2,1)S(1)}, bf16[1,8,128,128]{3,2,1,0:T(8,128)(2,1)}, u32[]{:S(2)}) copy-start(bf16[1,8,128,128]{3,2,1,0:T(8,128)(2,1)} %param.6) | copy-start | bytes 786436
  52.9 12.0 %collective-permute-start.2 = (bf16[2,2,32,128]{3,2,1,0:T(8,128)(2,1)S(1)}, bf16[2,2,32,128]{3,2,1,0:T(8,128)(2,1)S(1)}, u32[]{:S(2)}, u32[]{:S(2)}) collective-permute-start(bf16[2,2,32,128]{3,2,1,0:T(8,128)(2,1)S(1)} %pad_maximum_fusion.1), channel_id=1, source_target_pairs={{0,32},{16,48},{32,64},{48,80},{64,96},{80,112},{96,0},{112,16},{1... | collective-permute-start | bytes 98312 | tf_op jit(solution)/shard_map/ppermute | solution.py:100
  62.1 10.7 %collective-permute-start.3 = (bf16[2,32,128]{2,1,0:T(8,128)(2,1)S(1)}, bf16[2,32,128]{2,1,0:T(8,128)(2,1)S(1)}, u32[]{:S(2)}, u32[]{:S(2)}) collective-permute-start(bf16[2,32,128]{2,1,0:T(8,128)(2,1)S(1)} %get-tuple-element.6), channel_id=1, source_target_pairs={{0,96},{16,112},{32,0},{48,16},{64,32},{80,48},{96,64},{112,80},{1... | collective-permute-start | bytes 49160 | tf_op jit(solution)/shard_map/ppermute | solution.py:101
  64.9 10.0 %collective-permute-start.4 = (bf16[2,32,128]{2,1,0:T(8,128)(2,1)S(1)}, bf16[2,32,128]{2,1,0:T(8,128)(2,1)S(1)}, u32[]{:S(2)}, u32[]{:S(2)}) collective-permute-start(bf16[2,32,128]{2,1,0:T(8,128)(2,1)S(1)} %slice_bitcast_fusion), channel_id=1, source_target_pairs={{0,32},{16,48},{32,64},{48,80},{64,96},{80,112},{96,0},{112,16},{1... | collective-permute-start | bytes 49160 | tf_op jit(solution)/shard_map/ppermute | solution.py:102

commit v9 on v8

--- a/solution.py
+++ b/solution.py
@@ -1,6 +1,7 @@
 import jax
 import jax.numpy as jnp
 from jax import lax
+from jax.experimental import pallas as pl
 from jax.sharding import PartitionSpec as P
 
 LAYERS = 1
@@ -18,10 +19,23 @@
     return (received, second_product(received, left))
 
 
+def first_kernel(current_ref, right_ref, out_ref):
+    for block in range(current_ref.shape[0]):
+        out_ref[block] = lax.dot_general(
+            right_ref[block],
+            current_ref[block],
+            (((0,), (0,)), ((), ())),
+            preferred_element_type=jnp.float32,
+        ).astype(out_ref.dtype)
+
+
 def first_product(current, right):
-    return jnp.einsum("ikt,ikj->ijt", current, right, preferred_element_type=jnp.float32).astype(
-        jnp.bfloat16
-    )
+    blocks, _, tokens = current.shape
+    width = right.shape[2]
+    return pl.pallas_call(
+        first_kernel,
+        out_shape=jax.ShapeDtypeStruct((blocks, width, tokens), jnp.bfloat16),
+    )(current, right)
 
 
 def forward_layer(current, right, left):

time: 76.1 us -> 77.8 us (1.022)
  Pallas kernels: 0 us -> 2.04 us
  matrix products: 4.51 us -> 3.17 us
  local copies, waits for them, and re-layouts: 3.02 us -> 3.97 us
    pallas_call x0 -> x1, Pallas kernels: none -> 2.04 us  [first_product(): pl.pallas_call(first_kernel, out_shape=jax.ShapeDtypeStruct((blocks, widt...]
    dot_general x1 -> x0, matrix products: 1.34 us -> none  [first_product(): jnp.einsum('ikt,ikj->ijt', current, right, preferred_element_type=jnp.flo...]
    pallas_call x0 -> x1, local copies, waits for them, and re-layouts: none -> 1.12 us  [first_product(): pl.pallas_call(first_kernel, out_shape=jax.ShapeDtypeStruct((blocks, widt...]
where the time goes in v9:
time: 77.8 us; the launch traced here: 77.3 us
  starting transfers between devices  32.4 us (42%)
  blocking collectives  18.1 us (23%)
  waiting for transfers between devices  16.6 us (21%)
  local copies, waits for them, and re-layouts  3.97 us (5%)
  matrix products  3.17 us (4%)
  Pallas kernels  2.04 us (3%)
  between operations  0.84 us (1%)
    all_to_all x1, blocking collectives, forward_layer(): lax.all_to_all(first_out, 'mp', split_axis=1, concat_axis=0, tiled=True)  18.1 us
    ppermute x1, starting transfers between devices, reduce_stages(): ahead = lax.ppermute(ahead, 'dp', perm=pairs(1))  9.11 us
    all_to_all x1, waiting for transfers between devices, reduce_stages(): lax.all_to_all(x.astype(jnp.bfloat16), 'dp', 0, 0, tiled=True, axis_index...  6.98 us
    ppermute x1, starting transfers between devices, reduce_stages(): relayed = lax.ppermute(ahead[1], 'dp', perm=pairs(1))  6.9 us
    all_to_all x1, waiting for transfers between devices, shards(): lax.all_to_all(grad_first, 'mp', split_axis=0, concat_axis=1, tiled=True)  6.06 us
    all_to_all x1, starting transfers between devices, shards(): lax.all_to_all(grad_first, 'mp', split_axis=0, concat_axis=1, tiled=True)  5.14 us
    all_to_all x1, starting transfers between devices, reduce_stages(): lax.all_to_all(x.astype(jnp.bfloat16), 'dp', 0, 0, tiled=True, axis_index...  4.44 us
    ppermute x2, starting transfers between devices, reduce_stages(): lax.ppermute(pick(shift).astype(jnp.bfloat16), 'dp', perm=pairs(shift))  3.97 us
  transfers between devices with their start and end apart: 7, of which 4 were waited for; matrix products, arithmetic and copies ran while one was open for 3% of the time, Pallas kernels for 0%

profile of v9, /device:TPU:2, one launch (start us, length us, event | category | flops | bytes accessed | tf_op | source)
XLA Modules:
  0.0 77.3 jit_solution(12673979817321473401)
XLA Ops:
  0.6 0.0 copy-start
  0.6 2.0 %shard_map.75 = bf16[8,128,128]{2,1,0:T(8,128)(2,1)} custom-call(bf16[8,128,128]{2,1,0:T(8,128)(2,1)} %bitcast.105, bf16[8,128,128]{2,1,0:T(8,128)(2,1)} %bitcast.104), custom_call_target="tpu_custom_call" | custom-call | tf_op jit(solution)/shard_map/pallas_call | solution.py:35
  2.7 1.1 %copy.22 = bf16[8,128,128]{2,0,1:T(8,128)(2,1)S(1)} copy(bf16[8,128,128]{2,1,0:T(8,128)(2,1)} %shard_map.75) | data formatting | bytes 524288 | tf_op jit(solution)/shard_map/pallas_call | solution.py:35
  3.8 0.0 copy-start.3
  3.8 18.1 %all_to_all.41 = bf16[8,128,128]{2,0,1:T(8,128)(2,1)S(1)} all-to-all(bf16[8,128,128]{2,0,1:T(8,128)(2,1)S(1)} %copy.22), channel_id=1, replica_groups=mesh['dp'=32,'mp'=16] {'mp'}, dimensions={1} | all-to-all | bytes 524288 | tf_op jit(solution)/shard_map/all_to_all | solution.py:44
  22.0 0.0 copy-done
  22.0 0.0 copy-done.3
  22.0 1.3 %fusion.4 = (bf16[8,128,128]{2,1,0:T(8,128)(2,1)S(1)}, bf16[8,128,128]{2,1,0:T(8,128)(2,1)}) fusion(bf16[8,128,128]{2,1,0:T(8,128)(2,1)S(1)} %bitcast.112, bf16[1,8,128,128]{3,2,1,0:T(8,128)(2,1)S(1)} %copy-done, bf16[8,16,8,128]{3,0,2,1:T(8,128)(2,1)S(1)} %bitcast.107), kind=kOutput, calls=%fused_computation.13 | convolution fusion | flops 36569088 | bytes 1310720 | tf_op jit(solution)/shard_map/ijt,jim->jmt/dot_general | solution.py:15
  23.3 0.3 fusion.1
  23.6 0.9 %copy.26 = bf16[128,8,128]{2,1,0:T(8,128)(2,1)} copy(bf16[128,8,128]{0,2,1:T(8,128)(2,1)S(1)} %fusion.1) | data formatting | bytes 524288 | tf_op jit(solution)/shard_map/convert_element_type | solution.py:168
  24.5 5.1 %all-to-all-start.1 = ((bf16[128,8,128]{2,1,0:T(8,128)(2,1)}), bf16[128,8,128]{2,1,0:T(8,128)(2,1)S(1)}, u32[]{:S(2)}, u32[]{:S(2)}) async-start(bf16[128,8,128]{2,1,0:T(8,128)(2,1)} %copy.26), calls=%async_computation.1 | async-start | bytes 524288 | tf_op jit(solution)/shard_map/all_to_all | solution.py:175
  29.6 0.3 convolution_multiply_fusion.1
  30.0 0.1 copy.28
  30.1 0.0 copy-start.2
  30.1 2.1 %collective-permute-start = (bf16[4,4,32,128]{3,2,1,0:T(8,128)(2,1)S(1)}, bf16[4,4,32,128]{3,2,1,0:T(8,128)(2,1)S(1)}, u32[]{:S(2)}, u32[]{:S(2)}) collective-permute-start(bf16[4,4,32,128]{3,2,1,0:T(8,128)(2,1)S(1)} %fusion.24), channel_id=1, source_target_pairs={{0,16},{16,0},{32,48},{48,32},{64,80},{80,64},{96,112},{112,96},{1... | collective-permute-start | bytes 393224 | tf_op jit(solution)/shard_map/ppermute | solution.py:131
  32.2 6.1 %all-to-all-done.1 = bf16[128,8,128]{2,1,0:T(8,128)(2,1)S(1)} async-done(((bf16[128,8,128]{2,1,0:T(8,128)(2,1)}), bf16[128,8,128]{2,1,0:T(8,128)(2,1)S(1)}, u32[]{:S(2)}, u32[]{:S(2)}) %all-to-all-start.1) | async-done | bytes 262176 | tf_op jit(solution)/shard_map/all_to_all | solution.py:175
  38.3 0.0 copy-done.2
  38.3 0.3 fusion
  38.6 0.2 copy.30
  38.8 0.1 copy.31
  39.0 1.9 %collective-permute-start.1 = (bf16[4,4,32,128]{3,2,1,0:T(8,128)(2,1)S(1)}, bf16[4,4,32,128]{3,2,1,0:T(8,128)(2,1)S(1)}, u32[]{:S(2)}, u32[]{:S(2)}) collective-permute-start(bf16[4,4,32,128]{3,2,1,0:T(8,128)(2,1)S(1)} %fusion.25), channel_id=1, source_target_pairs={{0,16},{16,0},{32,48},{48,32},{64,80},{80,64},{96,112},{112,96},{1... | collective-permute-start | bytes 393224 | tf_op jit(solution)/shard_map/ppermute | solution.py:131
  40.9 0.0 collective-permute-done
  41.0 1.3 %collective-permute-done.1 = bf16[4,4,32,128]{3,2,1,0:T(8,128)(2,1)S(1)} collective-permute-done((bf16[4,4,32,128]{3,2,1,0:T(8,128)(2,1)S(1)}, bf16[4,4,32,128]{3,2,1,0:T(8,128)(2,1)S(1)}, u32[]{:S(2)}, u32[]{:S(2)}) %collective-permute-start.1) | collective-permute-done | bytes 131104 | tf_op jit(solution)/shard_map/ppermute | solution.py:131
  42.3 0.7 copy.32
  43.0 4.4 %all-to-all-start.2 = ((bf16[4,4,2,32,128]{4,3,1,2,0:T(8,128)(2,1)}), bf16[4,4,2,32,128]{4,3,1,2,0:T(8,128)(2,1)S(1)}, u32[]{:S(2)}, u32[]{:S(2)}) async-start(bf16[4,4,2,32,128]{4,3,1,2,0:T(8,128)(2,1)} %copy.32), calls=%async_computation.2 | async-start | bytes 524288 | tf_op jit(solution)/shard_map/all_to_all | solution.py:124
  47.5 0.0 copy-start.1
  47.5 7.0 %all-to-all-done.2 = bf16[4,4,2,32,128]{4,3,1,2,0:T(8,128)(2,1)S(1)} async-done(((bf16[4,4,2,32,128]{4,3,1,2,0:T(8,128)(2,1)}), bf16[4,4,2,32,128]{4,3,1,2,0:T(8,128)(2,1)S(1)}, u32[]{:S(2)}, u32[]{:S(2)}) %all-to-all-start.2) | async-done | bytes 262176 | tf_op jit(solution)/shard_map/all_to_all | solution.py:124
  54.5 9.1 %collective-permute-start.2 = (bf16[2,2,32,128]{3,2,1,0:T(8,128)(2,1)S(1)}, bf16[2,2,32,128]{3,2,1,0:T(8,128)(2,1)S(1)}, u32[]{:S(2)}, u32[]{:S(2)}) collective-permute-start(bf16[2,2,32,128]{3,2,1,0:T(8,128)(2,1)S(1)} %pad_maximum_fusion.1), channel_id=1, source_target_pairs={{0,32},{16,48},{32,64},{48,80},{64,96},{80,112},{96,0},{112,16},{1... | collective-permute-start | bytes 98312 | tf_op jit(solution)/shard_map/ppermute | solution.py:114
  63.7 2.9 %collective-permute-start.3 = (bf16[2,32,128]{2,1,0:T(8,128)(2,1)S(1)}, bf16[2,32,128]{2,1,0:T(8,128)(2,1)S(1)}, u32[]{:S(2)}, u32[]{:S(2)}) collective-permute-start(bf16[2,32,128]{2,1,0:T(8,128)(2,1)S(1)} %get-tuple-element.6), channel_id=1, source_target_pairs={{0,96},{16,112},{32,0},{48,16},{64,32},{80,48},{96,64},{112,80},{1... | collective-permute-start | bytes 49160 | tf_op jit(solution)/shard_map/ppermute | solution.py:115
  66.6 0.0 collective-permute-done.2
  66.6 6.9 %collective-permute-start.4 = (bf16[2,32,128]{2,1,0:T(8,128)(2,1)S(1)}, bf16[2,32,128]{2,1,0:T(8,128)(2,1)S(1)}, u32[]{:S(2)}, u32[]{:S(2)}) collective-permute-start(bf16[2,32,128]{2,1,0:T(8,128)(2,1)S(1)} %slice_bitcast_fusion), channel_id=1, source_target_pairs={{0,32},{16,48},{32,64},{48,80},{64,96},{80,112},{96,0},{112,16},{1... | collective-permute-start | bytes 49160 | tf_op jit(solution)/shard_map/ppermute | solution.py:116
  73.5 0.0 copy-done.1
  73.5 0.9 %convolution_convert_fusion = bf16[8,128,128]{1,2,0:T(8,128)(2,1)} fusion(bf16[8,16,8,128]{3,2,0,1:T(8,128)(2,1)S(1)} %bitcast.97, bf16[1,8,128,128]{3,2,1,0:T(8,128)(2,1)S(1)} %copy-done.1), kind=kOutput, calls=%fused_computation.4 | convolution fusion | flops 33685504 | bytes 786432 | tf_op jit(solution)/shard_map/ijt,ikj->ikt/dot_general | solution.py:171
  74.4 0.0 collective-permute-done.3
  74.4 2.3 %collective-permute-done.4 = bf16[2,32,128]{2,1,0:T(8,128)(2,1)S(1)} collective-permute-done((bf16[2,32,128]{2,1,0:T(8,128)(2,1)S(1)}, bf16[2,32,128]{2,1,0:T(8,128)(2,1)S(1)}, u32[]{:S(2)}, u32[]{:S(2)}) %collective-permute-start.4) | collective-permute-done | bytes 16416 | tf_op jit(solution)/shard_map/ppermute | solution.py:116
  76.7 0.6 fusion.33
  (10 shorter events, 0.2 us)
Async XLA Ops:
  0.6 21.3 %copy-start = (bf16[1,8,128,128]{3,2,1,0:T(8,128)(2,1)S(1)}, bf16[1,8,128,128]{3,2,1,0:T(8,128)(2,1)}, u32[]{:S(2)}) copy-start(bf16[1,8,128,128]{3,2,1,0:T(8,128)(2,1)} %param.7) | copy-start | bytes 786436
  3.8 18.2 %copy-start.3 = (bf16[1024,128]{1,0:T(8,128)(2,1)S(1)}, bf16[1024,128]{1,0:T(8,128)(2,1)}, u32[]{:S(2)}) copy-start(bf16[1024,128]{1,0:T(8,128)(2,1)} %param.5) | copy-start | bytes 786436
  24.5 13.8 %all-to-all-start.1 = ((bf16[128,8,128]{2,1,0:T(8,128)(2,1)}), bf16[128,8,128]{2,1,0:T(8,128)(2,1)S(1)}, u32[]{:S(2)}, u32[]{:S(2)}) async-start(bf16[128,8,128]{2,1,0:T(8,128)(2,1)} %copy.26), calls=%async_computation.1 | async-start | bytes 524288 | tf_op jit(solution)/shard_map/all_to_all | solution.py:175
  30.1 8.2 %copy-start.2 = (bf16[1024,128]{1,0:T(8,128)(2,1)S(1)}, bf16[1024,128]{1,0:T(8,128)(2,1)}, u32[]{:S(2)}) copy-start(bf16[1024,128]{1,0:T(8,128)(2,1)} %param.4) | copy-start | bytes 786436
  30.1 10.8 %collective-permute-start = (bf16[4,4,32,128]{3,2,1,0:T(8,128)(2,1)S(1)}, bf16[4,4,32,128]{3,2,1,0:T(8,128)(2,1)S(1)}, u32[]{:S(2)}, u32[]{:S(2)}) collective-permute-start(bf16[4,4,32,128]{3,2,1,0:T(8,128)(2,1)S(1)} %fusion.24), channel_id=1, source_target_pairs={{0,16},{16,0},{32,48},{48,32},{64,80},{80,64},{96,112},{112,96},{1... | collective-permute-start | bytes 393224 | tf_op jit(solution)/shard_map/ppermute | solution.py:131
  39.0 3.2 %collective-permute-start.1 = (bf16[4,4,32,128]{3,2,1,0:T(8,128)(2,1)S(1)}, bf16[4,4,32,128]{3,2,1,0:T(8,128)(2,1)S(1)}, u32[]{:S(2)}, u32[]{:S(2)}) collective-permute-start(bf16[4,4,32,128]{3,2,1,0:T(8,128)(2,1)S(1)} %fusion.25), channel_id=1, source_target_pairs={{0,16},{16,0},{32,48},{48,32},{64,80},{80,64},{96,112},{112,96},{1... | collective-permute-start | bytes 393224 | tf_op jit(solution)/shard_map/ppermute | solution.py:131
  43.0 11.4 %all-to-all-start.2 = ((bf16[4,4,2,32,128]{4,3,1,2,0:T(8,128)(2,1)}), bf16[4,4,2,32,128]{4,3,1,2,0:T(8,128)(2,1)S(1)}, u32[]{:S(2)}, u32[]{:S(2)}) async-start(bf16[4,4,2,32,128]{4,3,1,2,0:T(8,128)(2,1)} %copy.32), calls=%async_computation.2 | async-start | bytes 524288 | tf_op jit(solution)/shard_map/all_to_all | solution.py:124
  47.5 26.0 %copy-start.1 = (bf16[1,8,128,128]{3,2,1,0:T(8,128)(2,1)S(1)}, bf16[1,8,128,128]{3,2,1,0:T(8,128)(2,1)}, u32[]{:S(2)}) copy-start(bf16[1,8,128,128]{3,2,1,0:T(8,128)(2,1)} %param.6) | copy-start | bytes 786436
  54.5 12.0 %collective-permute-start.2 = (bf16[2,2,32,128]{3,2,1,0:T(8,128)(2,1)S(1)}, bf16[2,2,32,128]{3,2,1,0:T(8,128)(2,1)S(1)}, u32[]{:S(2)}, u32[]{:S(2)}) collective-permute-start(bf16[2,2,32,128]{3,2,1,0:T(8,128)(2,1)S(1)} %pad_maximum_fusion.1), channel_id=1, source_target_pairs={{0,32},{16,48},{32,64},{48,80},{64,96},{80,112},{96,0},{112,16},{1... | collective-permute-start | bytes 98312 | tf_op jit(solution)/shard_map/ppermute | solution.py:114
  63.7 10.7 %collective-permute-start.3 = (bf16[2,32,128]{2,1,0:T(8,128)(2,1)S(1)}, bf16[2,32,128]{2,1,0:T(8,128)(2,1)S(1)}, u32[]{:S(2)}, u32[]{:S(2)}) collective-permute-start(bf16[2,32,128]{2,1,0:T(8,128)(2,1)S(1)} %get-tuple-element.6), channel_id=1, source_target_pairs={{0,96},{16,112},{32,0},{48,16},{64,32},{80,48},{96,64},{112,80},{1... | collective-permute-start | bytes 49160 | tf_op jit(solution)/shard_map/ppermute | solution.py:115
  66.6 10.1 %collective-permute-start.4 = (bf16[2,32,128]{2,1,0:T(8,128)(2,1)S(1)}, bf16[2,32,128]{2,1,0:T(8,128)(2,1)S(1)}, u32[]{:S(2)}, u32[]{:S(2)}) collective-permute-start(bf16[2,32,128]{2,1,0:T(8,128)(2,1)S(1)} %slice_bitcast_fusion), channel_id=1, source_target_pairs={{0,32},{16,48},{32,64},{48,80},{64,96},{80,112},{96,0},{112,16},{1... | collective-permute-start | bytes 49160 | tf_op jit(solution)/shard_map/ppermute | solution.py:116

commit v10 on v8

--- a/solution.py
+++ b/solution.py
@@ -165,11 +165,12 @@
             * scale
         )
         early_r = reduce_stages(to_pieces(term_r, stages, dp_count), order[:1], dp_count)
-        both = jnp.stack([early_l, early_r], len(stages) - 1)
+        both = jnp.concatenate([early_l, early_r], -2)
         both = reduce_stages(both, order[1:], dp_count)
         piece = block_size // dp_count
-        parts_l[layer_index] = both[0].reshape(block_count, piece, block_size)
-        parts_r[layer_index] = both[1].reshape(block_count, piece, block_size)
+        half = block_count * piece
+        parts_l[layer_index] = both[:half].reshape(block_count, piece, block_size)
+        parts_r[layer_index] = both[half:].reshape(block_count, piece, block_size)
     stack_r = jnp.stack(parts_r, 0)
     stack_l = jnp.stack(parts_l, 0)
     grad_inputs = grad_now.reshape(block_count * block_size, tokens_here)

time: 76.1 us -> 76 us (level)
  no operation moved by 1% of the time
where the time goes in v10:
time: 76 us; the launch traced here: 75.6 us
  starting transfers between devices  32.4 us (43%)
  blocking collectives  18.1 us (24%)
  waiting for transfers between devices  16.5 us (22%)
  matrix products  4.51 us (6%)
  local copies, waits for them, and re-layouts  2.3 us (3%)
  other arithmetic  0.85 us (1%)
  between operations  0.85 us (1%)
    all_to_all x1, blocking collectives, forward_layer(): lax.all_to_all(first_out, 'mp', split_axis=1, concat_axis=0, tiled=True)  18.1 us
    ppermute x1, starting transfers between devices, reduce_stages(): ahead = lax.ppermute(ahead, 'dp', perm=pairs(1))  9.1 us
    all_to_all x1, waiting for transfers between devices, reduce_stages(): lax.all_to_all(x.astype(jnp.bfloat16), 'dp', 0, 0, tiled=True, axis_index...  6.98 us
    ppermute x1, starting transfers between devices, reduce_stages(): relayed = lax.ppermute(ahead[1], 'dp', perm=pairs(1))  6.9 us
    all_to_all x1, waiting for transfers between devices, shards(): lax.all_to_all(grad_first, 'mp', split_axis=0, concat_axis=1, tiled=True)  6.06 us
    all_to_all x1, starting transfers between devices, shards(): lax.all_to_all(grad_first, 'mp', split_axis=0, concat_axis=1, tiled=True)  5.13 us
    all_to_all x1, starting transfers between devices, reduce_stages(): lax.all_to_all(x.astype(jnp.bfloat16), 'dp', 0, 0, tiled=True, axis_index...  4.48 us
    ppermute x2, starting transfers between devices, reduce_stages(): lax.ppermute(pick(shift).astype(jnp.bfloat16), 'dp', perm=pairs(shift))  3.97 us
  transfers between devices with their start and end apart: 7, of which 4 were waited for; matrix products, arithmetic and copies ran while one was open for 3% of the time, Pallas kernels for 0%

profile of v10, /device:TPU:2, one launch (start us, length us, event | category | flops | bytes accessed | tf_op | source)
XLA Modules:
  0.0 75.6 jit_solution(17662893227215035304)
XLA Ops:
  0.6 0.0 copy-start
  0.6 1.3 %convolution_convert_fusion.2 = bf16[8,128,128]{2,1,0:T(8,128)(2,1)S(1)} fusion(bf16[8,128,128]{2,1,0:T(8,128)(2,1)} %bitcast.85, bf16[1,8,128,128]{3,2,1,0:T(8,128)(2,1)} %param.6), kind=kOutput, calls=%fused_computation.6 | convolution fusion | flops 33685504 | bytes 786432 | tf_op jit(solution)/shard_map/ikt,ikj->ijt/dot_general | solution.py:22
  2.0 0.2 copy.25
  2.2 0.0 copy-start.3
  2.2 18.1 %all_to_all.41 = bf16[8,128,128]{2,0,1:T(8,128)(2,1)S(1)} all-to-all(bf16[8,128,128]{2,0,1:T(8,128)(2,1)S(1)} %copy.25), channel_id=1, replica_groups=mesh['dp'=32,'mp'=16] {'mp'}, dimensions={1} | all-to-all | bytes 524288 | tf_op jit(solution)/shard_map/all_to_all | solution.py:30
  20.3 0.0 copy-done
  20.3 0.0 copy-done.3
  20.3 1.3 %fusion.4 = (bf16[8,128,128]{2,1,0:T(8,128)(2,1)S(1)}, bf16[8,128,128]{2,1,0:T(8,128)(2,1)}) fusion(bf16[8,128,128]{2,1,0:T(8,128)(2,1)S(1)} %bitcast.92, bf16[1,8,128,128]{3,2,1,0:T(8,128)(2,1)S(1)} %copy-done, bf16[8,16,8,128]{3,0,2,1:T(8,128)(2,1)S(1)} %bitcast.87), kind=kOutput, calls=%fused_computation.14 | convolution fusion | flops 36569088 | bytes 1310720 | tf_op jit(solution)/shard_map/ijt,jim->jmt/dot_general | solution.py:14
  21.7 0.3 fusion.1
  22.0 0.9 %copy.29 = bf16[128,8,128]{2,1,0:T(8,128)(2,1)} copy(bf16[128,8,128]{0,2,1:T(8,128)(2,1)S(1)} %fusion.1) | data formatting | bytes 524288 | tf_op jit(solution)/shard_map/convert_element_type | solution.py:154
  22.9 5.1 %all-to-all-start.1 = ((bf16[128,8,128]{2,1,0:T(8,128)(2,1)}), bf16[128,8,128]{2,1,0:T(8,128)(2,1)S(1)}, u32[]{:S(2)}, u32[]{:S(2)}) async-start(bf16[128,8,128]{2,1,0:T(8,128)(2,1)} %copy.29), calls=%async_computation.1 | async-start | bytes 524288 | tf_op jit(solution)/shard_map/all_to_all | solution.py:161
  28.0 0.3 convolution_multiply_fusion.1
  28.3 0.1 copy.31
  28.5 0.0 copy-start.2
  28.5 2.1 %collective-permute-start = (bf16[4,4,32,128]{3,2,1,0:T(8,128)(2,1)S(1)}, bf16[4,4,32,128]{3,2,1,0:T(8,128)(2,1)S(1)}, u32[]{:S(2)}, u32[]{:S(2)}) collective-permute-start(bf16[4,4,32,128]{3,2,1,0:T(8,128)(2,1)S(1)} %fusion.26), channel_id=1, source_target_pairs={{0,16},{16,0},{32,48},{48,32},{64,80},{80,64},{96,112},{112,96},{1... | collective-permute-start | bytes 393224 | tf_op jit(solution)/shard_map/ppermute | solution.py:117
  30.6 6.1 %all-to-all-done.1 = bf16[128,8,128]{2,1,0:T(8,128)(2,1)S(1)} async-done(((bf16[128,8,128]{2,1,0:T(8,128)(2,1)}), bf16[128,8,128]{2,1,0:T(8,128)(2,1)S(1)}, u32[]{:S(2)}, u32[]{:S(2)}) %all-to-all-start.1) | async-done | bytes 262176 | tf_op jit(solution)/shard_map/all_to_all | solution.py:161
  36.6 0.0 copy-done.2
  36.6 0.3 fusion
  36.9 0.2 copy.33
  37.2 0.1 copy.34
  37.4 1.9 %collective-permute-start.1 = (bf16[4,4,32,128]{3,2,1,0:T(8,128)(2,1)S(1)}, bf16[4,4,32,128]{3,2,1,0:T(8,128)(2,1)S(1)}, u32[]{:S(2)}, u32[]{:S(2)}) collective-permute-start(bf16[4,4,32,128]{3,2,1,0:T(8,128)(2,1)S(1)} %fusion.27), channel_id=1, source_target_pairs={{0,16},{16,0},{32,48},{48,32},{64,80},{80,64},{96,112},{112,96},{1... | collective-permute-start | bytes 393224 | tf_op jit(solution)/shard_map/ppermute | solution.py:117
  39.3 0.0 collective-permute-done
  39.3 1.3 %collective-permute-done.1 = bf16[4,4,32,128]{3,2,1,0:T(8,128)(2,1)S(1)} collective-permute-done((bf16[4,4,32,128]{3,2,1,0:T(8,128)(2,1)S(1)}, bf16[4,4,32,128]{3,2,1,0:T(8,128)(2,1)S(1)}, u32[]{:S(2)}, u32[]{:S(2)}) %collective-permute-start.1) | collective-permute-done | bytes 131104 | tf_op jit(solution)/shard_map/ppermute | solution.py:117
  40.6 0.7 pad_maximum_fusion
  41.4 4.5 %all-to-all-start.2 = ((bf16[4,4,64,128]{3,2,1,0:T(8,128)(2,1)}), bf16[4,4,64,128]{3,2,1,0:T(8,128)(2,1)S(1)}, u32[]{:S(2)}, u32[]{:S(2)}) async-start(bf16[4,4,64,128]{3,2,1,0:T(8,128)(2,1)} %pad_maximum_fusion), calls=%async_computation.2 | async-start | bytes 524288 | tf_op jit(solution)/shard_map/all_to_all | solution.py:110
  45.9 0.0 copy-start.1
  45.9 7.0 %all-to-all-done.2 = bf16[4,4,64,128]{3,2,1,0:T(8,128)(2,1)S(1)} async-done(((bf16[4,4,64,128]{3,2,1,0:T(8,128)(2,1)}), bf16[4,4,64,128]{3,2,1,0:T(8,128)(2,1)S(1)}, u32[]{:S(2)}, u32[]{:S(2)}) %all-to-all-start.2) | async-done | bytes 262176 | tf_op jit(solution)/shard_map/all_to_all | solution.py:110
  52.9 9.1 %collective-permute-start.2 = (bf16[2,64,128]{2,1,0:T(8,128)(2,1)S(1)}, bf16[2,64,128]{2,1,0:T(8,128)(2,1)S(1)}, u32[]{:S(2)}, u32[]{:S(2)}) collective-permute-start(bf16[2,64,128]{2,1,0:T(8,128)(2,1)S(1)} %pad_maximum_fusion.1), channel_id=1, source_target_pairs={{0,32},{16,48},{32,64},{48,80},{64,96},{80,112},{96,0},{112,16},{1... | collective-permute-start | bytes 98312 | tf_op jit(solution)/shard_map/ppermute | solution.py:100
  62.0 2.9 %collective-permute-start.3 = (bf16[64,128]{1,0:T(8,128)(2,1)S(1)}, bf16[64,128]{1,0:T(8,128)(2,1)S(1)}, u32[]{:S(2)}, u32[]{:S(2)}) collective-permute-start(bf16[64,128]{1,0:T(8,128)(2,1)S(1)} %get-tuple-element.6), channel_id=1, source_target_pairs={{0,96},{16,112},{32,0},{48,16},{64,32},{80,48},{96,64},{112,80},{1... | collective-permute-start | bytes 49160 | tf_op jit(solution)/shard_map/ppermute | solution.py:101
  64.9 0.0 collective-permute-done.2
  64.9 6.9 %collective-permute-start.4 = (bf16[64,128]{1,0:T(8,128)(2,1)S(1)}, bf16[64,128]{1,0:T(8,128)(2,1)S(1)}, u32[]{:S(2)}, u32[]{:S(2)}) collective-permute-start(bf16[64,128]{1,0:T(8,128)(2,1)S(1)} %slice_bitcast_fusion), channel_id=1, source_target_pairs={{0,32},{16,48},{32,64},{48,80},{64,96},{80,112},{96,0},{112,16},{1... | collective-permute-start | bytes 49160 | tf_op jit(solution)/shard_map/ppermute | solution.py:102
  71.8 0.0 copy-done.1
  71.8 0.9 %convolution_convert_fusion = bf16[8,128,128]{1,2,0:T(8,128)(2,1)} fusion(bf16[1,8,128,128]{3,2,1,0:T(8,128)(2,1)S(1)} %copy-done.1, bf16[8,16,8,128]{3,2,0,1:T(8,128)(2,1)S(1)} %bitcast.78), kind=kOutput, calls=%fused_computation.4 | convolution fusion | flops 33685504 | bytes 786432 | tf_op jit(solution)/shard_map/ijt,ikj->ikt/dot_general | solution.py:157
  72.8 0.0 collective-permute-done.3
  72.8 2.2 %collective-permute-done.4 = bf16[64,128]{1,0:T(8,128)(2,1)S(1)} collective-permute-done((bf16[64,128]{1,0:T(8,128)(2,1)S(1)}, bf16[64,128]{1,0:T(8,128)(2,1)S(1)}, u32[]{:S(2)}, u32[]{:S(2)}) %collective-permute-start.4) | collective-permute-done | bytes 16416 | tf_op jit(solution)/shard_map/ppermute | solution.py:102
  74.9 0.6 fusion.30
  (9 shorter events, 0.2 us)
Async XLA Ops:
  0.6 19.7 %copy-start = (bf16[1,8,128,128]{3,2,1,0:T(8,128)(2,1)S(1)}, bf16[1,8,128,128]{3,2,1,0:T(8,128)(2,1)}, u32[]{:S(2)}) copy-start(bf16[1,8,128,128]{3,2,1,0:T(8,128)(2,1)} %param.7) | copy-start | bytes 786436
  2.2 18.2 %copy-start.3 = (bf16[1024,128]{1,0:T(8,128)(2,1)S(1)}, bf16[1024,128]{1,0:T(8,128)(2,1)}, u32[]{:S(2)}) copy-start(bf16[1024,128]{1,0:T(8,128)(2,1)} %param.5) | copy-start | bytes 786436
  22.9 13.7 %all-to-all-start.1 = ((bf16[128,8,128]{2,1,0:T(8,128)(2,1)}), bf16[128,8,128]{2,1,0:T(8,128)(2,1)S(1)}, u32[]{:S(2)}, u32[]{:S(2)}) async-start(bf16[128,8,128]{2,1,0:T(8,128)(2,1)} %copy.29), calls=%async_computation.1 | async-start | bytes 524288 | tf_op jit(solution)/shard_map/all_to_all | solution.py:161
  28.5 8.2 %copy-start.2 = (bf16[1024,128]{1,0:T(8,128)(2,1)S(1)}, bf16[1024,128]{1,0:T(8,128)(2,1)}, u32[]{:S(2)}) copy-start(bf16[1024,128]{1,0:T(8,128)(2,1)} %param.4) | copy-start | bytes 786436
  28.5 10.8 %collective-permute-start = (bf16[4,4,32,128]{3,2,1,0:T(8,128)(2,1)S(1)}, bf16[4,4,32,128]{3,2,1,0:T(8,128)(2,1)S(1)}, u32[]{:S(2)}, u32[]{:S(2)}) collective-permute-start(bf16[4,4,32,128]{3,2,1,0:T(8,128)(2,1)S(1)} %fusion.26), channel_id=1, source_target_pairs={{0,16},{16,0},{32,48},{48,32},{64,80},{80,64},{96,112},{112,96},{1... | collective-permute-start | bytes 393224 | tf_op jit(solution)/shard_map/ppermute | solution.py:117
  37.4 3.2 %collective-permute-start.1 = (bf16[4,4,32,128]{3,2,1,0:T(8,128)(2,1)S(1)}, bf16[4,4,32,128]{3,2,1,0:T(8,128)(2,1)S(1)}, u32[]{:S(2)}, u32[]{:S(2)}) collective-permute-start(bf16[4,4,32,128]{3,2,1,0:T(8,128)(2,1)S(1)} %fusion.27), channel_id=1, source_target_pairs={{0,16},{16,0},{32,48},{48,32},{64,80},{80,64},{96,112},{112,96},{1... | collective-permute-start | bytes 393224 | tf_op jit(solution)/shard_map/ppermute | solution.py:117
  41.4 11.5 %all-to-all-start.2 = ((bf16[4,4,64,128]{3,2,1,0:T(8,128)(2,1)}), bf16[4,4,64,128]{3,2,1,0:T(8,128)(2,1)S(1)}, u32[]{:S(2)}, u32[]{:S(2)}) async-start(bf16[4,4,64,128]{3,2,1,0:T(8,128)(2,1)} %pad_maximum_fusion), calls=%async_computation.2 | async-start | bytes 524288 | tf_op jit(solution)/shard_map/all_to_all | solution.py:110
  45.9 26.0 %copy-start.1 = (bf16[1,8,128,128]{3,2,1,0:T(8,128)(2,1)S(1)}, bf16[1,8,128,128]{3,2,1,0:T(8,128)(2,1)}, u32[]{:S(2)}) copy-start(bf16[1,8,128,128]{3,2,1,0:T(8,128)(2,1)} %param.6) | copy-start | bytes 786436
  52.9 12.0 %collective-permute-start.2 = (bf16[2,64,128]{2,1,0:T(8,128)(2,1)S(1)}, bf16[2,64,128]{2,1,0:T(8,128)(2,1)S(1)}, u32[]{:S(2)}, u32[]{:S(2)}) collective-permute-start(bf16[2,64,128]{2,1,0:T(8,128)(2,1)S(1)} %pad_maximum_fusion.1), channel_id=1, source_target_pairs={{0,32},{16,48},{32,64},{48,80},{64,96},{80,112},{96,0},{112,16},{1... | collective-permute-start | bytes 98312 | tf_op jit(solution)/shard_map/ppermute | solution.py:100
  62.0 10.7 %collective-permute-start.3 = (bf16[64,128]{1,0:T(8,128)(2,1)S(1)}, bf16[64,128]{1,0:T(8,128)(2,1)S(1)}, u32[]{:S(2)}, u32[]{:S(2)}) collective-permute-start(bf16[64,128]{1,0:T(8,128)(2,1)S(1)} %get-tuple-element.6), channel_id=1, source_target_pairs={{0,96},{16,112},{32,0},{48,16},{64,32},{80,48},{96,64},{112,80},{1... | collective-permute-start | bytes 49160 | tf_op jit(solution)/shard_map/ppermute | solution.py:101
  64.9 10.0 %collective-permute-start.4 = (bf16[64,128]{1,0:T(8,128)(2,1)S(1)}, bf16[64,128]{1,0:T(8,128)(2,1)S(1)}, u32[]{:S(2)}, u32[]{:S(2)}) collective-permute-start(bf16[64,128]{1,0:T(8,128)(2,1)S(1)} %slice_bitcast_fusion), channel_id=1, source_target_pairs={{0,32},{16,48},{32,64},{48,80},{64,96},{80,112},{96,0},{112,16},{1... | collective-permute-start | bytes 49160 | tf_op jit(solution)/shard_map/ppermute | solution.py:102

commit v11 on v10

--- a/solution.py
+++ b/solution.py
@@ -149,9 +149,12 @@
         )
         order = stage_order(stages)
         early_l = reduce_stages(to_pieces(term_l, stages, dp_count), order[:1], dp_count)
+        owners = lax.axis_size("mp")
+        left_split = left.reshape(block_count, owners, block_size // owners, block_size)
         grad_first = jnp.einsum(
-            "jmt,jim->ijt", grad_pre, left, preferred_element_type=jnp.float32
+            "jpam,jmt->pjat", left_split, grad_pre, preferred_element_type=jnp.float32
         ).astype(jnp.bfloat16)
+        grad_first = grad_first.transpose(0, 2, 1, 3).reshape(block_size, block_count, tokens_here)
 
         def apply_back(returned, right=right):
             spread = jnp.einsum("ijt,ikj->ikt", returned, right, preferred_element_type=jnp.float32)

time: 76 us -> 76 us (level)
  no operation moved by 1% of the time
where the time goes in v11:
time: 76 us; the launch traced here: 75.5 us
  starting transfers between devices  32.4 us (43%)
  blocking collectives  18.1 us (24%)
  waiting for transfers between devices  16.5 us (22%)
  matrix products  4.4 us (6%)
  local copies, waits for them, and re-layouts  2.29 us (3%)
  between operations  0.86 us (1%)
  other arithmetic  0.85 us (1%)
    all_to_all x1, blocking collectives, forward_layer(): lax.all_to_all(first_out, 'mp', split_axis=1, concat_axis=0, tiled=True)  18.1 us
    ppermute x1, starting transfers between devices, reduce_stages(): ahead = lax.ppermute(ahead, 'dp', perm=pairs(1))  9.1 us
    all_to_all x1, waiting for transfers between devices, reduce_stages(): lax.all_to_all(x.astype(jnp.bfloat16), 'dp', 0, 0, tiled=True, axis_index...  6.98 us
    ppermute x1, starting transfers between devices, reduce_stages(): relayed = lax.ppermute(ahead[1], 'dp', perm=pairs(1))  6.89 us
    all_to_all x1, waiting for transfers between devices, shards(): lax.all_to_all(grad_first, 'mp', split_axis=0, concat_axis=1, tiled=True)  6.07 us
    all_to_all x1, starting transfers between devices, shards(): lax.all_to_all(grad_first, 'mp', split_axis=0, concat_axis=1, tiled=True)  5.14 us
    all_to_all x1, starting transfers between devices, reduce_stages(): lax.all_to_all(x.astype(jnp.bfloat16), 'dp', 0, 0, tiled=True, axis_index...  4.45 us
    ppermute x2, starting transfers between devices, reduce_stages(): lax.ppermute(pick(shift).astype(jnp.bfloat16), 'dp', perm=pairs(shift))  3.97 us
  transfers between devices with their start and end apart: 7, of which 4 were waited for; matrix products, arithmetic and copies ran while one was open for 3% of the time, Pallas kernels for 0%

profile of v11, /device:TPU:2, one launch (start us, length us, event | category | flops | bytes accessed | tf_op | source)
XLA Modules:
  0.0 75.5 jit_solution(8166264322939545124)
XLA Ops:
  0.6 0.0 copy-start
  0.6 1.3 %convolution_convert_fusion.2 = bf16[8,128,128]{2,1,0:T(8,128)(2,1)S(1)} fusion(bf16[8,128,128]{2,1,0:T(8,128)(2,1)} %bitcast.90, bf16[1,8,128,128]{3,2,1,0:T(8,128)(2,1)} %param.6), kind=kOutput, calls=%fused_computation.6 | convolution fusion | flops 33685504 | bytes 786432 | tf_op jit(solution)/shard_map/ikt,ikj->ijt/dot_general | solution.py:22
  2.0 0.2 copy.24
  2.2 0.0 copy-start.3
  2.2 18.1 %all_to_all.41 = bf16[8,128,128]{2,0,1:T(8,128)(2,1)S(1)} all-to-all(bf16[8,128,128]{2,0,1:T(8,128)(2,1)S(1)} %copy.24), channel_id=1, replica_groups=mesh['dp'=32,'mp'=16] {'mp'}, dimensions={1} | all-to-all | bytes 524288 | tf_op jit(solution)/shard_map/all_to_all | solution.py:30
  20.3 0.0 copy-done
  20.3 0.0 copy-done.3
  20.3 1.3 %fusion.4 = (bf16[8,128,128]{2,1,0:T(8,128)(2,1)S(1)}, bf16[8,128,128]{2,1,0:T(8,128)(2,1)}) fusion(bf16[8,128,128]{2,1,0:T(8,128)(2,1)S(1)} %bitcast.97, bf16[1,8,128,128]{3,2,1,0:T(8,128)(2,1)S(1)} %copy-done, bf16[8,16,8,128]{3,0,2,1:T(8,128)(2,1)S(1)} %bitcast.92), kind=kOutput, calls=%fused_computation.14 | convolution fusion | flops 36569088 | bytes 1310720 | tf_op jit(solution)/shard_map/ijt,jim->jmt/dot_general | solution.py:14
  21.7 0.2 fusion.1
  21.9 0.9 %copy.28 = bf16[16,8,8,128]{3,2,1,0:T(8,128)(2,1)} copy(bf16[16,8,8,128]{3,0,1,2:T(8,128)(2,1)S(1)} %fusion.1) | data formatting | bytes 524288 | tf_op jit(solution)/shard_map/convert_element_type | solution.py:156
  22.8 5.1 %all-to-all-start.1 = ((bf16[128,8,128]{2,1,0:T(8,128)(2,1)}), bf16[128,8,128]{2,1,0:T(8,128)(2,1)S(1)}, u32[]{:S(2)}, u32[]{:S(2)}) async-start(bf16[128,8,128]{2,1,0:T(8,128)(2,1)} %bitcast.14), calls=%async_computation.1 | async-start | bytes 524288 | tf_op jit(solution)/shard_map/all_to_all | solution.py:164
  27.9 0.3 convolution_multiply_fusion.1
  28.2 0.1 copy.30
  28.3 0.0 copy-start.2
  28.4 2.1 %collective-permute-start = (bf16[4,4,32,128]{3,2,1,0:T(8,128)(2,1)S(1)}, bf16[4,4,32,128]{3,2,1,0:T(8,128)(2,1)S(1)}, u32[]{:S(2)}, u32[]{:S(2)}) collective-permute-start(bf16[4,4,32,128]{3,2,1,0:T(8,128)(2,1)S(1)} %fusion.27), channel_id=1, source_target_pairs={{0,16},{16,0},{32,48},{48,32},{64,80},{80,64},{96,112},{112,96},{1... | collective-permute-start | bytes 393224 | tf_op jit(solution)/shard_map/ppermute | solution.py:117
  30.5 6.1 %all-to-all-done.1 = bf16[128,8,128]{2,1,0:T(8,128)(2,1)S(1)} async-done(((bf16[128,8,128]{2,1,0:T(8,128)(2,1)}), bf16[128,8,128]{2,1,0:T(8,128)(2,1)S(1)}, u32[]{:S(2)}, u32[]{:S(2)}) %all-to-all-start.1) | async-done | bytes 262176 | tf_op jit(solution)/shard_map/all_to_all | solution.py:164
  36.5 0.0 copy-done.2
  36.5 0.3 fusion
  36.8 0.2 copy.32
  37.1 0.1 copy.33
  37.3 1.9 %collective-permute-start.1 = (bf16[4,4,32,128]{3,2,1,0:T(8,128)(2,1)S(1)}, bf16[4,4,32,128]{3,2,1,0:T(8,128)(2,1)S(1)}, u32[]{:S(2)}, u32[]{:S(2)}) collective-permute-start(bf16[4,4,32,128]{3,2,1,0:T(8,128)(2,1)S(1)} %fusion.28), channel_id=1, source_target_pairs={{0,16},{16,0},{32,48},{48,32},{64,80},{80,64},{96,112},{112,96},{1... | collective-permute-start | bytes 393224 | tf_op jit(solution)/shard_map/ppermute | solution.py:117
  39.2 0.0 collective-permute-done
  39.2 1.3 %collective-permute-done.1 = bf16[4,4,32,128]{3,2,1,0:T(8,128)(2,1)S(1)} collective-permute-done((bf16[4,4,32,128]{3,2,1,0:T(8,128)(2,1)S(1)}, bf16[4,4,32,128]{3,2,1,0:T(8,128)(2,1)S(1)}, u32[]{:S(2)}, u32[]{:S(2)}) %collective-permute-start.1) | collective-permute-done | bytes 131104 | tf_op jit(solution)/shard_map/ppermute | solution.py:117
  40.5 0.7 pad_maximum_fusion
  41.3 4.5 %all-to-all-start.2 = ((bf16[4,4,64,128]{3,2,1,0:T(8,128)(2,1)}), bf16[4,4,64,128]{3,2,1,0:T(8,128)(2,1)S(1)}, u32[]{:S(2)}, u32[]{:S(2)}) async-start(bf16[4,4,64,128]{3,2,1,0:T(8,128)(2,1)} %pad_maximum_fusion), calls=%async_computation.2 | async-start | bytes 524288 | tf_op jit(solution)/shard_map/all_to_all | solution.py:110
  45.7 0.0 copy-start.1
  45.7 7.0 %all-to-all-done.2 = bf16[4,4,64,128]{3,2,1,0:T(8,128)(2,1)S(1)} async-done(((bf16[4,4,64,128]{3,2,1,0:T(8,128)(2,1)}), bf16[4,4,64,128]{3,2,1,0:T(8,128)(2,1)S(1)}, u32[]{:S(2)}, u32[]{:S(2)}) %all-to-all-start.2) | async-done | bytes 262176 | tf_op jit(solution)/shard_map/all_to_all | solution.py:110
  52.8 9.1 %collective-permute-start.2 = (bf16[2,64,128]{2,1,0:T(8,128)(2,1)S(1)}, bf16[2,64,128]{2,1,0:T(8,128)(2,1)S(1)}, u32[]{:S(2)}, u32[]{:S(2)}) collective-permute-start(bf16[2,64,128]{2,1,0:T(8,128)(2,1)S(1)} %pad_maximum_fusion.1), channel_id=1, source_target_pairs={{0,32},{16,48},{32,64},{48,80},{64,96},{80,112},{96,0},{112,16},{1... | collective-permute-start | bytes 98312 | tf_op jit(solution)/shard_map/ppermute | solution.py:100
  61.9 2.9 %collective-permute-start.3 = (bf16[64,128]{1,0:T(8,128)(2,1)S(1)}, bf16[64,128]{1,0:T(8,128)(2,1)S(1)}, u32[]{:S(2)}, u32[]{:S(2)}) collective-permute-start(bf16[64,128]{1,0:T(8,128)(2,1)S(1)} %get-tuple-element.6), channel_id=1, source_target_pairs={{0,96},{16,112},{32,0},{48,16},{64,32},{80,48},{96,64},{112,80},{1... | collective-permute-start | bytes 49160 | tf_op jit(solution)/shard_map/ppermute | solution.py:101
  64.8 0.0 collective-permute-done.2
  64.8 6.9 %collective-permute-start.4 = (bf16[64,128]{1,0:T(8,128)(2,1)S(1)}, bf16[64,128]{1,0:T(8,128)(2,1)S(1)}, u32[]{:S(2)}, u32[]{:S(2)}) collective-permute-start(bf16[64,128]{1,0:T(8,128)(2,1)S(1)} %slice_bitcast_fusion), channel_id=1, source_target_pairs={{0,32},{16,48},{32,64},{48,80},{64,96},{80,112},{96,0},{112,16},{1... | collective-permute-start | bytes 49160 | tf_op jit(solution)/shard_map/ppermute | solution.py:102
  71.7 0.0 copy-done.1
  71.7 0.9 %convolution_convert_fusion = bf16[8,128,128]{1,2,0:T(8,128)(2,1)} fusion(bf16[1,8,128,128]{3,2,1,0:T(8,128)(2,1)S(1)} %copy-done.1, bf16[8,16,8,128]{3,2,0,1:T(8,128)(2,1)S(1)} %bitcast.83), kind=kOutput, calls=%fused_computation.4 | convolution fusion | flops 33685504 | bytes 786432 | tf_op jit(solution)/shard_map/ijt,ikj->ikt/dot_general | solution.py:160
  72.6 0.0 collective-permute-done.3
  72.6 2.2 %collective-permute-done.4 = bf16[64,128]{1,0:T(8,128)(2,1)S(1)} collective-permute-done((bf16[64,128]{1,0:T(8,128)(2,1)S(1)}, bf16[64,128]{1,0:T(8,128)(2,1)S(1)}, u32[]{:S(2)}, u32[]{:S(2)}) %collective-permute-start.4) | collective-permute-done | bytes 16416 | tf_op jit(solution)/shard_map/ppermute | solution.py:102
  74.9 0.6 fusion.31
  (9 shorter events, 0.2 us)
Async XLA Ops:
  0.6 19.7 %copy-start = (bf16[1,8,128,128]{3,2,1,0:T(8,128)(2,1)S(1)}, bf16[1,8,128,128]{3,2,1,0:T(8,128)(2,1)}, u32[]{:S(2)}) copy-start(bf16[1,8,128,128]{3,2,1,0:T(8,128)(2,1)} %param.7) | copy-start | bytes 786436
  2.2 18.2 %copy-start.3 = (bf16[1024,128]{1,0:T(8,128)(2,1)S(1)}, bf16[1024,128]{1,0:T(8,128)(2,1)}, u32[]{:S(2)}) copy-start(bf16[1024,128]{1,0:T(8,128)(2,1)} %param.5) | copy-start | bytes 786436
  22.8 13.8 %all-to-all-start.1 = ((bf16[128,8,128]{2,1,0:T(8,128)(2,1)}), bf16[128,8,128]{2,1,0:T(8,128)(2,1)S(1)}, u32[]{:S(2)}, u32[]{:S(2)}) async-start(bf16[128,8,128]{2,1,0:T(8,128)(2,1)} %bitcast.14), calls=%async_computation.1 | async-start | bytes 524288 | tf_op jit(solution)/shard_map/all_to_all | solution.py:164
  28.3 8.2 %copy-start.2 = (bf16[1024,128]{1,0:T(8,128)(2,1)S(1)}, bf16[1024,128]{1,0:T(8,128)(2,1)}, u32[]{:S(2)}) copy-start(bf16[1024,128]{1,0:T(8,128)(2,1)} %param.4) | copy-start | bytes 786436
  28.4 10.8 %collective-permute-start = (bf16[4,4,32,128]{3,2,1,0:T(8,128)(2,1)S(1)}, bf16[4,4,32,128]{3,2,1,0:T(8,128)(2,1)S(1)}, u32[]{:S(2)}, u32[]{:S(2)}) collective-permute-start(bf16[4,4,32,128]{3,2,1,0:T(8,128)(2,1)S(1)} %fusion.27), channel_id=1, source_target_pairs={{0,16},{16,0},{32,48},{48,32},{64,80},{80,64},{96,112},{112,96},{1... | collective-permute-start | bytes 393224 | tf_op jit(solution)/shard_map/ppermute | solution.py:117
  37.3 3.2 %collective-permute-start.1 = (bf16[4,4,32,128]{3,2,1,0:T(8,128)(2,1)S(1)}, bf16[4,4,32,128]{3,2,1,0:T(8,128)(2,1)S(1)}, u32[]{:S(2)}, u32[]{:S(2)}) collective-permute-start(bf16[4,4,32,128]{3,2,1,0:T(8,128)(2,1)S(1)} %fusion.28), channel_id=1, source_target_pairs={{0,16},{16,0},{32,48},{48,32},{64,80},{80,64},{96,112},{112,96},{1... | collective-permute-start | bytes 393224 | tf_op jit(solution)/shard_map/ppermute | solution.py:117
  41.3 11.4 %all-to-all-start.2 = ((bf16[4,4,64,128]{3,2,1,0:T(8,128)(2,1)}), bf16[4,4,64,128]{3,2,1,0:T(8,128)(2,1)S(1)}, u32[]{:S(2)}, u32[]{:S(2)}) async-start(bf16[4,4,64,128]{3,2,1,0:T(8,128)(2,1)} %pad_maximum_fusion), calls=%async_computation.2 | async-start | bytes 524288 | tf_op jit(solution)/shard_map/all_to_all | solution.py:110
  45.7 26.0 %copy-start.1 = (bf16[1,8,128,128]{3,2,1,0:T(8,128)(2,1)S(1)}, bf16[1,8,128,128]{3,2,1,0:T(8,128)(2,1)}, u32[]{:S(2)}) copy-start(bf16[1,8,128,128]{3,2,1,0:T(8,128)(2,1)} %param.6) | copy-start | bytes 786436
  52.8 12.0 %collective-permute-start.2 = (bf16[2,64,128]{2,1,0:T(8,128)(2,1)S(1)}, bf16[2,64,128]{2,1,0:T(8,128)(2,1)S(1)}, u32[]{:S(2)}, u32[]{:S(2)}) collective-permute-start(bf16[2,64,128]{2,1,0:T(8,128)(2,1)S(1)} %pad_maximum_fusion.1), channel_id=1, source_target_pairs={{0,32},{16,48},{32,64},{48,80},{64,96},{80,112},{96,0},{112,16},{1... | collective-permute-start | bytes 98312 | tf_op jit(solution)/shard_map/ppermute | solution.py:100
  61.9 10.7 %collective-permute-start.3 = (bf16[64,128]{1,0:T(8,128)(2,1)S(1)}, bf16[64,128]{1,0:T(8,128)(2,1)S(1)}, u32[]{:S(2)}, u32[]{:S(2)}) collective-permute-start(bf16[64,128]{1,0:T(8,128)(2,1)S(1)} %get-tuple-element.6), channel_id=1, source_target_pairs={{0,96},{16,112},{32,0},{48,16},{64,32},{80,48},{96,64},{112,80},{1... | collective-permute-start | bytes 49160 | tf_op jit(solution)/shard_map/ppermute | solution.py:101
  64.8 10.0 %collective-permute-start.4 = (bf16[64,128]{1,0:T(8,128)(2,1)S(1)}, bf16[64,128]{1,0:T(8,128)(2,1)S(1)}, u32[]{:S(2)}, u32[]{:S(2)}) collective-permute-start(bf16[64,128]{1,0:T(8,128)(2,1)S(1)} %slice_bitcast_fusion), channel_id=1, source_target_pairs={{0,32},{16,48},{32,64},{48,80},{64,96},{80,112},{96,0},{112,16},{1... | collective-permute-start | bytes 49160 | tf_op jit(solution)/shard_map/ppermute | solution.py:102
